TPU v7x, 256 devices: a whole 4x4x8 slice. The times are simulated.
256 devices in a mesh: ctx: 16 (over z, core), ch: 16 (over y, x).
Axes of the slice: x: 4, y: 4, z: 8, core: 2. Of those that a mesh axis runs over, the one named last changes fastest.
Arguments:
- inputs: bfloat16 [4096, 4096], P('ctx', 'ch'), may hold values from -6 to 6
- gating: bfloat16 [4096, 4096], P('ctx', 'ch'), may hold values from -6 to 6
- filter_taps: bfloat16 [4096, 4096], P('ctx', 'ch'), may hold values from -2.25 to 2.25
- skip_gain: float32 [4096], P('ch'), may hold values from 0.5 to 1.5
- w_out: bfloat16 [4096, 4096], P('ch'), may hold values from -0.09375 to 0.09375
- cotangent: bfloat16 [4096, 4096], P('ctx', 'ch'), may hold values from -0.3125 to 0.3125
Outputs:
- output: bfloat16 [4096, 4096], P('ctx', 'ch')
- filter_grad: float32 [4096, 4096], P('ctx', 'ch')
All inputs are finite; a program needn't handle non-finite values.
Results may differ from a plain program's by a relative error of at most 0.015.
Values may be sent and summed in bfloat16 or wider, within the bound.
No kernel may reach another device: no remote copies, remote signals or barrier semaphores. Data moves between devices by JAX's collectives and lax.ppermute only.
A program may use at most 64 MiB of HBM per device.

v0:
```python
import math

import jax
import jax.numpy as jnp
from jax import lax
from jax.sharding import PartitionSpec as P

exact_prec = lax.Precision.HIGHEST


def spectral_tables(block_len):
    time_ids = jnp.arange(2 * block_len, dtype=jnp.int32)
    freq_ids = jnp.arange(block_len, dtype=jnp.int32)
    phase_ids = freq_ids[:, None] * time_ids[None, :] % (2 * block_len)
    angles = phase_ids.astype(jnp.float32) * (math.pi / block_len)
    parity = jnp.where(time_ids % 2 == 0, 1.0, -1.0).astype(jnp.float32)[None, :]
    is_first = (freq_ids == 0)[:, None]
    forward = jnp.concatenate(
        [jnp.cos(angles), jnp.where(is_first, parity, -jnp.sin(angles))], axis=0
    )
    norm_scale = 1.0 / (2 * block_len)
    real_rows = jnp.where(is_first, 1.0, 2.0) * jnp.cos(angles) * norm_scale
    imag_rows = jnp.where(is_first, parity, -2.0 * jnp.sin(angles)) * norm_scale
    inverse = jnp.concatenate([real_rows, imag_rows], axis=0).T
    first_bin = is_first.astype(jnp.float32)
    return (forward, inverse, first_bin)


def spec_product(first_spec, second_spec, first_bin):
    bin_count = first_bin.shape[0]
    first_real, first_imag = (first_spec[..., :bin_count, :], first_spec[..., bin_count:, :])
    second_real, second_imag = (second_spec[..., :bin_count, :], second_spec[..., bin_count:, :])
    others = 1.0 - first_bin
    real_part = first_real * second_real - others * first_imag * second_imag
    imag_part = (
        others * (first_real * second_imag + first_imag * second_real)
        + first_bin * first_imag * second_imag
    )
    return jnp.concatenate([real_part, imag_part], axis=-2)


def conj_product(first_spec, second_spec, first_bin):
    bin_count = first_bin.shape[0]
    first_real, first_imag = (first_spec[..., :bin_count, :], first_spec[..., bin_count:, :])
    second_real, second_imag = (second_spec[..., :bin_count, :], second_spec[..., bin_count:, :])
    others = 1.0 - first_bin
    real_part = first_real * second_real + others * first_imag * second_imag
    imag_part = (
        others * (first_imag * second_real - first_real * second_imag)
        + first_bin * first_imag * second_imag
    )
    return jnp.concatenate([real_part, imag_part], axis=-2)


def transform(dft_table, block_rows):
    return jnp.dot(dft_table, block_rows.astype(jnp.float32), precision=exact_prec)


def body(inputs, gating, filter_taps, skip_gain, w_out, cotangent):
    block_len, channels = inputs.shape
    ctx_count = lax.axis_size("ctx")
    position = lax.axis_index("ctx")
    forward, inverse, first_bin = spectral_tables(block_len)
    first_half = forward[:, :block_len]
    second_half = forward[:, block_len:]
    upstream = lax.dot_general(
        lax.all_gather(cotangent, "ch", axis=1, tiled=True),
        w_out,
        (((1,), (1,)), ((), ())),
        preferred_element_type=jnp.float32,
    )
    gate_wide = gating.astype(jnp.float32)
    grad_mixed = upstream * gate_wide
    signal_all, kernel_all = (
        lax.all_gather(inputs, "ctx", axis=0, tiled=True),
        lax.all_gather(filter_taps, "ctx", axis=0, tiled=True),
    )
    padded = jnp.concatenate(
        [jnp.zeros((block_len, channels), signal_all.dtype), signal_all], axis=0
    )
    own_spec = transform(second_half, grad_mixed)

    def lag_step(lag_index, state_pair):
        running, term_table = state_pair
        segment = lax.dynamic_slice_in_dim(
            padded, (position - lag_index) * block_len, 2 * block_len, 0
        )
        seg_spec = transform(forward, segment)
        kernel_block = lax.dynamic_slice_in_dim(kernel_all, lag_index * block_len, block_len, 0)
        running = running + spec_product(transform(first_half, kernel_block), seg_spec, first_bin)
        term_table = lax.dynamic_update_index_in_dim(
            term_table, conj_product(own_spec, seg_spec, first_bin), lag_index, 0
        )
        return (running, term_table)

    start_terms = jnp.zeros((ctx_count, 2 * block_len, channels), jnp.float32)
    start_spec = jnp.zeros((2 * block_len, channels), jnp.float32)
    running, term_table = lax.fori_loop(0, position + 1, lag_step, (start_spec, start_terms))
    convolved = jnp.dot(inverse[block_len:], running, precision=exact_prec)
    convolved, term_table = (convolved, term_table)
    summed = lax.psum_scatter(
        term_table.astype(jnp.bfloat16), "ctx", scatter_dimension=0, tiled=True
    ).astype(jnp.float32)
    filter_grad = jnp.dot(inverse[:block_len], summed[0], precision=exact_prec)
    mixed_sum = convolved + skip_gain[None, :] * inputs.astype(jnp.float32)
    gated_rows = (gate_wide * mixed_sum).astype(jnp.bfloat16)
    partial_out = jnp.dot(gated_rows, w_out, preferred_element_type=jnp.float32)
    output = lax.psum_scatter(
        partial_out.astype(jnp.bfloat16), "ch", scatter_dimension=1, tiled=True
    )
    return (output, filter_grad)


def solution(mesh):
    return jax.shard_map(
        body,
        mesh=mesh,
        in_specs=(
            P("ctx", "ch"),
            P("ctx", "ch"),
            P("ctx", "ch"),
            P("ch"),
            P("ch", None),
            P("ctx", "ch"),
        ),
        out_specs=(P("ctx", "ch"), P("ctx", "ch")),
        check_vma=False,
    )
```

profile of v0, /device:TPU:1, one launch (start us, length us, event | category | flops | bytes accessed | tf_op | source)
XLA Modules:
  0.0 418.6 jit_solution(11839190690769091835)
XLA Ops:
  7.2 0.0 copy-start
  7.2 0.0 all-gather.6.cloned.1.call-start
  7.2 0.7 all-gather.6.cloned.1.call-update
  7.9 0.0 all-gather.8.cloned.1.call-start
  8.0 0.7 all-gather.8.cloned.1.call-update
  8.7 0.0 all-gather.4.cloned.1.call-start
  8.7 0.7 all-gather.4.cloned.1.call-update
  9.4 0.0 reduce-scatter.5.cloned.1.call-start
  9.5 1.9 fusion.24
  11.4 2.8 select_multiply_fusion
  14.2 0.9 fusion.12
  15.0 1.1 pad_maximum_fusion
  16.2 0.0 copy-start.5
  16.2 37.3 %all-gather.6.cloned.1.call-done = bf16[4096,256]{1,0:T(8,128)(2,1)} async-done(((bf16[256,256]{1,0:T(8,128)(2,1)}), bf16[4096,256]{1,0:T(8,128)(2,1)}) %all-gather.6.cloned.1.call-update) | async-done | bytes 2097168 | tf_op jit(solution)/shard_map/all_gather | solution.py:75
  53.5 3.1 concatenate.17
  56.6 47.7 %all-gather.8.cloned.1.call-done = bf16[256,4096]{1,0:T(8,128)(2,1)} async-done(((bf16[256,256]{1,0:T(8,128)(2,1)}), bf16[256,4096]{1,0:T(8,128)(2,1)}) %all-gather.8.cloned.1.call-update) | async-done | bytes 2097168 | tf_op jit(solution)/shard_map/all_gather | solution.py:67
  104.3 0.0 copy-done
  104.3 0.0 copy-done.5
  104.3 2.3 convolution_multiply_fusion
  106.6 1.5 fusion.14
  108.1 38.9 %all-gather.4.cloned.1.call-done = bf16[4096,256]{1,0:T(8,128)(2,1)} async-done(((bf16[256,256]{1,0:T(8,128)(2,1)}), bf16[4096,256]{1,0:T(8,128)(2,1)}) %all-gather.4.cloned.1.call-update) | async-done | bytes 2097168 | tf_op jit(solution)/shard_map/all_gather | solution.py:76
  147.0 0.8 broadcast_in_dim.64
  147.9 2.3 broadcast_in_dim.65
  150.2 15.1 %while.14 = (s32[]{:T(128)}, f32[512,256]{0,1:T(8,128)}, bf16[16,512,256]{1,2,0:T(8,128)(2,1)}, s32[]{:T(128)}, bf16[4096,256]{1,0:T(8,128)(2,1)}, /*index=5*/f3...) while((s32[]{:T(128)}, f32[512,256]{0,1:T(8,128)}, ...), condition=%wide.region_1.2_spmd.clone.clone, body=%wide.region_0.1_spmd.clone.clone.sunk | while | flops 1210319616 | bytes 8002867 | solution.py:98
  150.2 1.6 convolution_bitcast_fusion.4
  151.8 2.1 convolution_bitcast_fusion.5
  153.9 0.1 multiply_subtract_fusion.2
  154.0 1.9 maximum_add_fusion.2
  155.9 1.1 multiply_add_fusion.4
  157.1 0.7 fusion.48
  157.8 1.6 convolution_bitcast_fusion.4
  159.4 2.1 convolution_bitcast_fusion.5
  161.5 0.1 multiply_subtract_fusion.2
  161.6 1.9 maximum_add_fusion.2
  163.5 1.1 multiply_add_fusion.4
  164.6 0.7 fusion.48
  165.3 0.0 copy-start.4
  165.3 0.0 reduce-scatter.5.cloned.1.call-update
  165.3 0.0 copy-start.1
  165.4 0.0 copy-start.6
  165.4 0.0 copy-start.7
  165.4 0.0 reduce-scatter.3.cloned.1.call-start
  165.4 2.0 multiply_multiply_fusion
  167.4 0.0 copy-done.4
  167.4 0.1 maximum_bitcast_fusion.1
  167.5 0.0 copy-start.2
  167.5 1.0 copy-done.2
  168.5 0.0 copy-done.1
  168.5 0.0 copy-done.6
  168.5 0.0 copy-done.7
  168.5 1.0 fusion.8
  169.5 2.1 convolution_convert_fusion
  171.6 0.0 copy-start.3
  171.6 0.0 reduce-scatter.3.cloned.1.call-update
  171.6 156.6 %reduce-scatter.5.cloned.1.call-done = bf16[1,512,256]{1,2,0:T(8,128)(2,1)} async-done(((bf16[16,512,256]{1,2,0:T(8,128)(2,1)}), bf16[1,512,256]{1,2,0:T(8,128)(2,1)}) %reduce-scatter.5.cloned.1.call-update) | async-done | bytes 262160 | tf_op jit(solution)/shard_map/reduce_scatter | solution.py:101
  328.2 0.0 copy-done.3
  328.2 2.2 fusion.16
  330.5 81.6 %reduce-scatter.3.cloned.1.call-done = bf16[256,256]{1,0:T(8,128)(2,1)} async-done(((bf16[256,4096]{1,0:T(8,128)(2,1)}), bf16[256,256]{1,0:T(8,128)(2,1)}) %reduce-scatter.3.cloned.1.call-update) | async-done | bytes 131088 | tf_op jit(solution)/shard_map/reduce_scatter | solution.py:108
  (7 shorter events, 0.0 us)
Async XLA Ops:
  7.2 97.1 %copy-start = (bf16[256,4096]{1,0:T(8,128)(2,1)S(1)}, bf16[256,4096]{1,0:T(8,128)(2,1)}, u32[]{:S(2)}) copy-start(bf16[256,4096]{1,0:T(8,128)(2,1)} %param.12) | copy-start | bytes 6291460
  7.2 46.3 %all-gather.6.cloned.1.call-start = ((), (), s32[]{:S(2)}) async-start(), calls=%async_computation.3 | async-start | bytes 2228224 | tf_op jit(solution)/shard_map/all_gather | solution.py:75
  7.9 96.4 %all-gather.8.cloned.1.call-start = ((), (), s32[]{:S(2)}) async-start(), calls=%async_computation.4 | async-start | bytes 2228224 | tf_op jit(solution)/shard_map/all_gather | solution.py:67
  8.7 138.4 %all-gather.4.cloned.1.call-start = ((), (), s32[]{:S(2)}) async-start(), calls=%async_computation.2 | async-start | bytes 2228224 | tf_op jit(solution)/shard_map/all_gather | solution.py:76
  9.4 318.8 %reduce-scatter.5.cloned.1.call-start = ((), (), s32[]{:S(2)}) async-start(), calls=%async_computation.6 | async-start | bytes 4456448 | tf_op jit(solution)/shard_map/reduce_scatter | solution.py:101
  16.2 88.1 %copy-start.5 = (bf16[256,256]{1,0:T(8,128)(2,1)S(1)}, bf16[256,256]{1,0:T(8,128)(2,1)}, u32[]{:S(2)}) copy-start(bf16[256,256]{1,0:T(8,128)(2,1)} %param.9) | copy-start | bytes 393220
  165.3 2.1 copy-start.4
  165.3 3.1 copy-start.1
  165.4 3.1 copy-start.6
  165.4 3.1 copy-start.7
  165.4 246.7 %reduce-scatter.3.cloned.1.call-start = ((), (), s32[]{:S(2)}) async-start(), calls=%async_computation.5 | async-start | bytes 2228224 | tf_op jit(solution)/shard_map/reduce_scatter | solution.py:108
  167.5 1.0 copy-start.2
  171.6 156.6 %copy-start.3 = (f32[512,512]{0,1:T(8,128)S(1)}, f32[512,512]{0,1:T(8,128)}, u32[]{:S(2)}) copy-start(f32[512,512]{0,1:T(8,128)} %copy-done.2) | copy-start | bytes 3145732
Sparse Core Ops, SparseCore 0:
  9.8 43.6 all-gather.5
  55.9 48.3 all-gather.7
  106.1 40.8 all-gather.3
  165.5 162.6 reduce-scatter.4
  332.2 79.8 reduce-scatter.2
where the time goes:
time: 421 us; the launch traced here: 419 us
  waiting for transfers between devices  364 us (86%)
  other arithmetic  16.4 us (4%)
  matrix products  16.4 us (4%)
  between operations  13.9 us (3%)
  local copies, waits for them, and re-layouts  7.34 us (2%)
    reduce_scatter x1, waiting for transfers between devices, body(): lax.psum_scatter(term_table.astype(jnp.bfloat16), 'ctx', scatter_dimensio...  157 us
    reduce_scatter x1, waiting for transfers between devices, body(): lax.psum_scatter(partial_out.astype(jnp.bfloat16), 'ch', scatter_dimensio...  81.6 us
    all_gather x1, waiting for transfers between devices, body(): lax.all_gather(cotangent, 'ch', axis=1, tiled=True)  47.7 us
    all_gather x1, waiting for transfers between devices, body(): lax.all_gather(filter_taps, 'ctx', axis=0, tiled=True)  38.9 us
    all_gather x1, waiting for transfers between devices, body(): lax.all_gather(inputs, 'ctx', axis=0, tiled=True)  37.3 us
    dot_general x5, matrix products, transform(): jnp.dot(dft_table, block_rows.astype(jnp.float32), precision=exact_prec)  8.77 us
  transfers between devices with their start and end apart: 5, of which 5 were waited for; matrix products, arithmetic and copies ran while one was open for 5% of the time, Pallas kernels for 0%

commit v1 on v0

--- a/solution.py
+++ b/solution.py
@@ -56,13 +56,26 @@
     return jnp.dot(dft_table, block_rows.astype(jnp.float32), precision=exact_prec)
 
 
+def shift_blocks(spec, blocks, width):
+    if blocks == 0:
+        return spec
+    rows = spec.shape[0]
+    pad = jnp.zeros((rows, blocks * width), spec.dtype)
+    return jnp.concatenate([pad, spec[:, : spec.shape[1] - blocks * width]], axis=1)
+
+
 def body(inputs, gating, filter_taps, skip_gain, w_out, cotangent):
     block_len, channels = inputs.shape
     ctx_count = lax.axis_size("ctx")
-    position = lax.axis_index("ctx")
+    width = channels // ctx_count
     forward, inverse, first_bin = spectral_tables(block_len)
     first_half = forward[:, :block_len]
     second_half = forward[:, block_len:]
+
+    pair = jnp.stack([inputs, filter_taps])
+    pair_t = lax.all_to_all(pair, "ctx", 2, 2, tiled=True)
+    signal_t, taps_t = pair_t[0], pair_t[1]
+
     upstream = lax.dot_general(
         lax.all_gather(cotangent, "ch", axis=1, tiled=True),
         w_out,
@@ -71,37 +84,35 @@
     )
     gate_wide = gating.astype(jnp.float32)
     grad_mixed = upstream * gate_wide
-    signal_all, kernel_all = (
-        lax.all_gather(inputs, "ctx", axis=0, tiled=True),
-        lax.all_gather(filter_taps, "ctx", axis=0, tiled=True),
+    grad_t = lax.all_to_all(grad_mixed, "ctx", 1, 1, tiled=True)
+
+    low_spec = transform(first_half, signal_t)
+    high_spec = transform(second_half, signal_t)
+    seg_spec = high_spec + shift_blocks(low_spec, 1, width)
+    taps_spec = transform(first_half, taps_t)
+    grad_spec = transform(second_half, grad_t)
+
+    running = jnp.zeros_like(seg_spec)
+    lag_terms = []
+    for lag in range(ctx_count):
+        shifted = shift_blocks(seg_spec, lag, width)
+        tap_block = taps_spec[:, lag * width : (lag + 1) * width]
+        running = running + spec_product(
+            jnp.tile(tap_block, (1, ctx_count)), shifted, first_bin
+        )
+        term = conj_product(grad_spec, shifted, first_bin)
+        lag_terms.append(
+            term.reshape(term.shape[0], ctx_count, width).sum(axis=1)
+        )
+    lag_spec = jnp.concatenate(lag_terms, axis=1)
+
+    convolved_t = jnp.dot(inverse[block_len:], running, precision=exact_prec)
+    filter_grad_t = jnp.dot(inverse[:block_len], lag_spec, precision=exact_prec)
+    back = lax.all_to_all(
+        jnp.stack([convolved_t, filter_grad_t]), "ctx", 2, 2, tiled=True
     )
-    padded = jnp.concatenate(
-        [jnp.zeros((block_len, channels), signal_all.dtype), signal_all], axis=0
-    )
-    own_spec = transform(second_half, grad_mixed)
+    convolved, filter_grad = back[0], back[1]
 
-    def lag_step(lag_index, state_pair):
-        running, term_table = state_pair
-        segment = lax.dynamic_slice_in_dim(
-            padded, (position - lag_index) * block_len, 2 * block_len, 0
-        )
-        seg_spec = transform(forward, segment)
-        kernel_block = lax.dynamic_slice_in_dim(kernel_all, lag_index * block_len, block_len, 0)
-        running = running + spec_product(transform(first_half, kernel_block), seg_spec, first_bin)
-        term_table = lax.dynamic_update_index_in_dim(
-            term_table, conj_product(own_spec, seg_spec, first_bin), lag_index, 0
-        )
-        return (running, term_table)
-
-    start_terms = jnp.zeros((ctx_count, 2 * block_len, channels), jnp.float32)
-    start_spec = jnp.zeros((2 * block_len, channels), jnp.float32)
-    running, term_table = lax.fori_loop(0, position + 1, lag_step, (start_spec, start_terms))
-    convolved = jnp.dot(inverse[block_len:], running, precision=exact_prec)
-    convolved, term_table = (convolved, term_table)
-    summed = lax.psum_scatter(
-        term_table.astype(jnp.bfloat16), "ctx", scatter_dimension=0, tiled=True
-    ).astype(jnp.float32)
-    filter_grad = jnp.dot(inverse[:block_len], summed[0], precision=exact_prec)
     mixed_sum = convolved + skip_gain[None, :] * inputs.astype(jnp.float32)
     gated_rows = (gate_wide * mixed_sum).astype(jnp.bfloat16)
     partial_out = jnp.dot(gated_rows, w_out, preferred_element_type=jnp.float32)

time: 421 us -> 266 us (0.63)
  waiting for transfers between devices: 364 us -> 126 us
  other arithmetic: 16.4 us -> 54.5 us
  starting transfers between devices: 0.19 us -> 22.8 us
  local copies, waits for them, and re-layouts: 7.34 us -> 28.6 us
    reduce_scatter x1 -> x0, waiting for transfers between devices: 157 us -> none  [body(): lax.psum_scatter(term_table.astype(jnp.bfloat16), 'ctx', scatter_dimensio...]
    all_gather x2 -> x0, waiting for transfers between devices: 76.2 us -> none  [the longest x1 38.9 us: body(): lax.all_gather(filter_taps, 'ctx', axis=0, tiled=True)]
    all_to_all x0 -> x3, waiting for transfers between devices: none -> 24.6 us  [the longest x1 16.6 us: body(): lax.all_to_all(jnp.stack([convolved_t, filter_grad_t]), 'ctx', 2, 2, tile...]
    all_to_all x0 -> x3, starting transfers between devices: none -> 22.7 us  [the longest x1 9.97 us: body(): pair_t = lax.all_to_all(pair, 'ctx', 2, 2, tiled=True)]
    unnamed x16 -> x106, local copies, waits for them, and re-layouts: 1.01 us -> 22.3 us
    reduce_sum x0 -> x16, other arithmetic: none -> 20.4 us  [body(): lag_terms.append(term.reshape(term.shape[0], ctx_count, width).sum(axis=1))]
    all_gather x1, waiting for transfers between devices: 47.7 us -> 27.5 us  [body(): lax.all_gather(cotangent, 'ch', axis=1, tiled=True)]
    sub x2 -> x11, other arithmetic: 0.21 us -> 18 us  [spec_product(): real_part = first_real * second_real - others * first_imag * second_imag]
  transfers between devices with their start and end apart: 5 -> 5, of which waited for: 5 -> 5; matrix products, arithmetic and copies ran while one was open for 5% -> 9% of each run, Pallas kernels for 0% -> 0%
where the time goes in v1:
time: 266 us; the launch traced here: 263 us
  waiting for transfers between devices  126 us (47%)
  other arithmetic  54.5 us (20%)
  local copies, waits for them, and re-layouts  28.6 us (11%)
  starting transfers between devices  22.8 us (9%)
  matrix products  17.2 us (6%)
  between operations  14.7 us (6%)
    reduce_scatter x1, waiting for transfers between devices, body(): lax.psum_scatter(partial_out.astype(jnp.bfloat16), 'ch', scatter_dimensio...  72.7 us
    all_gather x1, waiting for transfers between devices, body(): lax.all_gather(cotangent, 'ch', axis=1, tiled=True)  27.5 us
    unnamed x106, local copies, waits for them, and re-layouts  22.3 us
    reduce_sum x16, other arithmetic, body(): lag_terms.append(term.reshape(term.shape[0], ctx_count, width).sum(axis=1))  20.4 us
    sub x11, other arithmetic, spec_product(): real_part = first_real * second_real - others * first_imag * second_imag  18 us
    all_to_all x1, waiting for transfers between devices, body(): lax.all_to_all(jnp.stack([convolved_t, filter_grad_t]), 'ctx', 2, 2, tile...  16.6 us
    all_to_all x1, starting transfers between devices, body(): pair_t = lax.all_to_all(pair, 'ctx', 2, 2, tiled=True)  9.97 us
    all_to_all x1, starting transfers between devices, body(): grad_t = lax.all_to_all(grad_mixed, 'ctx', 1, 1, tiled=True)  9.29 us
  transfers between devices with their start and end apart: 5, of which 5 were waited for; matrix products, arithmetic and copies ran while one was open for 9% of the time, Pallas kernels for 0%

profile of v1, /device:TPU:1, one launch (start us, length us, event | category | flops | bytes accessed | tf_op | source)
XLA Modules:
  0.0 263.3 jit_solution(2376567963497250367)
XLA Ops:
  7.9 1.0 pad_maximum_fusion.18
  9.8 10.0 %all-to-all-start = ((bf16[2,256,256]{1,0,2:T(2,128)(2,1)}), bf16[2,256,256]{1,0,2:T(2,128)(2,1)S(1)}, u32[]{:S(2)}, u32[]{:S(2)}) async-start(bf16[2,256,256]{1,0,2:T(2,128)(2,1)} %copy.25), calls=%async_computation | async-start | bytes 524288 | tf_op jit(solution)/shard_map/all_to_all | solution.py:76
  19.8 1.0 copy.24
  20.8 1.9 fusion.170
  22.7 2.0 multiply_multiply_fusion
  24.7 2.0 select_multiply_fusion
  26.8 1.1 maximum_bitcast_fusion
  27.9 3.4 %all-to-all-done = bf16[2,256,256]{1,0,2:T(2,128)(2,1)S(1)} async-done(((bf16[2,256,256]{1,0,2:T(2,128)(2,1)}), bf16[2,256,256]{1,0,2:T(2,128)(2,1)S(1)}, u32[]{:S(2)}, u32[]{:S(2)}) %all-to-all-start) | async-done | bytes 262176 | tf_op jit(solution)/shard_map/all_to_all | solution.py:76
  31.3 1.2 fusion.195
  32.5 1.1 copy.36
  33.6 1.1 copy.37
  34.6 1.3 fusion.173
  35.9 1.3 fusion.175
  37.2 27.5 %all-gather.2.cloned.1.call-done = bf16[256,4096]{1,0:T(8,128)(2,1)} async-done(((bf16[256,256]{1,0:T(8,128)(2,1)}), bf16[256,4096]{1,0:T(8,128)(2,1)}) %all-gather.2.cloned.1.call-update) | async-done | bytes 2097168 | tf_op jit(solution)/shard_map/all_gather | solution.py:80
  64.6 3.0 %convolution_multiply_fusion = f32[256,256]{0,1:T(8,128)} fusion(bf16[256,4096]{1,0:T(8,128)(2,1)} %all-gather.2.cloned.1.call-done, bf16[256,4096]{1,0:T(8,128)(2,1)S(1)} %copy-done, bf16[256,256]{0,1:T(8,128)(2,1)S(1)} %copy.24), kind=kOutput, calls=%fused_computation.4 | convolution fusion | flops 537001984 | bytes 4587520 | tf_op jit(solution)/shard_map/dot_general | solution.py:79
  67.7 9.3 %all-to-all-start.1 = ((f32[256,16,16]{0,2,1:T(8,128)}), f32[256,16,16]{0,2,1:T(8,128)S(1)}, u32[]{:S(2)}, u32[]{:S(2)}) async-start(f32[256,16,16]{0,2,1:T(8,128)} %bitcast.38), calls=%async_computation.1 | async-start | bytes 524288 | tf_op jit(solution)/shard_map/all_to_all | solution.py:87
  77.0 1.6 convolution_add_fusion
  80.8 1.1 fusion.124
  81.9 1.3 fusion.128
  83.9 4.6 %all-to-all-done.1 = f32[256,16,16]{0,2,1:T(8,128)S(1)} async-done(((f32[256,16,16]{0,2,1:T(8,128)}), f32[256,16,16]{0,2,1:T(8,128)S(1)}, u32[]{:S(2)}, u32[]{:S(2)}) %all-to-all-start.1) | async-done | bytes 262176 | tf_op jit(solution)/shard_map/all_to_all | solution.py:87
  88.5 1.7 fusion.171
  90.3 1.7 fusion.72
  92.7 2.7 %fusion.76 = (f32[256,256]{0,1:T(8,128)}, f32[256,256]{0,1:T(8,128)}, f32[256,256]{0,1:T(8,128)S(1)}, f32[256,256]{0,1:T(8,128)S(1)}, f32[256,256]{0,1:T(8,128)S(1)}, /*index=5*/f32[256,256]{0,1:T(8,128)S(1)}) fusion(f32[256,16]{0,1:T(8,128)S(1)} %copy-done.40, f32[256,16]{0,1:T(8,128)S(1)} %copy-done.41, f32[256]{0:T(256)S(1)} %broadcast_subtract_fusion, ...), kind=kLoop, calls=%fused_computation.219 | loop fusion | flops 2031616 | bytes 2656256 | tf_op jit(solution)/shard_map/sub | solution.py:34
  95.4 1.1 pad_maximum_fusion.2
  96.5 1.7 reduce_sum.145
  98.2 1.7 reduce_sum.159
  99.9 1.0 fusion.84
  100.9 0.9 pad_maximum_fusion.4
  101.9 1.7 reduce_sum.147
  104.2 2.0 fusion.88
  106.2 1.1 pad_maximum_fusion.5
  107.4 1.7 reduce_sum.148
  109.0 1.1 reduce_sum.156
  110.1 1.0 fusion.80
  112.1 1.7 reduce_sum.146
  114.4 2.1 fusion.92
  116.6 0.9 pad_maximum_fusion.6
  117.5 1.7 reduce_sum.149
  119.9 1.9 fusion.132
  122.6 1.7 reduce_sum.152
  124.3 1.0 fusion.100
  126.3 1.7 reduce_sum.151
  128.6 2.1 fusion.96
  130.7 1.1 pad_maximum_fusion.7
  131.8 1.7 reduce_sum.150
  133.5 1.7 reduce_sum.154
  135.8 1.4 constant_dynamic-update-slice_fusion.13
  137.2 1.4 constant_dynamic-update-slice_fusion.12
  138.6 1.4 constant_dynamic-update-slice_fusion.11
  139.9 1.4 constant_dynamic-update-slice_fusion.10
  141.3 1.4 constant_dynamic-update-slice_fusion.9
  142.6 1.4 constant_dynamic-update-slice_fusion.8
  144.0 1.4 constant_dynamic-update-slice_fusion.7
  145.4 1.4 constant_dynamic-update-slice_fusion.6
  146.7 1.4 constant_dynamic-update-slice_fusion.5
  148.1 1.4 constant_dynamic-update-slice_fusion.4
  150.7 1.4 constant_dynamic-update-slice_fusion.1
  152.6 2.0 convolution_bitcast_fusion
  154.8 4.2 %convolution_bitcast_fusion.1 = f32[1,256,256]{2,1,0:T(8,128)S(1)} fusion(f32[512,512]{0,1:T(8,128)S(1)} %copy-done.4, f32[256,256]{0,1:T(8,128)} %get-tuple-element.37, f32[256,256]{0,1:T(8,128)S(1)} %copy-done.21, f32[256,256]{0,1:T(8,128)} %get-tuple-element.57, f32[256,256]{0,1:T(8,128)} %get-tuple-element.56, f32[256,256]{0,1:T(8,128)} %get-tuple-element.97, ...), kind=kOutput, calls=%fused_computation.3 | convolution fusion | flops 406716416 | bytes 9175040 | tf_op jit(solution)/shard_map/dot_general | solution.py:109
  159.0 1.0 copy.30
  160.0 3.5 %all-to-all-start.2 = ((f32[2,256,256]{1,0,2:T(2,128)}), f32[2,256,256]{1,0,2:T(2,128)S(1)}, u32[]{:S(2)}, u32[]{:S(2)}) async-start(f32[2,256,256]{1,0,2:T(2,128)} %copy.30), calls=%async_computation.2 | async-start | bytes 1048576 | tf_op jit(solution)/shard_map/all_to_all | solution.py:111
  163.7 16.6 %all-to-all-done.2 = f32[2,256,256]{1,0,2:T(2,128)S(1)} async-done(((f32[2,256,256]{1,0,2:T(2,128)}), f32[2,256,256]{1,0,2:T(2,128)S(1)}, u32[]{:S(2)}, u32[]{:S(2)}) %all-to-all-start.2) | async-done | bytes 524320 | tf_op jit(solution)/shard_map/all_to_all | solution.py:111
  180.7 2.2 convolution_convert_fusion
  183.8 72.7 %reduce-scatter.2.cloned.1.call-done = bf16[256,256]{1,0:T(8,128)(2,1)} async-done(((bf16[256,4096]{1,0:T(8,128)(2,1)}), bf16[256,256]{1,0:T(8,128)(2,1)}) %reduce-scatter.2.cloned.1.call-update) | async-done | bytes 131088 | tf_op jit(solution)/shard_map/reduce_scatter | solution.py:119
  (138 shorter events, 14.5 us)
Async XLA Ops:
  7.2 57.5 %copy-start = (bf16[256,4096]{1,0:T(8,128)(2,1)S(1)}, bf16[256,4096]{1,0:T(8,128)(2,1)}, u32[]{:S(2)}) copy-start(bf16[256,4096]{1,0:T(8,128)(2,1)} %param.10) | copy-start | bytes 6291460
  7.2 57.4 %all-gather.2.cloned.1.call-start = ((), (), s32[]{:S(2)}) async-start(), calls=%async_computation.4 | async-start | bytes 2228224 | tf_op jit(solution)/shard_map/all_gather | solution.py:80
  9.8 21.6 %all-to-all-start = ((bf16[2,256,256]{1,0,2:T(2,128)(2,1)}), bf16[2,256,256]{1,0,2:T(2,128)(2,1)S(1)}, u32[]{:S(2)}, u32[]{:S(2)}) async-start(bf16[2,256,256]{1,0,2:T(2,128)(2,1)} %copy.25), calls=%async_computation | async-start | bytes 524288 | tf_op jit(solution)/shard_map/all_to_all | solution.py:76
  20.8 43.9 %copy-start.10 = (bf16[256,256]{0,1:T(8,128)(2,1)}, bf16[256,256]{0,1:T(8,128)(2,1)S(1)}, u32[]{:S(2)}) copy-start(bf16[256,256]{0,1:T(8,128)(2,1)S(1)} %copy.24) | copy-start | bytes 393220
  22.7 54.2 %copy-start.2 = (f32[256,512]{1,0:T(8,128)}, f32[256,512]{1,0:T(8,128)S(1)}, u32[]{:S(2)}) copy-start(f32[256,512]{1,0:T(8,128)S(1)} %fusion.170) | copy-start | bytes 1572868
  26.8 9.1 %copy-start.3 = (f32[256,512]{1,0:T(8,128)}, f32[256,512]{1,0:T(8,128)S(1)}, u32[]{:S(2)}) copy-start(f32[256,512]{1,0:T(8,128)S(1)} %get-tuple-element.153) | copy-start | bytes 1572868
  67.7 20.9 %all-to-all-start.1 = ((f32[256,16,16]{0,2,1:T(8,128)}), f32[256,16,16]{0,2,1:T(8,128)S(1)}, u32[]{:S(2)}, u32[]{:S(2)}) async-start(f32[256,16,16]{0,2,1:T(8,128)} %bitcast.38), calls=%async_computation.1 | async-start | bytes 524288 | tf_op jit(solution)/shard_map/all_to_all | solution.py:87
  78.5 11.7 %copy-start.1 = (f32[512,256]{0,1:T(8,128)}, f32[512,256]{0,1:T(8,128)S(1)}, u32[]{:S(2)}) copy-start(f32[512,256]{0,1:T(8,128)S(1)} %convolution_add_fusion) | copy-start | bytes 1572868
  78.6 14.1 %copy-start.25 = (f32[512,16]{0,1:T(8,128)}, f32[512,16]{0,1:T(8,128)S(1)}, u32[]{:S(2)}) copy-start(f32[512,16]{0,1:T(8,128)S(1)} %slice.604) | copy-start | bytes 98308
  78.6 3.3 %copy-start.22 = (f32[512,32]{0,1:T(8,128)}, f32[512,32]{0,1:T(8,128)S(1)}, u32[]{:S(2)}) copy-start(f32[512,32]{0,1:T(8,128)S(1)} %slice.601) | copy-start | bytes 196612
  78.6 2.2 copy-start.12
  78.7 3.2 %copy-start.9 = (f32[512,80]{0,1:T(8,128)}, f32[512,80]{0,1:T(8,128)S(1)}, u32[]{:S(2)}) copy-start(f32[512,80]{0,1:T(8,128)S(1)} %slice.592) | copy-start | bytes 491524
  78.7 3.2 %copy-start.8 = (f32[512,96]{0,1:T(8,128)}, f32[512,96]{0,1:T(8,128)S(1)}, u32[]{:S(2)}) copy-start(f32[512,96]{0,1:T(8,128)S(1)} %slice.589) | copy-start | bytes 589828
  78.7 3.2 %copy-start.6 = (f32[512,112]{0,1:T(8,128)}, f32[512,112]{0,1:T(8,128)S(1)}, u32[]{:S(2)}) copy-start(f32[512,112]{0,1:T(8,128)S(1)} %slice.586) | copy-start | bytes 688132
  78.7 1.4 copy-start.5
  90.2 2.5 copy-start.40
  90.2 2.5 copy-start.41
  95.4 4.5 %slice-start.5 = ((f32[512,256]{0,1:T(8,128)}), f32[512,208]{0,1:T(8,128)S(1)}, s32[]{:S(2)}) async-start(f32[512,256]{0,1:T(8,128)} %copy-done.1), calls=%async_computation.11 | async-start | bytes 851968 | tf_op jit(solution)/shard_map/slice | solution.py:64
  95.4 4.5 %copy-start.38 = (f32[256,16]{0,1:T(8,128)S(1)}, f32[256,16]{0,1:T(8,128)}, u32[]{:S(2)}) copy-start(f32[256,16]{0,1:T(8,128)} %get-tuple-element.84) | copy-start | bytes 49156
  95.4 4.5 %copy-start.39 = (f32[256,16]{0,1:T(8,128)S(1)}, f32[256,16]{0,1:T(8,128)}, u32[]{:S(2)}) copy-start(f32[256,16]{0,1:T(8,128)} %get-tuple-element.85) | copy-start | bytes 49156
  100.9 3.3 %slice-start.4 = ((f32[512,256]{0,1:T(8,128)}), f32[512,192]{0,1:T(8,128)S(1)}, s32[]{:S(2)}) async-start(f32[512,256]{0,1:T(8,128)} %copy-done.1), calls=%async_computation.10 | async-start | bytes 786432 | tf_op jit(solution)/shard_map/slice | solution.py:64
  106.2 3.9 %slice-start.6 = ((f32[512,256]{0,1:T(8,128)}), f32[512,224]{0,1:T(8,128)S(1)}, s32[]{:S(2)}) async-start(f32[512,256]{0,1:T(8,128)} %copy-done.1), calls=%async_computation.12 | async-start | bytes 917504 | tf_op jit(solution)/shard_map/slice | solution.py:64
  106.2 3.9 %copy-start.23 = (f32[512,32]{0,1:T(8,128)S(1)}, f32[512,32]{0,1:T(8,128)}, u32[]{:S(2)}) copy-start(f32[512,32]{0,1:T(8,128)} %copy-done.22) | copy-start | bytes 196612
  106.2 3.9 %copy-start.36 = (f32[256,16]{0,1:T(8,128)S(1)}, f32[256,16]{0,1:T(8,128)}, u32[]{:S(2)}) copy-start(f32[256,16]{0,1:T(8,128)} %get-tuple-element.86) | copy-start | bytes 49156
  106.2 3.9 %copy-start.37 = (f32[256,16]{0,1:T(8,128)S(1)}, f32[256,16]{0,1:T(8,128)}, u32[]{:S(2)}) copy-start(f32[256,16]{0,1:T(8,128)} %get-tuple-element.87) | copy-start | bytes 49156
  111.2 3.3 %slice-start.3 = ((f32[512,256]{0,1:T(8,128)}), f32[512,176]{0,1:T(8,128)S(1)}, s32[]{:S(2)}) async-start(f32[512,256]{0,1:T(8,128)} %copy-done.1), calls=%async_computation.9 | async-start | bytes 720896 | tf_op jit(solution)/shard_map/slice | solution.py:64
  116.6 3.3 %slice-start = ((f32[512,256]{0,1:T(8,128)}), f32[512,128]{0,1:T(8,128)S(1)}, s32[]{:S(2)}) async-start(f32[512,256]{0,1:T(8,128)} %copy-done.1), calls=%async_computation.6 | async-start | bytes 524288 | tf_op jit(solution)/shard_map/slice | solution.py:64
  116.6 3.3 %copy-start.26 = (f32[512,16]{0,1:T(8,128)S(1)}, f32[512,16]{0,1:T(8,128)}, u32[]{:S(2)}) copy-start(f32[512,16]{0,1:T(8,128)} %copy-done.25) | copy-start | bytes 98308
  116.6 3.3 %copy-start.33 = (f32[256,16]{0,1:T(8,128)S(1)}, f32[256,16]{0,1:T(8,128)}, u32[]{:S(2)}) copy-start(f32[256,16]{0,1:T(8,128)} %get-tuple-element.60) | copy-start | bytes 49156
  116.6 3.3 %copy-start.34 = (f32[256,16]{0,1:T(8,128)S(1)}, f32[256,16]{0,1:T(8,128)}, u32[]{:S(2)}) copy-start(f32[256,16]{0,1:T(8,128)} %get-tuple-element.61) | copy-start | bytes 49156
  119.8 4.5 %slice-start.1 = ((f32[512,256]{0,1:T(8,128)}), f32[512,144]{0,1:T(8,128)S(1)}, s32[]{:S(2)}) async-start(f32[512,256]{0,1:T(8,128)} %copy-done.1), calls=%async_computation.7 | async-start | bytes 589824 | tf_op jit(solution)/shard_map/slice | solution.py:64
  119.8 4.5 %copy-start.7 = (f32[512,112]{0,1:T(8,128)S(1)}, f32[512,112]{0,1:T(8,128)}, u32[]{:S(2)}) copy-start(f32[512,112]{0,1:T(8,128)} %copy-done.6) | copy-start | bytes 688132
  119.8 4.5 %copy-start.31 = (f32[256,16]{0,1:T(8,128)S(1)}, f32[256,16]{0,1:T(8,128)}, u32[]{:S(2)}) copy-start(f32[256,16]{0,1:T(8,128)} %get-tuple-element.76) | copy-start | bytes 49156
  119.8 4.5 %copy-start.32 = (f32[256,16]{0,1:T(8,128)S(1)}, f32[256,16]{0,1:T(8,128)}, u32[]{:S(2)}) copy-start(f32[256,16]{0,1:T(8,128)} %get-tuple-element.77) | copy-start | bytes 49156
  125.3 3.3 %slice-start.2 = ((f32[512,256]{0,1:T(8,128)}), f32[512,160]{0,1:T(8,128)S(1)}, s32[]{:S(2)}) async-start(f32[512,256]{0,1:T(8,128)} %copy-done.1), calls=%async_computation.8 | async-start | bytes 655360 | tf_op jit(solution)/shard_map/slice | solution.py:64
  125.3 3.3 %copy-start.30 = (f32[256,16]{0,1:T(8,128)S(1)}, f32[256,16]{0,1:T(8,128)}, u32[]{:S(2)}) copy-start(f32[256,16]{0,1:T(8,128)} %get-tuple-element.78) | copy-start | bytes 49156
  125.3 3.3 %copy-start.35 = (f32[256,16]{0,1:T(8,128)S(1)}, f32[256,16]{0,1:T(8,128)}, u32[]{:S(2)}) copy-start(f32[256,16]{0,1:T(8,128)} %get-tuple-element.79) | copy-start | bytes 49156
  130.6 4.5 %copy-start.29 = (f32[512,16]{0,1:T(8,128)S(1)}, f32[512,16]{0,1:T(8,128)}, u32[]{:S(2)}) copy-start(f32[512,16]{0,1:T(8,128)} %reduce_sum.145) | copy-start | bytes 98308
  130.6 19.4 %copy-start.28 = (f32[512,16]{0,1:T(8,128)S(1)}, f32[512,16]{0,1:T(8,128)}, u32[]{:S(2)}) copy-start(f32[512,16]{0,1:T(8,128)} %reduce_sum.157) | copy-start | bytes 98308
  130.6 21.4 %copy-start.27 = (f32[512,16]{0,1:T(8,128)S(1)}, f32[512,16]{0,1:T(8,128)}, u32[]{:S(2)}) copy-start(f32[512,16]{0,1:T(8,128)} %reduce_sum.159) | copy-start | bytes 98308
  130.7 22.0 %copy-start.4 = (f32[512,512]{0,1:T(8,128)S(1)}, f32[512,512]{0,1:T(8,128)}, u32[]{:S(2)}) copy-start(f32[512,512]{0,1:T(8,128)} %maximum_bitcast_fusion) | copy-start | bytes 3145732
  131.8 22.9 %copy-start.13 = (f32[256,256]{0,1:T(8,128)S(1)}, f32[256,256]{0,1:T(8,128)}, u32[]{:S(2)}) copy-start(f32[256,256]{0,1:T(8,128)} %get-tuple-element.148) | copy-start | bytes 786436
  135.2 19.5 %copy-start.14 = (f32[256,256]{0,1:T(8,128)S(1)}, f32[256,256]{0,1:T(8,128)}, u32[]{:S(2)}) copy-start(f32[256,256]{0,1:T(8,128)} %get-tuple-element.149) | copy-start | bytes 786436
  135.2 19.5 %copy-start.15 = (f32[256,256]{0,1:T(8,128)S(1)}, f32[256,256]{0,1:T(8,128)}, u32[]{:S(2)}) copy-start(f32[256,256]{0,1:T(8,128)} %get-tuple-element.158) | copy-start | bytes 786436
  135.2 19.5 %copy-start.16 = (f32[256,256]{0,1:T(8,128)S(1)}, f32[256,256]{0,1:T(8,128)}, u32[]{:S(2)}) copy-start(f32[256,256]{0,1:T(8,128)} %get-tuple-element.159) | copy-start | bytes 786436
  135.2 19.5 %copy-start.17 = (f32[256,256]{0,1:T(8,128)S(1)}, f32[256,256]{0,1:T(8,128)}, u32[]{:S(2)}) copy-start(f32[256,256]{0,1:T(8,128)} %get-tuple-element.160) | copy-start | bytes 786436
  135.2 19.5 %copy-start.18 = (f32[256,256]{0,1:T(8,128)S(1)}, f32[256,256]{0,1:T(8,128)}, u32[]{:S(2)}) copy-start(f32[256,256]{0,1:T(8,128)} %get-tuple-element.161) | copy-start | bytes 786436
  135.2 19.5 %copy-start.19 = (f32[256,256]{0,1:T(8,128)S(1)}, f32[256,256]{0,1:T(8,128)}, u32[]{:S(2)}) copy-start(f32[256,256]{0,1:T(8,128)} %get-tuple-element.162) | copy-start | bytes 786436
  135.2 19.5 %copy-start.20 = (f32[256,256]{0,1:T(8,128)S(1)}, f32[256,256]{0,1:T(8,128)}, u32[]{:S(2)}) copy-start(f32[256,256]{0,1:T(8,128)} %get-tuple-element.163) | copy-start | bytes 786436
  135.2 19.5 %copy-start.21 = (f32[256,256]{0,1:T(8,128)S(1)}, f32[256,256]{0,1:T(8,128)}, u32[]{:S(2)}) copy-start(f32[256,256]{0,1:T(8,128)} %get-tuple-element.36) | copy-start | bytes 786436
  159.0 4.6 %copy-start.24 = (bf16[256,256]{1,0:T(8,128)(2,1)S(1)}, bf16[256,256]{1,0:T(8,128)(2,1)}, u32[]{:S(2)}) copy-start(bf16[256,256]{1,0:T(8,128)(2,1)} %param.6) | copy-start | bytes 393220
  159.0 21.7 %copy-start.11 = (bf16[256,256]{0,1:T(8,128)(2,1)S(1)}, bf16[256,256]{0,1:T(8,128)(2,1)}, u32[]{:S(2)}) copy-start(bf16[256,256]{0,1:T(8,128)(2,1)} %copy-done.10) | copy-start | bytes 393220
  159.0 21.7 %copy-start.42 = (f32[256]{0:T(256)S(1)}, f32[256]{0:T(256)}, u32[]{:S(2)}) copy-start(f32[256]{0:T(256)} %param.9) | copy-start | bytes 3076
  160.0 20.2 %all-to-all-start.2 = ((f32[2,256,256]{1,0,2:T(2,128)}), f32[2,256,256]{1,0,2:T(2,128)S(1)}, u32[]{:S(2)}, u32[]{:S(2)}) async-start(f32[2,256,256]{1,0,2:T(2,128)} %copy.30), calls=%async_computation.2 | async-start | bytes 1048576 | tf_op jit(solution)/shard_map/all_to_all | solution.py:111
  163.5 93.0 %reduce-scatter.2.cloned.1.call-start = ((), (), s32[]{:S(2)}) async-start(), calls=%async_computation.5 | async-start | bytes 2228224 | tf_op jit(solution)/shard_map/reduce_scatter | solution.py:119
Sparse Core Ops, SparseCore 0:
  10.4 54.1 all-gather.1
  183.0 73.4 reduce-scatter.1

commit v2 on v1

--- a/solution.py
+++ b/solution.py
@@ -76,8 +76,12 @@
     pair_t = lax.all_to_all(pair, "ctx", 2, 2, tiled=True)
     signal_t, taps_t = pair_t[0], pair_t[1]
 
+    ch_count = lax.axis_size("ch")
+    cot_rows = lax.all_to_all(
+        jnp.tile(cotangent, (1, ch_count)), "ch", 1, 1, tiled=True
+    )
     upstream = lax.dot_general(
-        lax.all_gather(cotangent, "ch", axis=1, tiled=True),
+        cot_rows,
         w_out,
         (((1,), (1,)), ((), ())),
         preferred_element_type=jnp.float32,
@@ -107,17 +111,21 @@
     lag_spec = jnp.concatenate(lag_terms, axis=1)
 
     convolved_t = jnp.dot(inverse[block_len:], running, precision=exact_prec)
-    filter_grad_t = jnp.dot(inverse[:block_len], lag_spec, precision=exact_prec)
-    back = lax.all_to_all(
-        jnp.stack([convolved_t, filter_grad_t]), "ctx", 2, 2, tiled=True
-    )
-    convolved, filter_grad = back[0], back[1]
+    convolved = lax.all_to_all(convolved_t, "ctx", 1, 1, tiled=True)
 
     mixed_sum = convolved + skip_gain[None, :] * inputs.astype(jnp.float32)
     gated_rows = (gate_wide * mixed_sum).astype(jnp.bfloat16)
     partial_out = jnp.dot(gated_rows, w_out, preferred_element_type=jnp.float32)
-    output = lax.psum_scatter(
-        partial_out.astype(jnp.bfloat16), "ch", scatter_dimension=1, tiled=True
+    pieces = lax.all_to_all(partial_out.astype(jnp.bfloat16), "ch", 1, 0, tiled=True)
+
+    filter_grad_t = jnp.dot(inverse[:block_len], lag_spec, precision=exact_prec)
+    filter_grad = lax.all_to_all(filter_grad_t, "ctx", 1, 1, tiled=True)
+
+    output = (
+        pieces.astype(jnp.float32)
+        .reshape(ch_count, block_len, channels)
+        .sum(axis=0)
+        .astype(jnp.bfloat16)
     )
     return (output, filter_grad)
 

time: 266 us -> 234 us (0.88)
  waiting for transfers between devices: 126 us -> 69 us
  blocking collectives: 0 us -> 21.4 us
  between operations: 14.7 us -> 1.09 us
  local copies, waits for them, and re-layouts: 28.6 us -> 35.9 us
  other arithmetic: 54.5 us -> 61.6 us
  starting transfers between devices: 22.8 us -> 26.2 us
    reduce_scatter x1 -> x0, waiting for transfers between devices: 72.7 us -> none  [body(): lax.psum_scatter(partial_out.astype(jnp.bfloat16), 'ch', scatter_dimensio...]
    all_to_all x2 -> x4, waiting for transfers between devices: 20 us -> 62.7 us  [the longest x1 33.6 us: body(): lax.all_to_all(partial_out.astype(jnp.bfloat16), 'ch', 1, 0, tiled=True)]
    all_gather x1 -> x0, waiting for transfers between devices: 27.5 us -> none  [body(): lax.all_gather(cotangent, 'ch', axis=1, tiled=True)]
    all_to_all x0 -> x1, blocking collectives: none -> 21.4 us  [body(): pair_t = lax.all_to_all(pair, 'ctx', 2, 2, tiled=True)]
    all_to_all x2 -> x4, starting transfers between devices: 13.4 us -> 21.4 us  [the longest x1 6.94 us: body(): lax.all_to_all(jnp.tile(cotangent, (1, ch_count)), 'ch', 1, 1, tiled=True)]
    all_to_all x0 -> x2, local copies, waits for them, and re-layouts: none -> 5.41 us  [the longest x1 3.89 us: body(): lax.all_to_all(jnp.tile(cotangent, (1, ch_count)), 'ch', 1, 1, tiled=True)]
    all_to_all x1, starting transfers between devices: 9.29 us -> 4.71 us  [body(): grad_t = lax.all_to_all(grad_mixed, 'ctx', 1, 1, tiled=True)]
    reduce_sum x16, other arithmetic: 20.4 us -> 24.3 us  [body(): lag_terms.append(term.reshape(term.shape[0], ctx_count, width).sum(axis=1))]
  transfers between devices with their start and end apart: 5 -> 5, of which waited for: 5 -> 4; matrix products, arithmetic and copies ran while one was open for 9% -> 21% of each run, Pallas kernels for 0% -> 0%
where the time goes in v2:
time: 234 us; the launch traced here: 231 us
  waiting for transfers between devices  69 us (29%)
  other arithmetic  61.6 us (26%)
  local copies, waits for them, and re-layouts  35.9 us (15%)
  starting transfers between devices  26.2 us (11%)
  blocking collectives  21.4 us (9%)
  matrix products  16 us (7%)
    all_to_all x1, waiting for transfers between devices, body(): lax.all_to_all(partial_out.astype(jnp.bfloat16), 'ch', 1, 0, tiled=True)  33.6 us
    reduce_sum x16, other arithmetic, body(): lag_terms.append(term.reshape(term.shape[0], ctx_count, width).sum(axis=1))  24.3 us
    unnamed x82, local copies, waits for them, and re-layouts  23.8 us
    all_to_all x1, blocking collectives, body(): pair_t = lax.all_to_all(pair, 'ctx', 2, 2, tiled=True)  21.4 us
    all_to_all x1, waiting for transfers between devices, body(): lax.all_to_all(jnp.tile(cotangent, (1, ch_count)), 'ch', 1, 1, tiled=True)  20.8 us
    sub x11, other arithmetic, spec_product(): real_part = first_real * second_real - others * first_imag * second_imag  16.1 us
    concatenate x9, other arithmetic, conj_product(): return jnp.concatenate([real_part, imag_part], axis=-2)  9.37 us
    all_to_all x1, waiting for transfers between devices, body(): filter_grad = lax.all_to_all(filter_grad_t, 'ctx', 1, 1, tiled=True)  8.27 us
  transfers between devices with their start and end apart: 5, of which 4 were waited for; matrix products, arithmetic and copies ran while one was open for 21% of the time, Pallas kernels for 0%

profile of v2, /device:TPU:1, one launch (start us, length us, event | category | flops | bytes accessed | tf_op | source)
XLA Modules:
  0.0 231.1 jit_solution(9265646488986018263)
XLA Ops:
  0.6 1.1 pad_maximum_fusion.17
  2.0 21.4 %all_to_all.63 = bf16[2,256,256]{1,0,2:T(2,128)(2,1)S(1)} all-to-all(bf16[2,256,256]{1,0,2:T(2,128)(2,1)S(1)} %copy.27), channel_id=1, replica_groups=mesh['ctx'=16,'ch'=16] {'ctx'}, dimensions={2} | all-to-all | bytes 524288 | tf_op jit(solution)/shard_map/all_to_all | solution.py:76
  23.3 2.4 %tile.279 = bf16[256,16,256]{2,0,1:T(8,128)(2,1)} broadcast(bf16[256,256]{1,0:T(8,128)(2,1)} %param.11), dimensions={0,2} | broadcast | bytes 2228224 | tf_op jit(solution)/shard_map/tile | solution.py:81
  25.7 6.9 %all-to-all-start.3 = ((bf16[256,16,256]{2,0,1:T(8,128)(2,1)}), bf16[256,16,256]{2,0,1:T(8,128)(2,1)}, u32[]{:S(2)}, u32[]{:S(2)}) async-start(bf16[256,16,256]{2,0,1:T(8,128)(2,1)} %tile.279), calls=%async_computation.3 | async-start | bytes 4194304 | tf_op jit(solution)/shard_map/all_to_all | solution.py:80
  33.6 1.9 fusion.171
  35.6 2.0 multiply_multiply_fusion
  37.5 2.0 negate_select_fusion.2
  39.6 1.1 maximum_bitcast_fusion
  40.7 1.2 fusion.193
  44.5 1.4 convolution_add_fusion
  45.9 20.8 %all-to-all-done.3 = bf16[256,16,256]{2,0,1:T(8,128)(2,1)} async-done(((bf16[256,16,256]{2,0,1:T(8,128)(2,1)}), bf16[256,16,256]{2,0,1:T(8,128)(2,1)}, u32[]{:S(2)}, u32[]{:S(2)}) %all-to-all-start.3) | async-done | bytes 2097184 | tf_op jit(solution)/shard_map/all_to_all | solution.py:80
  66.7 3.9 %copy.32 = bf16[256,16,256]{0,2,1:T(8,128)(2,1)} copy(bf16[256,16,256]{2,0,1:T(8,128)(2,1)} %all-to-all-done.3) | data formatting | bytes 4194304 | tf_op jit(solution)/shard_map/all_to_all | solution.py:80
  70.6 3.0 %convolution_multiply_fusion = f32[256,256]{0,1:T(8,128)} fusion(bf16[256,4096]{1,0:T(8,128)(2,1)S(1)} %copy-done, bf16[256,4096]{0,1:T(8,128)(2,1)} %bitcast.447, bf16[256,256]{0,1:T(8,128)(2,1)S(1)} %copy.26), kind=kOutput, calls=%fused_computation.3 | convolution fusion | flops 537001984 | bytes 4587520 | tf_op jit(solution)/shard_map/dot_general | solution.py:83
  73.6 4.7 %all-to-all-start.4 = ((f32[256,16,16]{0,2,1:T(8,128)}), f32[256,16,16]{0,2,1:T(8,128)}, u32[]{:S(2)}, u32[]{:S(2)}) async-start(f32[256,16,16]{0,2,1:T(8,128)} %bitcast.40), calls=%async_computation.4 | async-start | bytes 524288 | tf_op jit(solution)/shard_map/all_to_all | solution.py:91
  78.4 1.4 fusion.175
  81.8 1.4 fusion.130
  83.9 6.3 %all-to-all-done.4 = f32[256,16,16]{0,2,1:T(8,128)} async-done(((f32[256,16,16]{0,2,1:T(8,128)}), f32[256,16,16]{0,2,1:T(8,128)}, u32[]{:S(2)}, u32[]{:S(2)}) %all-to-all-start.4) | async-done | bytes 262176 | tf_op jit(solution)/shard_map/all_to_all | solution.py:91
  90.2 1.7 fusion.172
  94.0 1.7 reduce_sum.165
  95.7 2.2 fusion.102
  99.4 2.1 fusion.98
  103.1 2.1 fusion.94
  105.2 1.1 pad_maximum_fusion.6
  106.4 1.7 reduce_sum.162
  109.1 1.1 pad_maximum_fusion.5
  110.2 1.7 reduce_sum.161
  111.9 2.0 fusion.86
  113.9 1.1 pad_maximum_fusion.4
  115.1 1.7 reduce_sum.160
  117.9 1.2 pad_maximum_fusion.3
  119.1 1.7 reduce_sum.159
  121.8 1.1 pad_maximum_fusion.2
  122.9 1.7 reduce_sum.158
  128.2 1.7 reduce_sum.166
  129.9 1.7 reduce_sum.167
  131.6 1.7 reduce_sum.168
  133.3 1.7 reduce_sum.169
  135.0 1.7 reduce_sum.170
  136.7 5.0 %fusion.6 = f32[256,256]{0,1:T(8,128)} fusion(f32[512,512]{0,1:T(8,128)S(1)} %copy-done.6, f32[256,256]{0,1:T(8,128)} %get-tuple-element.41, f32[256,256]{0,1:T(8,128)} %get-tuple-element.40, f32[256,256]{0,1:T(8,128)} %get-tuple-element.59, f32[256,256]{0,1:T(8,128)} %get-tuple-element.58, f32[256,256]{0,1:T(8,128)} %get-tuple-element.97, ...), kind=kOutput, calls=%fused_computation.45 | convolution fusion | flops 406716416 | bytes 9175040 | tf_op jit(solution)/shard_map/dot_general | solution.py:113
  141.6 3.4 %all-to-all-start.1 = ((f32[256,16,16]{0,2,1:T(8,128)}), f32[256,16,16]{0,2,1:T(8,128)S(1)}, u32[]{:S(2)}, u32[]{:S(2)}) async-start(f32[256,16,16]{0,2,1:T(8,128)} %bitcast.466), calls=%async_computation.1 | async-start | bytes 524288 | tf_op jit(solution)/shard_map/all_to_all | solution.py:114
  145.1 1.4 constant_dynamic-update-slice_fusion.14
  146.5 1.4 constant_dynamic-update-slice_fusion.13
  147.9 1.4 constant_dynamic-update-slice_fusion.12
  149.2 1.4 constant_dynamic-update-slice_fusion.11
  150.6 1.4 constant_dynamic-update-slice_fusion.10
  152.0 1.4 constant_dynamic-update-slice_fusion.9
  153.3 1.4 constant_dynamic-update-slice_fusion.8
  154.7 1.4 constant_dynamic-update-slice_fusion.7
  156.1 1.4 constant_dynamic-update-slice_fusion.6
  157.4 1.4 constant_dynamic-update-slice_fusion.5
  158.8 1.4 constant_dynamic-update-slice_fusion.4
  160.2 1.4 constant_dynamic-update-slice_fusion.3
  161.6 1.4 constant_dynamic-update-slice_fusion.2
  162.9 1.7 reduce_sum.171
  164.6 1.7 reduce_sum.172
  166.3 1.4 constant_dynamic-update-slice_fusion.1
  167.7 1.4 constant_dynamic-update-slice_fusion
  169.0 2.4 %fusion.4 = f32[256,256]{0,1:T(8,128)} fusion(f32[512,256]{0,1:T(8,128)} %constant_dynamic-update-slice_fusion, f32[512,512]{0,1:T(8,128)S(1)} %copy-done.6), kind=kOutput, calls=%fused_computation.42 | convolution fusion | flops 402653184 | bytes 1310720 | tf_op jit(solution)/shard_map/dot_general | solution.py:121
  171.4 6.6 %all-to-all-start.5 = ((f32[256,16,16]{0,2,1:T(8,128)}), f32[256,16,16]{0,2,1:T(8,128)S(1)}, u32[]{:S(2)}, u32[]{:S(2)}) async-start(f32[256,16,16]{0,2,1:T(8,128)} %bitcast.467), calls=%async_computation.5 | async-start | bytes 524288 | tf_op jit(solution)/shard_map/all_to_all | solution.py:122
  179.8 1.5 copy.41
  181.3 8.3 %all-to-all-done.5 = f32[256,16,16]{0,2,1:T(8,128)S(1)} async-done(((f32[256,16,16]{0,2,1:T(8,128)}), f32[256,16,16]{0,2,1:T(8,128)S(1)}, u32[]{:S(2)}, u32[]{:S(2)}) %all-to-all-start.5) | async-done | bytes 262176 | tf_op jit(solution)/shard_map/all_to_all | solution.py:122
  189.6 4.5 %all-to-all-start.2 = ((bf16[256,16,256]{2,0,1:T(8,128)(2,1)}), bf16[256,16,256]{2,0,1:T(8,128)(2,1)}, u32[]{:S(2)}, u32[]{:S(2)}) async-start(bf16[256,16,256]{2,0,1:T(8,128)(2,1)} %bitcast.446), calls=%async_computation.2 | async-start | bytes 4194304 | tf_op jit(solution)/shard_map/all_to_all | solution.py:119
  194.9 33.6 %all-to-all-done.2 = bf16[256,16,256]{2,0,1:T(8,128)(2,1)} async-done(((bf16[256,16,256]{2,0,1:T(8,128)(2,1)}), bf16[256,16,256]{2,0,1:T(8,128)(2,1)}, u32[]{:S(2)}, u32[]{:S(2)}) %all-to-all-start.2) | async-done | bytes 2097184 | tf_op jit(solution)/shard_map/all_to_all | solution.py:119
  228.5 2.6 %reduce_sum.156 = bf16[256,256]{1,0:T(8,128)(2,1)} reduce(bf16[256,16,256]{2,0,1:T(8,128)(2,1)} %all-to-all-done.2, bf16[]{:T(256)} %constant.33.clone.1), dimensions={1}, to_apply=%region_0.1 | reduce | flops 983040 | bytes 2228226 | tf_op jit(solution)/shard_map/reduce_sum | solution.py:127
  (116 shorter events, 20.9 us)
Async XLA Ops:
  0.6 70.0 %copy-start = (bf16[256,4096]{1,0:T(8,128)(2,1)S(1)}, bf16[256,4096]{1,0:T(8,128)(2,1)}, u32[]{:S(2)}) copy-start(bf16[256,4096]{1,0:T(8,128)(2,1)} %param.10) | copy-start | bytes 6291460
  25.7 7.0 %copy-start.18 = (bf16[256,256]{1,0:T(8,128)(2,1)S(1)}, bf16[256,256]{1,0:T(8,128)(2,1)}, u32[]{:S(2)}) copy-start(bf16[256,256]{1,0:T(8,128)(2,1)} %param.6) | copy-start | bytes 393220
  25.7 7.7 %copy-start.19 = (bf16[256,256]{1,0:T(8,128)(2,1)S(1)}, bf16[256,256]{1,0:T(8,128)(2,1)}, u32[]{:S(2)}) copy-start(bf16[256,256]{1,0:T(8,128)(2,1)} %param.7) | copy-start | bytes 393220
  25.7 41.0 %all-to-all-start.3 = ((bf16[256,16,256]{2,0,1:T(8,128)(2,1)}), bf16[256,16,256]{2,0,1:T(8,128)(2,1)}, u32[]{:S(2)}, u32[]{:S(2)}) async-start(bf16[256,16,256]{2,0,1:T(8,128)(2,1)} %tile.279), calls=%async_computation.3 | async-start | bytes 4194304 | tf_op jit(solution)/shard_map/all_to_all | solution.py:80
  33.6 37.0 %copy-start.10 = (bf16[256,256]{0,1:T(8,128)(2,1)}, bf16[256,256]{0,1:T(8,128)(2,1)S(1)}, u32[]{:S(2)}) copy-start(bf16[256,256]{0,1:T(8,128)(2,1)S(1)} %copy.26) | copy-start | bytes 393220
  35.5 42.8 %copy-start.3 = (f32[256,512]{1,0:T(8,128)}, f32[256,512]{1,0:T(8,128)S(1)}, u32[]{:S(2)}) copy-start(f32[256,512]{1,0:T(8,128)S(1)} %fusion.171) | copy-start | bytes 1572868
  39.6 4.5 %copy-start.5 = (f32[256,512]{1,0:T(8,128)}, f32[256,512]{1,0:T(8,128)S(1)}, u32[]{:S(2)}) copy-start(f32[256,512]{1,0:T(8,128)S(1)} %get-tuple-element.152) | copy-start | bytes 1572868
  45.9 34.0 %copy-start.1 = (f32[512,256]{0,1:T(8,128)}, f32[512,256]{0,1:T(8,128)S(1)}, u32[]{:S(2)}) copy-start(f32[512,256]{0,1:T(8,128)S(1)} %convolution_add_fusion) | copy-start | bytes 1572868
  73.6 16.6 %all-to-all-start.4 = ((f32[256,16,16]{0,2,1:T(8,128)}), f32[256,16,16]{0,2,1:T(8,128)}, u32[]{:S(2)}, u32[]{:S(2)}) async-start(f32[256,16,16]{0,2,1:T(8,128)} %bitcast.40), calls=%async_computation.4 | async-start | bytes 524288 | tf_op jit(solution)/shard_map/all_to_all | solution.py:91
  79.8 2.0 copy-start.7
  79.8 1.9 copy-start.8
  79.9 1.9 copy-start.9
  79.9 0.8 copy-start.12
  79.9 1.8 copy-start.15
  79.9 3.3 %copy-start.16 = (f32[512,32]{0,1:T(8,128)}, f32[512,32]{0,1:T(8,128)S(1)}, u32[]{:S(2)}) copy-start(f32[512,32]{0,1:T(8,128)S(1)} %slice.593) | copy-start | bytes 196612
  80.7 9.5 %copy-start.4 = (f32[256,512]{1,0:T(8,128)S(1)}, f32[256,512]{1,0:T(8,128)}, u32[]{:S(2)}) copy-start(f32[256,512]{1,0:T(8,128)} %copy-done.3) | copy-start | bytes 1572868
  81.8 10.2 %slice-start = ((f32[512,256]{0,1:T(8,128)}), f32[512,128]{0,1:T(8,128)S(1)}, s32[]{:S(2)}) async-start(f32[512,256]{0,1:T(8,128)} %copy-done.1), calls=%async_computation.6 | async-start | bytes 524288 | tf_op jit(solution)/shard_map/slice | solution.py:64
  91.9 3.7 %slice-start.1 = ((f32[512,256]{0,1:T(8,128)}), f32[512,144]{0,1:T(8,128)S(1)}, s32[]{:S(2)}) async-start(f32[512,256]{0,1:T(8,128)} %copy-done.1), calls=%async_computation.7 | async-start | bytes 589824 | tf_op jit(solution)/shard_map/slice | solution.py:64
  95.7 3.8 %slice-start.2 = ((f32[512,256]{0,1:T(8,128)}), f32[512,160]{0,1:T(8,128)S(1)}, s32[]{:S(2)}) async-start(f32[512,256]{0,1:T(8,128)} %copy-done.1), calls=%async_computation.8 | async-start | bytes 655360 | tf_op jit(solution)/shard_map/slice | solution.py:64
  97.8 1.6 copy-start.20
  97.8 1.6 copy-start.29
  99.4 3.7 %slice-start.3 = ((f32[512,256]{0,1:T(8,128)}), f32[512,176]{0,1:T(8,128)S(1)}, s32[]{:S(2)}) async-start(f32[512,256]{0,1:T(8,128)} %copy-done.1), calls=%async_computation.9 | async-start | bytes 720896 | tf_op jit(solution)/shard_map/slice | solution.py:64
  103.1 4.9 %slice-start.4 = ((f32[512,256]{0,1:T(8,128)}), f32[512,192]{0,1:T(8,128)S(1)}, s32[]{:S(2)}) async-start(f32[512,256]{0,1:T(8,128)} %copy-done.1), calls=%async_computation.10 | async-start | bytes 786432 | tf_op jit(solution)/shard_map/slice | solution.py:64
  103.1 4.9 %copy-start.13 = (f32[512,64]{0,1:T(8,128)S(1)}, f32[512,64]{0,1:T(8,128)}, u32[]{:S(2)}) copy-start(f32[512,64]{0,1:T(8,128)} %copy-done.12) | copy-start | bytes 393220
  105.2 2.8 %copy-start.27 = (f32[256,16]{0,1:T(8,128)S(1)}, f32[256,16]{0,1:T(8,128)}, u32[]{:S(2)}) copy-start(f32[256,16]{0,1:T(8,128)} %get-tuple-element.82) | copy-start | bytes 49156
  105.2 2.8 %copy-start.28 = (f32[256,16]{0,1:T(8,128)S(1)}, f32[256,16]{0,1:T(8,128)}, u32[]{:S(2)}) copy-start(f32[256,16]{0,1:T(8,128)} %get-tuple-element.83) | copy-start | bytes 49156
  109.1 2.8 %slice-start.5 = ((f32[512,256]{0,1:T(8,128)}), f32[512,208]{0,1:T(8,128)S(1)}, s32[]{:S(2)}) async-start(f32[512,256]{0,1:T(8,128)} %copy-done.1), calls=%async_computation.11 | async-start | bytes 851968 | tf_op jit(solution)/shard_map/slice | solution.py:64
  111.9 4.9 %slice-start.6 = ((f32[512,256]{0,1:T(8,128)}), f32[512,224]{0,1:T(8,128)S(1)}, s32[]{:S(2)}) async-start(f32[512,256]{0,1:T(8,128)} %copy-done.1), calls=%async_computation.12 | async-start | bytes 917504 | tf_op jit(solution)/shard_map/slice | solution.py:64
  113.9 2.9 %copy-start.17 = (f32[512,32]{0,1:T(8,128)S(1)}, f32[512,32]{0,1:T(8,128)}, u32[]{:S(2)}) copy-start(f32[512,32]{0,1:T(8,128)} %copy-done.16) | copy-start | bytes 196612
  113.9 2.9 %copy-start.25 = (f32[256,16]{0,1:T(8,128)S(1)}, f32[256,16]{0,1:T(8,128)}, u32[]{:S(2)}) copy-start(f32[256,16]{0,1:T(8,128)} %get-tuple-element.86) | copy-start | bytes 49156
  113.9 2.9 %copy-start.26 = (f32[256,16]{0,1:T(8,128)S(1)}, f32[256,16]{0,1:T(8,128)}, u32[]{:S(2)}) copy-start(f32[256,16]{0,1:T(8,128)} %get-tuple-element.87) | copy-start | bytes 49156
  117.9 2.9 %slice-start.7 = ((f32[512,256]{0,1:T(8,128)}), f32[512,240]{0,1:T(8,128)S(1)}, s32[]{:S(2)}) async-start(f32[512,256]{0,1:T(8,128)} %copy-done.1), calls=%async_computation.13 | async-start | bytes 983040 | tf_op jit(solution)/shard_map/slice | solution.py:64
  117.9 2.9 %copy-start.23 = (f32[256,16]{0,1:T(8,128)S(1)}, f32[256,16]{0,1:T(8,128)}, u32[]{:S(2)}) copy-start(f32[256,16]{0,1:T(8,128)} %get-tuple-element.88) | copy-start | bytes 49156
  117.9 2.9 %copy-start.24 = (f32[256,16]{0,1:T(8,128)S(1)}, f32[256,16]{0,1:T(8,128)}, u32[]{:S(2)}) copy-start(f32[256,16]{0,1:T(8,128)} %get-tuple-element.89) | copy-start | bytes 49156
  120.8 3.9 %copy-start.21 = (f32[256,16]{0,1:T(8,128)S(1)}, f32[256,16]{0,1:T(8,128)}, u32[]{:S(2)}) copy-start(f32[256,16]{0,1:T(8,128)} %get-tuple-element.90) | copy-start | bytes 49156
  120.8 3.9 %copy-start.22 = (f32[256,16]{0,1:T(8,128)S(1)}, f32[256,16]{0,1:T(8,128)}, u32[]{:S(2)}) copy-start(f32[256,16]{0,1:T(8,128)} %get-tuple-element.91) | copy-start | bytes 49156
  121.8 2.8 %copy-start.2 = (f32[512,256]{0,1:T(8,128)S(1)}, f32[512,256]{0,1:T(8,128)}, u32[]{:S(2)}) copy-start(f32[512,256]{0,1:T(8,128)} %copy-done.1) | copy-start | bytes 1572868
  125.6 11.0 %copy-start.6 = (f32[512,512]{0,1:T(8,128)S(1)}, f32[512,512]{0,1:T(8,128)}, u32[]{:S(2)}) copy-start(f32[512,512]{0,1:T(8,128)} %maximum_bitcast_fusion) | copy-start | bytes 3145732
  125.6 11.0 %copy-start.14 = (f32[256,256]{0,1:T(8,128)S(1)}, f32[256,256]{0,1:T(8,128)}, u32[]{:S(2)}) copy-start(f32[256,256]{0,1:T(8,128)} %get-tuple-element.148) | copy-start | bytes 786436
  141.6 29.8 %all-to-all-start.1 = ((f32[256,16,16]{0,2,1:T(8,128)}), f32[256,16,16]{0,2,1:T(8,128)S(1)}, u32[]{:S(2)}, u32[]{:S(2)}) async-start(f32[256,16,16]{0,2,1:T(8,128)} %bitcast.466), calls=%async_computation.1 | async-start | bytes 524288 | tf_op jit(solution)/shard_map/all_to_all | solution.py:114
  145.1 32.9 %copy-start.11 = (bf16[256,256]{0,1:T(8,128)(2,1)S(1)}, bf16[256,256]{0,1:T(8,128)(2,1)}, u32[]{:S(2)}) copy-start(bf16[256,256]{0,1:T(8,128)(2,1)} %copy-done.10) | copy-start | bytes 393220
  145.1 32.9 %copy-start.30 = (f32[256]{0:T(256)S(1)}, f32[256]{0:T(256)}, u32[]{:S(2)}) copy-start(f32[256]{0:T(256)} %param.9) | copy-start | bytes 3076
  171.4 18.2 %all-to-all-start.5 = ((f32[256,16,16]{0,2,1:T(8,128)}), f32[256,16,16]{0,2,1:T(8,128)S(1)}, u32[]{:S(2)}, u32[]{:S(2)}) async-start(f32[256,16,16]{0,2,1:T(8,128)} %bitcast.467), calls=%async_computation.5 | async-start | bytes 524288 | tf_op jit(solution)/shard_map/all_to_all | solution.py:122
  189.6 38.9 %all-to-all-start.2 = ((bf16[256,16,256]{2,0,1:T(8,128)(2,1)}), bf16[256,16,256]{2,0,1:T(8,128)(2,1)}, u32[]{:S(2)}, u32[]{:S(2)}) async-start(bf16[256,16,256]{2,0,1:T(8,128)(2,1)} %bitcast.446), calls=%async_computation.2 | async-start | bytes 4194304 | tf_op jit(solution)/shard_map/all_to_all | solution.py:119

commit v3 on v2

--- a/solution.py
+++ b/solution.py
@@ -1,8 +1,11 @@
+import functools
 import math
 
 import jax
 import jax.numpy as jnp
 from jax import lax
+from jax.experimental import pallas as pl
+from jax.experimental.pallas import tpu as pltpu
 from jax.sharding import PartitionSpec as P
 
 exact_prec = lax.Precision.HIGHEST
@@ -64,6 +67,71 @@
     return jnp.concatenate([pad, spec[:, : spec.shape[1] - blocks * width]], axis=1)
 
 
+def to_slabs(spec, blocks, width):
+    bins = spec.shape[0]
+    slab = spec.reshape(bins, blocks, width).transpose(1, 0, 2)
+    return slab.reshape(blocks, bins * width // 128, 128)
+
+
+def from_slabs(slab, width):
+    blocks = slab.shape[0]
+    bins = slab.shape[1] * 128 // width
+    spec = slab.reshape(blocks, bins, width).transpose(1, 0, 2)
+    return spec.reshape(bins, blocks * width)
+
+
+def block_products_kernel(width, seg_ref, taps_ref, grad_ref, conv_ref, lag_ref):
+    blocks, rows, lanes = seg_ref.shape
+    half = rows // 2
+    row_ids = lax.broadcasted_iota(jnp.int32, (half, lanes), 0)
+    lane_ids = lax.broadcasted_iota(jnp.int32, (half, lanes), 1)
+    first_bin = (row_ids == 0) & (lane_ids < width)
+    zero = jnp.zeros((half, lanes), jnp.float32)
+
+    def parts(ref, i):
+        return ref[i, :half, :], ref[i, half:, :]
+
+    for p in range(blocks):
+        acc_re, acc_im = zero, zero
+        for k in range(p + 1):
+            a_re, a_im = parts(taps_ref, k)
+            b_re, b_im = parts(seg_ref, p - k)
+            both_im = a_im * b_im
+            acc_re = acc_re + a_re * b_re - jnp.where(first_bin, 0.0, both_im)
+            acc_im = acc_im + jnp.where(first_bin, both_im, a_re * b_im + a_im * b_re)
+        conv_ref[p, :half, :] = acc_re
+        conv_ref[p, half:, :] = acc_im
+
+    for k in range(blocks):
+        acc_re, acc_im = zero, zero
+        for p in range(k, blocks):
+            a_re, a_im = parts(grad_ref, p)
+            b_re, b_im = parts(seg_ref, p - k)
+            both_im = a_im * b_im
+            acc_re = acc_re + a_re * b_re + jnp.where(first_bin, 0.0, both_im)
+            acc_im = acc_im + jnp.where(first_bin, both_im, a_im * b_re - a_re * b_im)
+        lag_ref[k, :half, :] = acc_re
+        lag_ref[k, half:, :] = acc_im
+
+
+def block_products(seg_slab, taps_slab, grad_slab, width):
+    blocks, rows, lanes = seg_slab.shape
+    pairs = blocks * (blocks + 1)
+    vmem = pl.BlockSpec(memory_space=pltpu.VMEM)
+    shape = jax.ShapeDtypeStruct(seg_slab.shape, jnp.float32)
+    return pl.pallas_call(
+        functools.partial(block_products_kernel, width),
+        out_shape=(shape, shape),
+        in_specs=[vmem, vmem, vmem],
+        out_specs=(vmem, vmem),
+        cost_estimate=pl.CostEstimate(
+            flops=pairs * rows * lanes * 4,
+            bytes_accessed=5 * blocks * rows * lanes * 4,
+            transcendentals=0,
+        ),
+    )(seg_slab, taps_slab, grad_slab)
+
+
 def body(inputs, gating, filter_taps, skip_gain, w_out, cotangent):
     block_len, channels = inputs.shape
     ctx_count = lax.axis_size("ctx")
@@ -96,19 +164,14 @@
     taps_spec = transform(first_half, taps_t)
     grad_spec = transform(second_half, grad_t)
 
-    running = jnp.zeros_like(seg_spec)
-    lag_terms = []
-    for lag in range(ctx_count):
-        shifted = shift_blocks(seg_spec, lag, width)
-        tap_block = taps_spec[:, lag * width : (lag + 1) * width]
-        running = running + spec_product(
-            jnp.tile(tap_block, (1, ctx_count)), shifted, first_bin
-        )
-        term = conj_product(grad_spec, shifted, first_bin)
-        lag_terms.append(
-            term.reshape(term.shape[0], ctx_count, width).sum(axis=1)
-        )
-    lag_spec = jnp.concatenate(lag_terms, axis=1)
+    conv_slab, lag_slab = block_products(
+        to_slabs(seg_spec, ctx_count, width),
+        to_slabs(taps_spec, ctx_count, width),
+        to_slabs(grad_spec, ctx_count, width),
+        width,
+    )
+    running = from_slabs(conv_slab, width)
+    lag_spec = from_slabs(lag_slab, width)
 
     convolved_t = jnp.dot(inverse[block_len:], running, precision=exact_prec)
     convolved = lax.all_to_all(convolved_t, "ctx", 1, 1, tiled=True)

time: 234 us -> 200 us (0.85)
  other arithmetic: 61.6 us -> 11.7 us
  local copies, waits for them, and re-layouts: 35.9 us -> 49.9 us
  Pallas kernels: 0 us -> 4.14 us
  starting transfers between devices: 26.2 us -> 30.3 us
    reduce_sum x16 -> x0, other arithmetic: 24.3 us -> none  [body(): lag_terms.append(term.reshape(term.shape[0], ctx_count, width).sum(axis=1))]
    reshape x0 -> x6, local copies, waits for them, and re-layouts: none -> 22.8 us  [the longest x3 11.8 us: to_slabs(): return slab.reshape(blocks, bins * width // 128, 128)]
    unnamed x82 -> x14, local copies, waits for them, and re-layouts: 23.8 us -> 3.69 us
    sub x12 -> x0, other arithmetic: 16.1 us -> none  [the longest x11 16.1 us: spec_product(): real_part = first_real * second_real - others * first_imag * second_imag]
    transpose x0 -> x4, local copies, waits for them, and re-layouts: none -> 14.1 us  [the longest x2 7.1 us: from_slabs(): spec = slab.reshape(blocks, bins, width).transpose(1, 0, 2)]
    concatenate x9 -> x0, other arithmetic: 9.37 us -> none  [conj_product(): return jnp.concatenate([real_part, imag_part], axis=-2)]
    all_to_all x1, waiting for transfers between devices: 6.31 us -> 0.01 us  [body(): grad_t = lax.all_to_all(grad_mixed, 'ctx', 1, 1, tiled=True)]
    pallas_call x0 -> x1, Pallas kernels: none -> 4.14 us  [block_products(): pl.pallas_call(functools.partial(block_products_kernel, width), out_shape...]
where the time goes in v3:
time: 200 us; the launch traced here: 199 us
  waiting for transfers between devices  66.9 us (33%)
  local copies, waits for them, and re-layouts  49.9 us (25%)
  starting transfers between devices  30.3 us (15%)
  blocking collectives  21.4 us (11%)
  matrix products  13.9 us (7%)
  other arithmetic  11.7 us (6%)
  Pallas kernels  4.14 us (2%)
    all_to_all x1, waiting for transfers between devices, body(): lax.all_to_all(partial_out.astype(jnp.bfloat16), 'ch', 1, 0, tiled=True)  33.6 us
    all_to_all x1, waiting for transfers between devices, body(): lax.all_to_all(jnp.tile(cotangent, (1, ch_count)), 'ch', 1, 1, tiled=True)  24.7 us
    all_to_all x1, blocking collectives, body(): pair_t = lax.all_to_all(pair, 'ctx', 2, 2, tiled=True)  21.4 us
    reshape x3, local copies, waits for them, and re-layouts, to_slabs(): return slab.reshape(blocks, bins * width // 128, 128)  11.8 us
    all_to_all x1, waiting for transfers between devices, body(): filter_grad = lax.all_to_all(filter_grad_t, 'ctx', 1, 1, tiled=True)  8.25 us
    reshape x2, local copies, waits for them, and re-layouts, from_slabs(): spec = slab.reshape(blocks, bins, width).transpose(1, 0, 2)  7.45 us
    all_to_all x1, starting transfers between devices, body(): convolved = lax.all_to_all(convolved_t, 'ctx', 1, 1, tiled=True)  7.26 us
    transpose x2, local copies, waits for them, and re-layouts, from_slabs(): spec = slab.reshape(blocks, bins, width).transpose(1, 0, 2)  7.1 us
  transfers between devices with their start and end apart: 5, of which 4 were waited for; matrix products, arithmetic and copies ran while one was open for 21% of the time, Pallas kernels for 0%

profile of v3, /device:TPU:1, one launch (start us, length us, event | category | flops | bytes accessed | tf_op | source)
XLA Modules:
  0.0 198.8 jit_solution(4531232755204872081)
XLA Ops:
  0.6 0.0 copy-start
  0.6 1.1 pad_maximum_fusion.1
  1.8 0.2 copy.42
  2.0 21.4 %all_to_all.57 = bf16[2,256,256]{1,0,2:T(2,128)(2,1)S(1)} all-to-all(bf16[2,256,256]{1,0,2:T(2,128)(2,1)S(1)} %copy.42), channel_id=1, replica_groups=mesh['ctx'=16,'ch'=16] {'ctx'}, dimensions={2} | all-to-all | bytes 524288 | tf_op jit(solution)/shard_map/all_to_all | solution.py:144
  23.3 2.4 %tile.2 = bf16[256,16,256]{2,0,1:T(8,128)(2,1)} broadcast(bf16[256,256]{1,0:T(8,128)(2,1)} %param.11), dimensions={0,2} | broadcast | bytes 2228224 | tf_op jit(solution)/shard_map/tile | solution.py:149
  25.8 0.0 copy-start.3
  25.8 6.9 %all-to-all-start.1 = ((bf16[256,16,256]{2,0,1:T(8,128)(2,1)}), bf16[256,16,256]{2,0,1:T(8,128)(2,1)}, u32[]{:S(2)}, u32[]{:S(2)}) async-start(bf16[256,16,256]{2,0,1:T(8,128)(2,1)} %tile.2), calls=%async_computation.1 | async-start | bytes 4194304 | tf_op jit(solution)/shard_map/all_to_all | solution.py:148
  32.7 0.0 copy-done.3
  32.7 0.1 copy.41
  32.8 1.9 fusion.16
  34.8 2.0 multiply_multiply_fusion
  36.7 2.0 %negate_select_fusion.2 = (f32[256,512]{1,0:T(8,128)S(1)}, f32[256,512]{1,0:T(8,128)S(1)}) fusion(f32[512]{0:T(512)S(1)} %fusion.24, pred[256]{0:T(512)(128)(4,1)S(1)} %iota_compare_fusion), kind=kLoop, calls=%fused_computation.25 | loop fusion | flops 2490368 | bytes 1050880 | tf_op jit(solution)/shard_map/jit(_where)/select_n | solution.py:22
  38.8 1.0 maximum_bitcast_fusion
  39.8 1.2 fusion.31
  41.0 1.1 copy.61
  42.0 24.7 %all-to-all-done.1 = bf16[256,16,256]{2,0,1:T(8,128)(2,1)} async-done(((bf16[256,16,256]{2,0,1:T(8,128)(2,1)}), bf16[256,16,256]{2,0,1:T(8,128)(2,1)}, u32[]{:S(2)}, u32[]{:S(2)}) %all-to-all-start.1) | async-done | bytes 2097184 | tf_op jit(solution)/shard_map/all_to_all | solution.py:148
  66.7 3.9 %copy.48 = bf16[256,16,256]{0,2,1:T(8,128)(2,1)} copy(bf16[256,16,256]{2,0,1:T(8,128)(2,1)} %all-to-all-done.1) | data formatting | bytes 4194304 | tf_op jit(solution)/shard_map/all_to_all | solution.py:148
  70.6 0.0 copy-done
  70.6 3.0 %convolution_multiply_fusion = f32[256,256]{0,1:T(8,128)} fusion(bf16[256,4096]{1,0:T(8,128)(2,1)S(1)} %copy-done, bf16[256,4096]{0,1:T(8,128)(2,1)} %bitcast.74, bf16[256,256]{0,1:T(8,128)(2,1)S(1)} %copy.41), kind=kOutput, calls=%fused_computation.5 | convolution fusion | flops 537001984 | bytes 4587520 | tf_op jit(solution)/shard_map/dot_general | solution.py:151
  73.6 4.7 %all-to-all-start.2 = ((f32[256,16,16]{0,2,1:T(8,128)}), f32[256,16,16]{0,2,1:T(8,128)}, u32[]{:S(2)}, u32[]{:S(2)}) async-start(f32[256,16,16]{0,2,1:T(8,128)} %bitcast.78), calls=%async_computation.2 | async-start | bytes 524288 | tf_op jit(solution)/shard_map/all_to_all | solution.py:159
  78.4 0.5 fusion.17
  78.8 1.3 convolution_add_fusion
  80.1 3.5 %copy.44 = f32[512,16,16]{2,0,1:T(8,128)} copy(f32[512,16,16]{0,2,1:T(8,128)} %bitcast.76) | data formatting | bytes 1048576 | tf_op jit(solution)/shard_map/reshape | solution.py:72
  83.6 0.0 copy-start.2
  83.6 4.0 %reshape.72.seg_ref = f32[16,64,128]{2,1,0:T(8,128)} reshape(f32[16,512,16]{2,1,0:T(8,128)} %bitcast.70) | data formatting | bytes 1048576 | tf_op jit(solution)/shard_map/reshape | solution.py:73
  87.6 0.0 copy-done.2
  87.6 1.3 convolution_bitcast_fusion.1
  88.9 3.5 %copy.47 = f32[16,512,16]{2,1,0:T(8,128)} copy(f32[16,512,16]{1,2,0:T(8,128)} %convolution_bitcast_fusion.1) | data formatting | bytes 1048576 | tf_op jit(solution)/shard_map/transpose | solution.py:72
  92.4 3.9 %reshape.73.taps_ref = f32[16,64,128]{2,1,0:T(8,128)} reshape(f32[16,512,16]{2,1,0:T(8,128)} %copy.47) | data formatting | bytes 1048576 | tf_op jit(solution)/shard_map/reshape | solution.py:73
  96.3 0.0 all-to-all-done.2
  96.3 2.4 %convolution_bitcast_fusion = f32[16,512,16]{1,2,0:T(8,128)} fusion(f32[256,16,16]{0,2,1:T(8,128)} %all-to-all-done.2, f32[256,512]{1,0:T(8,128)S(1)} %fusion.16, f32[256,512]{1,0:T(8,128)S(1)} %get-tuple-element.16), kind=kOutput, calls=%fused_computation.2 | convolution fusion | flops 402784256 | bytes 1835008 | tf_op jit(solution)/shard_map/dot_general | solution.py:59
  98.7 3.5 %copy.49 = f32[16,512,16]{2,1,0:T(8,128)} copy(f32[16,512,16]{1,2,0:T(8,128)} %convolution_bitcast_fusion) | data formatting | bytes 1048576 | tf_op jit(solution)/shard_map/transpose | solution.py:72
  102.3 3.9 %reshape.74.grad_ref = f32[16,64,128]{2,1,0:T(8,128)} reshape(f32[16,512,16]{2,1,0:T(8,128)} %copy.49) | data formatting | bytes 1048576 | tf_op jit(solution)/shard_map/reshape | solution.py:73
  106.2 4.1 %shard_map.77 = (f32[16,64,128]{2,1,0:T(8,128)}, f32[16,64,128]{2,1,0:T(8,128)}) custom-call(f32[16,64,128]{2,1,0:T(8,128)} %reshape.72.seg_ref, f32[16,64,128]{2,1,0:T(8,128)} %reshape.73.taps_ref, f32[16,64,128]{2,1,0:T(8,128)} %reshape.74.grad_ref), custom_call_target="tpu_custom_call" | custom-call | flops 8912896 | bytes 2621440 | tf_op jit(solution)/shard_map/pallas_call | solution.py:122
  110.3 3.7 %reshape.75 = f32[16,512,16]{2,1,0:T(8,128)} reshape(f32[16,64,128]{2,1,0:T(8,128)} %get-tuple-element.4) | data formatting | bytes 1048576 | tf_op jit(solution)/shard_map/reshape | solution.py:79
  114.1 0.0 copy-start.1
  114.1 3.6 %copy.50 = f32[512,16,16]{0,2,1:T(8,128)} copy(f32[512,16,16]{2,0,1:T(8,128)} %bitcast.71) | data formatting | bytes 1048576 | tf_op jit(solution)/shard_map/transpose | solution.py:79
  117.7 0.0 copy-done.1
  117.7 2.4 %fusion.5 = f32[256,16,16]{0,2,1:T(8,128)} fusion(f32[512,512]{0,1:T(8,128)S(1)} %copy-done.1, f32[512,16,16]{0,2,1:T(8,128)} %copy.50), kind=kOutput, calls=%fused_computation.20 | convolution fusion | flops 402653184 | bytes 1310720 | tf_op jit(solution)/shard_map/dot_general | solution.py:176
  120.0 7.3 %all-to-all-start.3 = ((f32[256,16,16]{0,2,1:T(8,128)}), f32[256,16,16]{0,2,1:T(8,128)S(1)}, u32[]{:S(2)}, u32[]{:S(2)}) async-start(f32[256,16,16]{0,2,1:T(8,128)} %fusion.5), calls=%async_computation.3 | async-start | bytes 524288 | tf_op jit(solution)/shard_map/all_to_all | solution.py:177
  127.3 1.7 copy.52
  128.9 3.7 %reshape.77 = f32[16,512,16]{2,1,0:T(8,128)} reshape(f32[16,64,128]{2,1,0:T(8,128)} %get-tuple-element.5) | data formatting | bytes 1048576 | tf_op jit(solution)/shard_map/reshape | solution.py:79
  132.7 3.5 %copy.54 = f32[512,16,16]{0,2,1:T(8,128)} copy(f32[512,16,16]{2,0,1:T(8,128)} %bitcast.72) | data formatting | bytes 1048576 | tf_op jit(solution)/shard_map/transpose | solution.py:79
  136.2 0.0 copy-start.4
  136.2 2.4 %fusion.4 = f32[256,16,16]{0,2,1:T(8,128)} fusion(f32[512,512]{0,1:T(8,128)S(1)} %copy-done.1, f32[512,16,16]{0,2,1:T(8,128)} %copy.54), kind=kOutput, calls=%fused_computation.17 | convolution fusion | flops 402653184 | bytes 1310720 | tf_op jit(solution)/shard_map/dot_general | solution.py:184
  138.6 0.3 all-to-all-done.3
  138.9 6.9 %all-to-all-start.5 = ((f32[256,16,16]{0,2,1:T(8,128)}), f32[256,16,16]{0,2,1:T(8,128)S(1)}, u32[]{:S(2)}, u32[]{:S(2)}) async-start(f32[256,16,16]{0,2,1:T(8,128)} %fusion.4), calls=%async_computation.5 | async-start | bytes 524288 | tf_op jit(solution)/shard_map/all_to_all | solution.py:185
  145.8 0.0 copy-done.4
  145.8 1.0 fusion.13
  146.8 0.7 convolution_convert_fusion
  147.6 1.5 copy.66
  149.1 8.3 %all-to-all-done.5 = f32[256,16,16]{0,2,1:T(8,128)S(1)} async-done(((f32[256,16,16]{0,2,1:T(8,128)}), f32[256,16,16]{0,2,1:T(8,128)S(1)}, u32[]{:S(2)}, u32[]{:S(2)}) %all-to-all-start.5) | async-done | bytes 262176 | tf_op jit(solution)/shard_map/all_to_all | solution.py:185
  157.4 4.4 %all-to-all-start.4 = ((bf16[256,16,256]{2,0,1:T(8,128)(2,1)}), bf16[256,16,256]{2,0,1:T(8,128)(2,1)}, u32[]{:S(2)}, u32[]{:S(2)}) async-start(bf16[256,16,256]{2,0,1:T(8,128)(2,1)} %bitcast.73), calls=%async_computation.4 | async-start | bytes 4194304 | tf_op jit(solution)/shard_map/all_to_all | solution.py:182
  161.8 0.8 copy.56
  162.7 33.6 %all-to-all-done.4 = bf16[256,16,256]{2,0,1:T(8,128)(2,1)} async-done(((bf16[256,16,256]{2,0,1:T(8,128)(2,1)}), bf16[256,16,256]{2,0,1:T(8,128)(2,1)}, u32[]{:S(2)}, u32[]{:S(2)}) %all-to-all-start.4) | async-done | bytes 2097184 | tf_op jit(solution)/shard_map/all_to_all | solution.py:182
  196.3 2.6 %reduce_sum.12 = bf16[256,256]{1,0:T(8,128)(2,1)} reduce(bf16[256,16,256]{2,0,1:T(8,128)(2,1)} %all-to-all-done.4, bf16[]{:T(256)} %constant.48.clone.1), dimensions={1}, to_apply=%region_0.1 | reduce | flops 983040 | bytes 2228226 | tf_op jit(solution)/shard_map/reduce_sum | solution.py:190
  (4 shorter events, 0.0 us)
Async XLA Ops:
  0.6 70.0 %copy-start = (bf16[256,4096]{1,0:T(8,128)(2,1)S(1)}, bf16[256,4096]{1,0:T(8,128)(2,1)}, u32[]{:S(2)}) copy-start(bf16[256,4096]{1,0:T(8,128)(2,1)} %param.10) | copy-start | bytes 6291460
  25.8 6.9 %copy-start.3 = (bf16[256,256]{1,0:T(8,128)(2,1)S(1)}, bf16[256,256]{1,0:T(8,128)(2,1)}, u32[]{:S(2)}) copy-start(bf16[256,256]{1,0:T(8,128)(2,1)} %param.7) | copy-start | bytes 393220
  25.8 41.0 %all-to-all-start.1 = ((bf16[256,16,256]{2,0,1:T(8,128)(2,1)}), bf16[256,16,256]{2,0,1:T(8,128)(2,1)}, u32[]{:S(2)}, u32[]{:S(2)}) async-start(bf16[256,16,256]{2,0,1:T(8,128)(2,1)} %tile.2), calls=%async_computation.1 | async-start | bytes 4194304 | tf_op jit(solution)/shard_map/all_to_all | solution.py:148
  73.6 22.7 %all-to-all-start.2 = ((f32[256,16,16]{0,2,1:T(8,128)}), f32[256,16,16]{0,2,1:T(8,128)}, u32[]{:S(2)}, u32[]{:S(2)}) async-start(f32[256,16,16]{0,2,1:T(8,128)} %bitcast.78), calls=%async_computation.2 | async-start | bytes 524288 | tf_op jit(solution)/shard_map/all_to_all | solution.py:159
  83.6 4.0 %copy-start.2 = (bf16[1,256,256]{1,0,2:T(2,128)(2,1)S(1)}, bf16[1,256,256]{1,0,2:T(2,128)(2,1)}, u32[]{:S(2)}) copy-start(bf16[1,256,256]{1,0,2:T(2,128)(2,1)} %get-tuple-element.14) | copy-start | bytes 393220
  114.1 3.6 %copy-start.1 = (f32[512,512]{0,1:T(8,128)S(1)}, f32[512,512]{0,1:T(8,128)}, u32[]{:S(2)}) copy-start(f32[512,512]{0,1:T(8,128)} %maximum_bitcast_fusion) | copy-start | bytes 3145732
  120.0 18.9 %all-to-all-start.3 = ((f32[256,16,16]{0,2,1:T(8,128)}), f32[256,16,16]{0,2,1:T(8,128)S(1)}, u32[]{:S(2)}, u32[]{:S(2)}) async-start(f32[256,16,16]{0,2,1:T(8,128)} %fusion.5), calls=%async_computation.3 | async-start | bytes 524288 | tf_op jit(solution)/shard_map/all_to_all | solution.py:177
  136.2 9.6 %copy-start.4 = (f32[256]{0:T(256)S(1)}, f32[256]{0:T(256)}, u32[]{:S(2)}) copy-start(f32[256]{0:T(256)} %param.9) | copy-start | bytes 3076
  138.9 18.5 %all-to-all-start.5 = ((f32[256,16,16]{0,2,1:T(8,128)}), f32[256,16,16]{0,2,1:T(8,128)S(1)}, u32[]{:S(2)}, u32[]{:S(2)}) async-start(f32[256,16,16]{0,2,1:T(8,128)} %fusion.4), calls=%async_computation.5 | async-start | bytes 524288 | tf_op jit(solution)/shard_map/all_to_all | solution.py:185
  157.4 38.9 %all-to-all-start.4 = ((bf16[256,16,256]{2,0,1:T(8,128)(2,1)}), bf16[256,16,256]{2,0,1:T(8,128)(2,1)}, u32[]{:S(2)}, u32[]{:S(2)}) async-start(bf16[256,16,256]{2,0,1:T(8,128)(2,1)} %bitcast.73), calls=%async_computation.4 | async-start | bytes 4194304 | tf_op jit(solution)/shard_map/all_to_all | solution.py:182

commit v4 on v3

--- a/solution.py
+++ b/solution.py
@@ -67,29 +67,23 @@
     return jnp.concatenate([pad, spec[:, : spec.shape[1] - blocks * width]], axis=1)
 
 
-def to_slabs(spec, blocks, width):
-    bins = spec.shape[0]
-    slab = spec.reshape(bins, blocks, width).transpose(1, 0, 2)
-    return slab.reshape(blocks, bins * width // 128, 128)
-
-
-def from_slabs(slab, width):
-    blocks = slab.shape[0]
-    bins = slab.shape[1] * 128 // width
-    spec = slab.reshape(blocks, bins, width).transpose(1, 0, 2)
-    return spec.reshape(bins, blocks * width)
-
-
-def block_products_kernel(width, seg_ref, taps_ref, grad_ref, conv_ref, lag_ref):
-    blocks, rows, lanes = seg_ref.shape
-    half = rows // 2
-    row_ids = lax.broadcasted_iota(jnp.int32, (half, lanes), 0)
-    lane_ids = lax.broadcasted_iota(jnp.int32, (half, lanes), 1)
-    first_bin = (row_ids == 0) & (lane_ids < width)
-    zero = jnp.zeros((half, lanes), jnp.float32)
+def block_products_kernel(width, low_ref, high_ref, taps_ref, grad_ref, conv_ref, lag_ref, seg_ref):
+    rows, bins = low_ref.shape
+    blocks = rows // width
+    half = bins // 2
+    for p in range(blocks):
+        here = pl.ds(p * width, width)
+        if p == 0:
+            seg_ref[here, :] = high_ref[here, :]
+        else:
+            seg_ref[here, :] = high_ref[here, :] + low_ref[pl.ds((p - 1) * width, width), :]
+    lane_ids = lax.broadcasted_iota(jnp.int32, (width, half), 1)
+    first_bin = lane_ids == 0
+    zero = jnp.zeros((width, half), jnp.float32)
 
     def parts(ref, i):
-        return ref[i, :half, :], ref[i, half:, :]
+        rows_i = pl.ds(i * width, width)
+        return ref[rows_i, :half], ref[rows_i, half:]
 
     for p in range(blocks):
         acc_re, acc_im = zero, zero
@@ -99,8 +93,8 @@
             both_im = a_im * b_im
             acc_re = acc_re + a_re * b_re - jnp.where(first_bin, 0.0, both_im)
             acc_im = acc_im + jnp.where(first_bin, both_im, a_re * b_im + a_im * b_re)
-        conv_ref[p, :half, :] = acc_re
-        conv_ref[p, half:, :] = acc_im
+        conv_ref[pl.ds(p * width, width), :half] = acc_re
+        conv_ref[pl.ds(p * width, width), half:] = acc_im
 
     for k in range(blocks):
         acc_re, acc_im = zero, zero
@@ -110,26 +104,41 @@
             both_im = a_im * b_im
             acc_re = acc_re + a_re * b_re + jnp.where(first_bin, 0.0, both_im)
             acc_im = acc_im + jnp.where(first_bin, both_im, a_im * b_re - a_re * b_im)
-        lag_ref[k, :half, :] = acc_re
-        lag_ref[k, half:, :] = acc_im
-
-
-def block_products(seg_slab, taps_slab, grad_slab, width):
-    blocks, rows, lanes = seg_slab.shape
+        lag_ref[pl.ds(k * width, width), :half] = acc_re
+        lag_ref[pl.ds(k * width, width), half:] = acc_im
+
+
+def block_products(low_spec, high_spec, taps_spec, grad_spec, width):
+    rows, bins = low_spec.shape
+    blocks = rows // width
     pairs = blocks * (blocks + 1)
     vmem = pl.BlockSpec(memory_space=pltpu.VMEM)
-    shape = jax.ShapeDtypeStruct(seg_slab.shape, jnp.float32)
+    shape = jax.ShapeDtypeStruct(low_spec.shape, jnp.float32)
     return pl.pallas_call(
         functools.partial(block_products_kernel, width),
         out_shape=(shape, shape),
-        in_specs=[vmem, vmem, vmem],
+        in_specs=[vmem, vmem, vmem, vmem],
         out_specs=(vmem, vmem),
+        scratch_shapes=[pltpu.VMEM(low_spec.shape, jnp.float32)],
         cost_estimate=pl.CostEstimate(
-            flops=pairs * rows * lanes * 4,
-            bytes_accessed=5 * blocks * rows * lanes * 4,
+            flops=pairs * width * bins * 4,
+            bytes_accessed=6 * rows * bins * 4,
             transcendentals=0,
         ),
-    )(seg_slab, taps_slab, grad_slab)
+    )(low_spec, high_spec, taps_spec, grad_spec)
+
+
+def transform_t(dft_table, block_rows):
+    return lax.dot_general(
+        block_rows.astype(jnp.float32), dft_table, (((0,), (1,)), ((), ())),
+        precision=exact_prec,
+    )
+
+
+def inverse_t(inverse_rows, spec_t):
+    return lax.dot_general(
+        inverse_rows, spec_t, (((1,), (1,)), ((), ())), precision=exact_prec
+    )
 
 
 def body(inputs, gating, filter_taps, skip_gain, w_out, cotangent):
@@ -158,22 +167,15 @@
     grad_mixed = upstream * gate_wide
     grad_t = lax.all_to_all(grad_mixed, "ctx", 1, 1, tiled=True)
 
-    low_spec = transform(first_half, signal_t)
-    high_spec = transform(second_half, signal_t)
-    seg_spec = high_spec + shift_blocks(low_spec, 1, width)
-    taps_spec = transform(first_half, taps_t)
-    grad_spec = transform(second_half, grad_t)
-
-    conv_slab, lag_slab = block_products(
-        to_slabs(seg_spec, ctx_count, width),
-        to_slabs(taps_spec, ctx_count, width),
-        to_slabs(grad_spec, ctx_count, width),
+    conv_spec, lag_spec = block_products(
+        transform_t(first_half, signal_t),
+        transform_t(second_half, signal_t),
+        transform_t(first_half, taps_t),
+        transform_t(second_half, grad_t),
         width,
     )
-    running = from_slabs(conv_slab, width)
-    lag_spec = from_slabs(lag_slab, width)
-
-    convolved_t = jnp.dot(inverse[block_len:], running, precision=exact_prec)
+
+    convolved_t = inverse_t(inverse[block_len:], conv_spec)
     convolved = lax.all_to_all(convolved_t, "ctx", 1, 1, tiled=True)
 
     mixed_sum = convolved + skip_gain[None, :] * inputs.astype(jnp.float32)
@@ -181,7 +183,7 @@
     partial_out = jnp.dot(gated_rows, w_out, preferred_element_type=jnp.float32)
     pieces = lax.all_to_all(partial_out.astype(jnp.bfloat16), "ch", 1, 0, tiled=True)
 
-    filter_grad_t = jnp.dot(inverse[:block_len], lag_spec, precision=exact_prec)
+    filter_grad_t = inverse_t(inverse[:block_len], lag_spec)
     filter_grad = lax.all_to_all(filter_grad_t, "ctx", 1, 1, tiled=True)
 
     output = (

time: 200 us -> 171 us (0.85)
  local copies, waits for them, and re-layouts: 49.9 us -> 14 us
  waiting for transfers between devices: 66.9 us -> 80.7 us
  starting transfers between devices: 30.3 us -> 22.9 us
    reshape x6 -> x0, local copies, waits for them, and re-layouts: 22.8 us -> none  [the longest x3 11.8 us: to_slabs(): return slab.reshape(blocks, bins * width // 128, 128)]
    transpose x4 -> x0, local copies, waits for them, and re-layouts: 14.1 us -> none  [the longest x2 7.1 us: from_slabs(): spec = slab.reshape(blocks, bins, width).transpose(1, 0, 2)]
    all_to_all x1, waiting for transfers between devices: 0.01 us -> 7.01 us  [body(): grad_t = lax.all_to_all(grad_mixed, 'ctx', 1, 1, tiled=True)]
    all_to_all x1, waiting for transfers between devices: 0.31 us -> 6.86 us  [body(): convolved = lax.all_to_all(convolved_t, 'ctx', 1, 1, tiled=True)]
    all_to_all x1, starting transfers between devices: 7.26 us -> 3.43 us  [body(): convolved = lax.all_to_all(convolved_t, 'ctx', 1, 1, tiled=True)]
    all_to_all x1, starting transfers between devices: 6.92 us -> 3.43 us  [body(): filter_grad = lax.all_to_all(filter_grad_t, 'ctx', 1, 1, tiled=True)]
    select_n x1 -> x0, other arithmetic: 2.05 us -> none  [spectral_tables(): jnp.where(is_first, parity, -jnp.sin(angles))]
    mul x0 -> x1, other arithmetic: none -> 2.05 us  [spectral_tables(): imag_rows = jnp.where(is_first, parity, -2.0 * jnp.sin(angles)) * norm_scale]
  transfers between devices with their start and end apart: 5 -> 5, of which waited for: 4 -> 5; matrix products, arithmetic and copies ran while one was open for 21% -> 13% of each run, Pallas kernels for 0% -> 0%
where the time goes in v4:
time: 171 us; the launch traced here: 170 us
  waiting for transfers between devices  80.7 us (47%)
  starting transfers between devices  22.9 us (13%)
  blocking collectives  21.4 us (13%)
  matrix products  14.7 us (9%)
  local copies, waits for them, and re-layouts  14 us (8%)
  other arithmetic  11.7 us (7%)
  Pallas kernels  4.03 us (2%)
    all_to_all x1, waiting for transfers between devices, body(): lax.all_to_all(partial_out.astype(jnp.bfloat16), 'ch', 1, 0, tiled=True)  33.8 us
    all_to_all x1, waiting for transfers between devices, body(): lax.all_to_all(jnp.tile(cotangent, (1, ch_count)), 'ch', 1, 1, tiled=True)  24.7 us
    all_to_all x1, blocking collectives, body(): pair_t = lax.all_to_all(pair, 'ctx', 2, 2, tiled=True)  21.4 us
    all_to_all x1, waiting for transfers between devices, body(): filter_grad = lax.all_to_all(filter_grad_t, 'ctx', 1, 1, tiled=True)  8.36 us
    all_to_all x1, waiting for transfers between devices, body(): grad_t = lax.all_to_all(grad_mixed, 'ctx', 1, 1, tiled=True)  7.01 us
    all_to_all x1, starting transfers between devices, body(): lax.all_to_all(jnp.tile(cotangent, (1, ch_count)), 'ch', 1, 1, tiled=True)  6.94 us
    all_to_all x1, waiting for transfers between devices, body(): convolved = lax.all_to_all(convolved_t, 'ctx', 1, 1, tiled=True)  6.86 us
    dot_general x4, matrix products, transform_t(): lax.dot_general(block_rows.astype(jnp.float32), dft_table, (((0,), (1,)),...  6.19 us
  transfers between devices with their start and end apart: 5, of which 5 were waited for; matrix products, arithmetic and copies ran while one was open for 13% of the time, Pallas kernels for 0%

profile of v4, /device:TPU:1, one launch (start us, length us, event | category | flops | bytes accessed | tf_op | source)
XLA Modules:
  0.0 170.2 jit_solution(9469203627827702325)
XLA Ops:
  0.6 0.0 copy-start
  0.6 1.1 pad_maximum_fusion.1
  1.8 0.2 copy.21
  2.0 21.4 %all_to_all.63 = bf16[2,256,256]{1,0,2:T(2,128)(2,1)S(1)} all-to-all(bf16[2,256,256]{1,0,2:T(2,128)(2,1)S(1)} %copy.21), channel_id=1, replica_groups=mesh['ctx'=16,'ch'=16] {'ctx'}, dimensions={2} | all-to-all | bytes 524288 | tf_op jit(solution)/shard_map/all_to_all | solution.py:153
  23.3 2.4 %tile.2 = bf16[256,16,256]{2,0,1:T(8,128)(2,1)} broadcast(bf16[256,256]{1,0:T(8,128)(2,1)} %param.11), dimensions={0,2} | broadcast | bytes 2228224 | tf_op jit(solution)/shard_map/tile | solution.py:158
  25.8 0.0 copy-start.2
  25.8 6.9 %all-to-all-start.1 = ((bf16[256,16,256]{2,0,1:T(8,128)(2,1)}), bf16[256,16,256]{2,0,1:T(8,128)(2,1)}, u32[]{:S(2)}, u32[]{:S(2)}) async-start(bf16[256,16,256]{2,0,1:T(8,128)(2,1)} %tile.2), calls=%async_computation.1 | async-start | bytes 4194304 | tf_op jit(solution)/shard_map/all_to_all | solution.py:157
  32.7 0.0 copy-done.2
  32.7 0.1 copy.20
  32.9 1.9 %fusion.13 = f32[256,512]{1,0:T(8,128)S(1)} fusion(), kind=kLoop, calls=%fused_computation.29 | loop fusion | flops 1835008 | bytes 524288 | tf_op jit(solution)/shard_map/cos | solution.py:25
  34.8 2.0 %multiply_multiply_fusion = f32[256,512]{1,0:T(8,128)S(1)} fusion(f32[256]{0:T(256)S(1)} %broadcast_select_fusion), kind=kLoop, calls=%fused_computation.20 | loop fusion | flops 2097152 | bytes 525312 | tf_op jit(solution)/shard_map/mul | solution.py:25
  36.7 2.0 %select_multiply_fusion = (f32[256,512]{1,0:T(8,128)S(1)}, f32[256,512]{1,0:T(8,128)S(1)}) fusion(f32[512]{0:T(512)S(1)} %fusion.26, pred[256]{0:T(512)(128)(4,1)S(1)} %iota_compare_fusion), kind=kLoop, calls=%fused_computation.19 | loop fusion | flops 2490368 | bytes 1050880 | tf_op jit(solution)/shard_map/mul | solution.py:26
  38.8 1.0 maximum_bitcast_fusion
  39.8 1.2 fusion.32
  41.0 1.1 copy.28
  42.1 24.7 %all-to-all-done.1 = bf16[256,16,256]{2,0,1:T(8,128)(2,1)} async-done(((bf16[256,16,256]{2,0,1:T(8,128)(2,1)}), bf16[256,16,256]{2,0,1:T(8,128)(2,1)}, u32[]{:S(2)}, u32[]{:S(2)}) %all-to-all-start.1) | async-done | bytes 2097184 | tf_op jit(solution)/shard_map/all_to_all | solution.py:157
  66.7 3.9 %copy.24 = bf16[256,16,256]{0,2,1:T(8,128)(2,1)} copy(bf16[256,16,256]{2,0,1:T(8,128)(2,1)} %all-to-all-done.1) | data formatting | bytes 4194304 | tf_op jit(solution)/shard_map/all_to_all | solution.py:157
  70.6 0.0 copy-done
  70.6 3.0 %convolution_multiply_fusion = f32[256,256]{0,1:T(8,128)} fusion(bf16[256,4096]{1,0:T(8,128)(2,1)S(1)} %copy-done, bf16[256,4096]{0,1:T(8,128)(2,1)} %bitcast.34, bf16[256,256]{0,1:T(8,128)(2,1)S(1)} %copy.20), kind=kOutput, calls=%fused_computation.2 | convolution fusion | flops 537001984 | bytes 4587520 | tf_op jit(solution)/shard_map/dot_general | solution.py:160
  73.7 4.7 %all-to-all-start.2 = ((f32[256,16,16]{0,2,1:T(8,128)}), f32[256,16,16]{0,2,1:T(8,128)}, u32[]{:S(2)}, u32[]{:S(2)}) async-start(f32[256,16,16]{0,2,1:T(8,128)} %bitcast.37), calls=%async_computation.2 | async-start | bytes 524288 | tf_op jit(solution)/shard_map/all_to_all | solution.py:168
  78.4 1.3 fusion.14.high_ref
  79.6 1.1 copy.29
  80.7 1.3 fusion.19.low_ref
  82.0 1.3 fusion.16.taps_ref
  83.3 7.0 %all-to-all-done.2 = f32[256,16,16]{0,2,1:T(8,128)} async-done(((f32[256,16,16]{0,2,1:T(8,128)}), f32[256,16,16]{0,2,1:T(8,128)}, u32[]{:S(2)}, u32[]{:S(2)}) %all-to-all-start.2) | async-done | bytes 262176 | tf_op jit(solution)/shard_map/all_to_all | solution.py:168
  90.3 2.4 %fusion.15.grad_ref = f32[256,512]{1,0:T(8,128)} fusion(f32[256,256]{0,1:T(8,128)} %bitcast.7, f32[256,512]{1,0:T(8,128)S(1)} %get-tuple-element.15, f32[256,512]{1,0:T(8,128)S(1)} %fusion.13), kind=kOutput, calls=%fused_computation.31 | convolution fusion | flops 402784256 | bytes 1835008 | tf_op jit(solution)/shard_map/dot_general | solution.py:132
  92.6 0.0 copy-start.1
  92.7 4.0 %shard_map.77 = (f32[256,512]{1,0:T(8,128)}, f32[256,512]{1,0:T(8,128)}) custom-call(f32[256,512]{1,0:T(8,128)} %fusion.19.low_ref, f32[256,512]{1,0:T(8,128)} %fusion.14.high_ref, f32[256,512]{1,0:T(8,128)} %fusion.16.taps_ref, f32[256,512]{1,0:T(8,128)} %fusion.15.grad_ref), custom_call_target="tpu_custom_call" | custom-call | flops 8912896 | bytes 3145728 | tf_op jit(solution)/shard_map/pallas_call | solution.py:117
  96.7 0.0 copy-start.3
  96.7 0.0 copy-done.1
  96.7 2.4 %fusion.6 = f32[256,256]{0,1:T(8,128)} fusion(f32[256,512]{1,0:T(8,128)} %get-tuple-element.4, f32[512,512]{0,1:T(8,128)S(1)} %copy-done.1), kind=kOutput, calls=%fused_computation.16 | convolution fusion | flops 402653184 | bytes 1310720 | tf_op jit(solution)/shard_map/dot_general | solution.py:139
  99.1 3.4 %all-to-all-start.3 = ((f32[256,16,16]{0,2,1:T(8,128)}), f32[256,16,16]{0,2,1:T(8,128)S(1)}, u32[]{:S(2)}, u32[]{:S(2)}) async-start(f32[256,16,16]{0,2,1:T(8,128)} %bitcast.38), calls=%async_computation.3 | async-start | bytes 524288 | tf_op jit(solution)/shard_map/all_to_all | solution.py:179
  102.5 1.7 copy.25
  104.2 2.4 %fusion.4 = f32[256,256]{0,1:T(8,128)} fusion(f32[256,512]{1,0:T(8,128)} %get-tuple-element.5, f32[512,512]{0,1:T(8,128)S(1)} %copy-done.1), kind=kOutput, calls=%fused_computation.13 | convolution fusion | flops 402653184 | bytes 1310720 | tf_op jit(solution)/shard_map/dot_general | solution.py:139
  106.5 6.9 %all-to-all-done.3 = f32[256,16,16]{0,2,1:T(8,128)S(1)} async-done(((f32[256,16,16]{0,2,1:T(8,128)}), f32[256,16,16]{0,2,1:T(8,128)S(1)}, u32[]{:S(2)}, u32[]{:S(2)}) %all-to-all-start.3) | async-done | bytes 262176 | tf_op jit(solution)/shard_map/all_to_all | solution.py:179
  113.4 3.4 %all-to-all-start.5 = ((f32[256,16,16]{0,2,1:T(8,128)}), f32[256,16,16]{0,2,1:T(8,128)S(1)}, u32[]{:S(2)}, u32[]{:S(2)}) async-start(f32[256,16,16]{0,2,1:T(8,128)} %bitcast.36), calls=%async_computation.5 | async-start | bytes 524288 | tf_op jit(solution)/shard_map/all_to_all | solution.py:187
  116.8 0.0 copy-done.3
  116.8 1.0 fusion.11
  117.9 0.7 convolution_convert_fusion
  118.6 1.6 copy.32
  120.2 8.4 %all-to-all-done.5 = f32[256,16,16]{0,2,1:T(8,128)S(1)} async-done(((f32[256,16,16]{0,2,1:T(8,128)}), f32[256,16,16]{0,2,1:T(8,128)S(1)}, u32[]{:S(2)}, u32[]{:S(2)}) %all-to-all-start.5) | async-done | bytes 262176 | tf_op jit(solution)/shard_map/all_to_all | solution.py:187
  128.5 4.4 %all-to-all-start.4 = ((bf16[256,16,256]{2,0,1:T(8,128)(2,1)}), bf16[256,16,256]{2,0,1:T(8,128)(2,1)}, u32[]{:S(2)}, u32[]{:S(2)}) async-start(bf16[256,16,256]{2,0,1:T(8,128)(2,1)} %bitcast.33), calls=%async_computation.4 | async-start | bytes 4194304 | tf_op jit(solution)/shard_map/all_to_all | solution.py:184
  133.0 0.8 copy.27
  133.8 33.8 %all-to-all-done.4 = bf16[256,16,256]{2,0,1:T(8,128)(2,1)} async-done(((bf16[256,16,256]{2,0,1:T(8,128)(2,1)}), bf16[256,16,256]{2,0,1:T(8,128)(2,1)}, u32[]{:S(2)}, u32[]{:S(2)}) %all-to-all-start.4) | async-done | bytes 2097184 | tf_op jit(solution)/shard_map/all_to_all | solution.py:184
  167.6 2.6 %reduce_sum.12 = bf16[256,256]{1,0:T(8,128)(2,1)} reduce(bf16[256,16,256]{2,0,1:T(8,128)(2,1)} %all-to-all-done.4, bf16[]{:T(256)} %constant.46.clone.1), dimensions={1}, to_apply=%region_0.1 | reduce | flops 983040 | bytes 2228226 | tf_op jit(solution)/shard_map/reduce_sum | solution.py:192
  (3 shorter events, 0.0 us)
Async XLA Ops:
  0.6 70.0 %copy-start = (bf16[256,4096]{1,0:T(8,128)(2,1)S(1)}, bf16[256,4096]{1,0:T(8,128)(2,1)}, u32[]{:S(2)}) copy-start(bf16[256,4096]{1,0:T(8,128)(2,1)} %param.10) | copy-start | bytes 6291460
  25.8 6.9 %copy-start.2 = (bf16[256,256]{1,0:T(8,128)(2,1)S(1)}, bf16[256,256]{1,0:T(8,128)(2,1)}, u32[]{:S(2)}) copy-start(bf16[256,256]{1,0:T(8,128)(2,1)} %param.7) | copy-start | bytes 393220
  25.8 41.0 %all-to-all-start.1 = ((bf16[256,16,256]{2,0,1:T(8,128)(2,1)}), bf16[256,16,256]{2,0,1:T(8,128)(2,1)}, u32[]{:S(2)}, u32[]{:S(2)}) async-start(bf16[256,16,256]{2,0,1:T(8,128)(2,1)} %tile.2), calls=%async_computation.1 | async-start | bytes 4194304 | tf_op jit(solution)/shard_map/all_to_all | solution.py:157
  73.7 16.6 %all-to-all-start.2 = ((f32[256,16,16]{0,2,1:T(8,128)}), f32[256,16,16]{0,2,1:T(8,128)}, u32[]{:S(2)}, u32[]{:S(2)}) async-start(f32[256,16,16]{0,2,1:T(8,128)} %bitcast.37), calls=%async_computation.2 | async-start | bytes 524288 | tf_op jit(solution)/shard_map/all_to_all | solution.py:168
  92.6 4.0 %copy-start.1 = (f32[512,512]{0,1:T(8,128)S(1)}, f32[512,512]{0,1:T(8,128)}, u32[]{:S(2)}) copy-start(f32[512,512]{0,1:T(8,128)} %maximum_bitcast_fusion) | copy-start | bytes 3145732
  96.7 20.2 %copy-start.3 = (f32[256]{0:T(256)S(1)}, f32[256]{0:T(256)}, u32[]{:S(2)}) copy-start(f32[256]{0:T(256)} %param.9) | copy-start | bytes 3076
  99.1 14.3 %all-to-all-start.3 = ((f32[256,16,16]{0,2,1:T(8,128)}), f32[256,16,16]{0,2,1:T(8,128)S(1)}, u32[]{:S(2)}, u32[]{:S(2)}) async-start(f32[256,16,16]{0,2,1:T(8,128)} %bitcast.38), calls=%async_computation.3 | async-start | bytes 524288 | tf_op jit(solution)/shard_map/all_to_all | solution.py:179
  113.4 15.1 %all-to-all-start.5 = ((f32[256,16,16]{0,2,1:T(8,128)}), f32[256,16,16]{0,2,1:T(8,128)S(1)}, u32[]{:S(2)}, u32[]{:S(2)}) async-start(f32[256,16,16]{0,2,1:T(8,128)} %bitcast.36), calls=%async_computation.5 | async-start | bytes 524288 | tf_op jit(solution)/shard_map/all_to_all | solution.py:187
  128.5 39.1 %all-to-all-start.4 = ((bf16[256,16,256]{2,0,1:T(8,128)(2,1)}), bf16[256,16,256]{2,0,1:T(8,128)(2,1)}, u32[]{:S(2)}, u32[]{:S(2)}) async-start(bf16[256,16,256]{2,0,1:T(8,128)(2,1)} %bitcast.33), calls=%async_computation.4 | async-start | bytes 4194304 | tf_op jit(solution)/shard_map/all_to_all | solution.py:184

commit v5 on v4

--- a/solution.py
+++ b/solution.py
@@ -67,7 +67,7 @@
     return jnp.concatenate([pad, spec[:, : spec.shape[1] - blocks * width]], axis=1)
 
 
-def block_products_kernel(width, low_ref, high_ref, taps_ref, grad_ref, conv_ref, lag_ref, seg_ref):
+def conv_products_kernel(width, low_ref, high_ref, taps_ref, conv_ref, seg_ref):
     rows, bins = low_ref.shape
     blocks = rows // width
     half = bins // 2
@@ -80,27 +80,30 @@
     lane_ids = lax.broadcasted_iota(jnp.int32, (width, half), 1)
     first_bin = lane_ids == 0
     zero = jnp.zeros((width, half), jnp.float32)
-
-    def parts(ref, i):
-        rows_i = pl.ds(i * width, width)
-        return ref[rows_i, :half], ref[rows_i, half:]
-
     for p in range(blocks):
         acc_re, acc_im = zero, zero
         for k in range(p + 1):
-            a_re, a_im = parts(taps_ref, k)
-            b_re, b_im = parts(seg_ref, p - k)
+            a_re, a_im = block_parts(taps_ref, k, width)
+            b_re, b_im = block_parts(seg_ref, p - k, width)
             both_im = a_im * b_im
             acc_re = acc_re + a_re * b_re - jnp.where(first_bin, 0.0, both_im)
             acc_im = acc_im + jnp.where(first_bin, both_im, a_re * b_im + a_im * b_re)
         conv_ref[pl.ds(p * width, width), :half] = acc_re
         conv_ref[pl.ds(p * width, width), half:] = acc_im
 
+
+def lag_products_kernel(width, seg_ref, grad_ref, lag_ref):
+    rows, bins = seg_ref.shape
+    blocks = rows // width
+    half = bins // 2
+    lane_ids = lax.broadcasted_iota(jnp.int32, (width, half), 1)
+    first_bin = lane_ids == 0
+    zero = jnp.zeros((width, half), jnp.float32)
     for k in range(blocks):
         acc_re, acc_im = zero, zero
         for p in range(k, blocks):
-            a_re, a_im = parts(grad_ref, p)
-            b_re, b_im = parts(seg_ref, p - k)
+            a_re, a_im = block_parts(grad_ref, p, width)
+            b_re, b_im = block_parts(seg_ref, p - k, width)
             both_im = a_im * b_im
             acc_re = acc_re + a_re * b_re + jnp.where(first_bin, 0.0, both_im)
             acc_im = acc_im + jnp.where(first_bin, both_im, a_im * b_re - a_re * b_im)
@@ -108,24 +111,45 @@
         lag_ref[pl.ds(k * width, width), half:] = acc_im
 
 
-def block_products(low_spec, high_spec, taps_spec, grad_spec, width):
+def block_parts(ref, i, width):
+    half = ref.shape[1] // 2
+    rows_i = pl.ds(i * width, width)
+    return ref[rows_i, :half], ref[rows_i, half:]
+
+
+def conv_products(low_spec, high_spec, taps_spec, width):
     rows, bins = low_spec.shape
     blocks = rows // width
-    pairs = blocks * (blocks + 1)
     vmem = pl.BlockSpec(memory_space=pltpu.VMEM)
     shape = jax.ShapeDtypeStruct(low_spec.shape, jnp.float32)
     return pl.pallas_call(
-        functools.partial(block_products_kernel, width),
+        functools.partial(conv_products_kernel, width),
         out_shape=(shape, shape),
-        in_specs=[vmem, vmem, vmem, vmem],
+        in_specs=[vmem, vmem, vmem],
         out_specs=(vmem, vmem),
-        scratch_shapes=[pltpu.VMEM(low_spec.shape, jnp.float32)],
         cost_estimate=pl.CostEstimate(
-            flops=pairs * width * bins * 4,
-            bytes_accessed=6 * rows * bins * 4,
+            flops=blocks * (blocks + 1) // 2 * width * bins * 4,
+            bytes_accessed=5 * rows * bins * 4,
             transcendentals=0,
         ),
-    )(low_spec, high_spec, taps_spec, grad_spec)
+    )(low_spec, high_spec, taps_spec)
+
+
+def lag_products(seg_spec, grad_spec, width):
+    rows, bins = seg_spec.shape
+    blocks = rows // width
+    vmem = pl.BlockSpec(memory_space=pltpu.VMEM)
+    return pl.pallas_call(
+        functools.partial(lag_products_kernel, width),
+        out_shape=jax.ShapeDtypeStruct(seg_spec.shape, jnp.float32),
+        in_specs=[vmem, vmem],
+        out_specs=vmem,
+        cost_estimate=pl.CostEstimate(
+            flops=blocks * (blocks + 1) // 2 * width * bins * 4,
+            bytes_accessed=3 * rows * bins * 4,
+            transcendentals=0,
+        ),
+    )(seg_spec, grad_spec)
 
 
 def transform_t(dft_table, block_rows):
@@ -154,9 +178,7 @@
     signal_t, taps_t = pair_t[0], pair_t[1]
 
     ch_count = lax.axis_size("ch")
-    cot_rows = lax.all_to_all(
-        jnp.tile(cotangent, (1, ch_count)), "ch", 1, 1, tiled=True
-    )
+    cot_rows = lax.all_gather(cotangent, "ch", axis=1, tiled=True)
     upstream = lax.dot_general(
         cot_rows,
         w_out,
@@ -167,11 +189,10 @@
     grad_mixed = upstream * gate_wide
     grad_t = lax.all_to_all(grad_mixed, "ctx", 1, 1, tiled=True)
 
-    conv_spec, lag_spec = block_products(
+    conv_spec, seg_spec = conv_products(
         transform_t(first_half, signal_t),
         transform_t(second_half, signal_t),
         transform_t(first_half, taps_t),
-        transform_t(second_half, grad_t),
         width,
     )
 
@@ -183,6 +204,7 @@
     partial_out = jnp.dot(gated_rows, w_out, preferred_element_type=jnp.float32)
     pieces = lax.all_to_all(partial_out.astype(jnp.bfloat16), "ch", 1, 0, tiled=True)
 
+    lag_spec = lag_products(seg_spec, transform_t(second_half, grad_t), width)
     filter_grad_t = inverse_t(inverse[:block_len], lag_spec)
     filter_grad = lax.all_to_all(filter_grad_t, "ctx", 1, 1, tiled=True)
 

time: 171 us -> 152 us (0.89)
  blocking collectives: 21.4 us -> 0 us
  waiting for transfers between devices: 80.7 us -> 65.3 us
  between operations: 0.77 us -> 14.1 us
  starting transfers between devices: 22.9 us -> 31.6 us
  local copies, waits for them, and re-layouts: 14 us -> 9.04 us
  Pallas kernels: 4.03 us -> 5.86 us
    all_to_all x1 -> x0, blocking collectives: 21.4 us -> none  [body(): pair_t = lax.all_to_all(pair, 'ctx', 2, 2, tiled=True)]
    all_to_all x1, waiting for transfers between devices: 24.7 us -> 4.58 us  [body(): pair_t = lax.all_to_all(pair, 'ctx', 2, 2, tiled=True)]
    all_gather x0 -> x1, waiting for transfers between devices: none -> 15.5 us  [body(): cot_rows = lax.all_gather(cotangent, 'ch', axis=1, tiled=True)]
    all_to_all x1, waiting for transfers between devices: 6.86 us -> 0.01 us  [body(): convolved = lax.all_to_all(convolved_t, 'ctx', 1, 1, tiled=True)]
    all_to_all x1, waiting for transfers between devices: 33.8 us -> 27.1 us  [body(): lax.all_to_all(partial_out.astype(jnp.bfloat16), 'ch', 1, 0, tiled=True)]
    all_to_all x1, starting transfers between devices: 4.72 us -> 9.3 us  [body(): grad_t = lax.all_to_all(grad_mixed, 'ctx', 1, 1, tiled=True)]
    all_to_all x1 -> x0, local copies, waits for them, and re-layouts: 3.9 us -> none  [body(): lax.all_to_all(jnp.tile(cotangent, (1, ch_count)), 'ch', 1, 1, tiled=True)]
    all_to_all x1, starting transfers between devices: 6.94 us -> 9.97 us  [body(): pair_t = lax.all_to_all(pair, 'ctx', 2, 2, tiled=True)]
  transfers between devices with their start and end apart: 5 -> 6, of which waited for: 5 -> 5; matrix products, arithmetic and copies ran while one was open for 13% -> 22% of each run, Pallas kernels for 0% -> 4%
where the time goes in v5:
time: 152 us
  waiting for transfers between devices  65.3 us (43%)
  starting transfers between devices  31.6 us (21%)
  matrix products  14.1 us (9%)
  between operations  14.1 us (9%)
  other arithmetic  11.6 us (8%)
  local copies, waits for them, and re-layouts  9.04 us (6%)
  Pallas kernels  5.86 us (4%)
    all_to_all x1, waiting for transfers between devices, body(): lax.all_to_all(partial_out.astype(jnp.bfloat16), 'ch', 1, 0, tiled=True)  27.1 us
    all_gather x1, waiting for transfers between devices, body(): cot_rows = lax.all_gather(cotangent, 'ch', axis=1, tiled=True)  15.5 us
    all_to_all x1, starting transfers between devices, body(): pair_t = lax.all_to_all(pair, 'ctx', 2, 2, tiled=True)  9.97 us
    all_to_all x1, starting transfers between devices, body(): grad_t = lax.all_to_all(grad_mixed, 'ctx', 1, 1, tiled=True)  9.3 us
    all_to_all x1, waiting for transfers between devices, body(): filter_grad = lax.all_to_all(filter_grad_t, 'ctx', 1, 1, tiled=True)  9.18 us
    all_to_all x1, waiting for transfers between devices, body(): grad_t = lax.all_to_all(grad_mixed, 'ctx', 1, 1, tiled=True)  8.18 us
    unnamed x13, local copies, waits for them, and re-layouts  5.47 us
    dot_general x4, matrix products, transform_t(): lax.dot_general(block_rows.astype(jnp.float32), dft_table, (((0,), (1,)),...  5.23 us
  transfers between devices with their start and end apart: 6, of which 5 were waited for; matrix products, arithmetic and copies ran while one was open for 22% of the time, Pallas kernels for 4%

profile of v5, /device:TPU:1, one launch (start us, length us, event | category | flops | bytes accessed | tf_op | source)
XLA Modules:
  0.0 151.6 jit_solution(17987181292255561316)
XLA Ops:
  7.2 0.0 copy-start
  7.2 0.0 all-gather.2.cloned.1.call-start
  7.2 0.7 all-gather.2.cloned.1.call-update
  7.9 1.0 pad_maximum_fusion.1
  8.9 0.9 copy.21
  9.8 10.0 %all-to-all-start = ((bf16[2,256,256]{1,0,2:T(2,128)(2,1)}), bf16[2,256,256]{1,0,2:T(2,128)(2,1)S(1)}, u32[]{:S(2)}, u32[]{:S(2)}) async-start(bf16[2,256,256]{1,0,2:T(2,128)(2,1)} %copy.21), calls=%async_computation | async-start | bytes 524288 | tf_op jit(solution)/shard_map/all_to_all | solution.py:177
  19.8 1.9 %fusion.13 = f32[256,512]{1,0:T(8,128)S(1)} fusion(), kind=kLoop, calls=%fused_computation.29 | loop fusion | flops 1835008 | bytes 524288 | tf_op jit(solution)/shard_map/cos | solution.py:25
  21.7 2.0 %multiply_multiply_fusion = f32[256,512]{1,0:T(8,128)S(1)} fusion(f32[256]{0:T(256)S(1)} %broadcast_select_fusion), kind=kLoop, calls=%fused_computation.20 | loop fusion | flops 2097152 | bytes 525312 | tf_op jit(solution)/shard_map/mul | solution.py:25
  23.7 2.0 %select_multiply_fusion = (f32[256,512]{1,0:T(8,128)S(1)}, f32[256,512]{1,0:T(8,128)S(1)}) fusion(f32[512]{0:T(512)S(1)} %fusion.26, pred[256]{0:T(512)(128)(4,1)S(1)} %iota_compare_fusion), kind=kLoop, calls=%fused_computation.19 | loop fusion | flops 2490368 | bytes 1050880 | tf_op jit(solution)/shard_map/mul | solution.py:26
  25.7 1.1 maximum_bitcast_fusion
  26.8 4.6 %all-to-all-done = bf16[2,256,256]{1,0,2:T(2,128)(2,1)S(1)} async-done(((bf16[2,256,256]{1,0,2:T(2,128)(2,1)}), bf16[2,256,256]{1,0,2:T(2,128)(2,1)S(1)}, u32[]{:S(2)}, u32[]{:S(2)}) %all-to-all-start) | async-done | bytes 262176 | tf_op jit(solution)/shard_map/all_to_all | solution.py:177
  31.3 1.2 fusion.32
  32.5 1.1 copy.28
  33.6 1.1 copy.27
  34.6 1.3 fusion.14.high_ref
  35.9 1.3 fusion.19.low_ref
  37.2 1.3 fusion.16.taps_ref
  38.4 0.0 copy-start.2
  38.4 2.9 %shard_map.77 = (f32[256,512]{1,0:T(8,128)}, f32[256,512]{1,0:T(8,128)}) custom-call(f32[256,512]{1,0:T(8,128)} %fusion.19.low_ref, f32[256,512]{1,0:T(8,128)} %fusion.14.high_ref, f32[256,512]{1,0:T(8,128)} %fusion.16.taps_ref), custom_call_target="tpu_custom_call" | custom-call | flops 4456448 | bytes 2621440 | tf_op jit(solution)/shard_map/pallas_call | solution.py:125
  41.3 2.5 %fusion.6 = f32[256,256]{0,1:T(8,128)} fusion(f32[256,512]{1,0:T(8,128)} %get-tuple-element.4, f32[512,512]{0,1:T(8,128)} %maximum_bitcast_fusion), kind=kOutput, calls=%fused_computation.16 | convolution fusion | flops 402653184 | bytes 1310720 | tf_op jit(solution)/shard_map/dot_general | solution.py:163
  43.9 3.4 %all-to-all-start.1 = ((f32[256,16,16]{0,2,1:T(8,128)}), f32[256,16,16]{0,2,1:T(8,128)S(1)}, u32[]{:S(2)}, u32[]{:S(2)}) async-start(f32[256,16,16]{0,2,1:T(8,128)} %bitcast.36), calls=%async_computation.1 | async-start | bytes 524288 | tf_op jit(solution)/shard_map/all_to_all | solution.py:200
  47.3 0.0 copy-done.2
  47.3 0.8 copy.24
  48.1 1.0 copy.20
  49.1 0.0 copy-start.3
  49.1 15.5 %all-gather.2.cloned.1.call-done = bf16[256,4096]{1,0:T(8,128)(2,1)} async-done(((bf16[256,256]{1,0:T(8,128)(2,1)}), bf16[256,4096]{1,0:T(8,128)(2,1)}) %all-gather.2.cloned.1.call-update) | async-done | bytes 2097168 | tf_op jit(solution)/shard_map/all_gather | solution.py:181
  64.6 0.0 copy-done
  64.6 3.0 %convolution_multiply_fusion = f32[256,256]{0,1:T(8,128)} fusion(bf16[256,4096]{1,0:T(8,128)(2,1)} %all-gather.2.cloned.1.call-done, bf16[256,4096]{1,0:T(8,128)(2,1)S(1)} %copy-done, bf16[256,256]{0,1:T(8,128)(2,1)S(1)} %copy.20), kind=kOutput, calls=%fused_computation.2 | convolution fusion | flops 537001984 | bytes 4587520 | tf_op jit(solution)/shard_map/dot_general | solution.py:182
  67.7 0.0 all-to-all-done.1
  67.7 0.0 copy-start.1
  67.7 0.7 copy-done.1
  68.4 9.3 %all-to-all-start.3 = ((f32[256,16,16]{0,2,1:T(8,128)}), f32[256,16,16]{0,2,1:T(8,128)S(1)}, u32[]{:S(2)}, u32[]{:S(2)}) async-start(f32[256,16,16]{0,2,1:T(8,128)} %bitcast.35), calls=%async_computation.3 | async-start | bytes 524288 | tf_op jit(solution)/shard_map/all_to_all | solution.py:190
  77.7 0.0 copy-done.3
  77.7 1.1 fusion.11
  78.8 0.7 convolution_convert_fusion
  79.5 1.6 %copy.31 = bf16[32,16,8,256]{3,2,0,1:T(8,128)(2,1)} copy(bf16[32,16,8,256]{3,2,1,0:T(8,128)(2,1)S(1)} %bitcast.33) | data formatting | bytes 4194304 | tf_op jit(solution)/shard_map/all_to_all | solution.py:205
  81.1 8.2 %all-to-all-done.3 = f32[256,16,16]{0,2,1:T(8,128)S(1)} async-done(((f32[256,16,16]{0,2,1:T(8,128)}), f32[256,16,16]{0,2,1:T(8,128)S(1)}, u32[]{:S(2)}, u32[]{:S(2)}) %all-to-all-start.3) | async-done | bytes 262176 | tf_op jit(solution)/shard_map/all_to_all | solution.py:190
  89.3 4.7 %all-to-all-start.2 = ((bf16[256,16,256]{2,0,1:T(8,128)(2,1)}), bf16[256,16,256]{2,0,1:T(8,128)(2,1)}, u32[]{:S(2)}, u32[]{:S(2)}) async-start(bf16[256,16,256]{2,0,1:T(8,128)(2,1)} %bitcast.32), calls=%async_computation.2 | async-start | bytes 4194304 | tf_op jit(solution)/shard_map/all_to_all | solution.py:205
  94.0 1.4 fusion.15.grad_ref
  95.4 3.0 %shard_map.78 = f32[256,512]{1,0:T(8,128)} custom-call(f32[256,512]{1,0:T(8,128)} %get-tuple-element.5.seg_ref, f32[256,512]{1,0:T(8,128)} %fusion.15.grad_ref), custom_call_target="tpu_custom_call" | custom-call | flops 4456448 | bytes 1572864 | tf_op jit(solution)/shard_map/pallas_call | solution.py:142
  98.4 2.5 %fusion.4 = f32[256,256]{0,1:T(8,128)} fusion(f32[256,512]{1,0:T(8,128)} %shard_map.78, f32[512,512]{0,1:T(8,128)} %maximum_bitcast_fusion), kind=kOutput, calls=%fused_computation.13 | convolution fusion | flops 402653184 | bytes 1310720 | tf_op jit(solution)/shard_map/dot_general | solution.py:163
  100.9 27.1 %all-to-all-done.2 = bf16[256,16,256]{2,0,1:T(8,128)(2,1)} async-done(((bf16[256,16,256]{2,0,1:T(8,128)(2,1)}), bf16[256,16,256]{2,0,1:T(8,128)(2,1)}, u32[]{:S(2)}, u32[]{:S(2)}) %all-to-all-start.2) | async-done | bytes 2097184 | tf_op jit(solution)/shard_map/all_to_all | solution.py:205
  128.0 4.1 %all-to-all-start.4 = ((f32[256,16,16]{0,2,1:T(8,128)}), f32[256,16,16]{0,2,1:T(8,128)S(1)}, u32[]{:S(2)}, u32[]{:S(2)}) async-start(f32[256,16,16]{0,2,1:T(8,128)} %bitcast.9), calls=%async_computation.4 | async-start | bytes 524288 | tf_op jit(solution)/shard_map/all_to_all | solution.py:209
  132.2 2.6 %reduce_sum.12 = bf16[256,256]{1,0:T(8,128)(2,1)} reduce(bf16[256,16,256]{2,0,1:T(8,128)(2,1)} %all-to-all-done.2, bf16[]{:T(256)} %constant.46.clone.1), dimensions={1}, to_apply=%region_0.1 | reduce | flops 983040 | bytes 2228226 | tf_op jit(solution)/shard_map/reduce_sum | solution.py:214
  134.7 9.2 %all-to-all-done.4 = f32[256,16,16]{0,2,1:T(8,128)S(1)} async-done(((f32[256,16,16]{0,2,1:T(8,128)}), f32[256,16,16]{0,2,1:T(8,128)S(1)}, u32[]{:S(2)}, u32[]{:S(2)}) %all-to-all-start.4) | async-done | bytes 262176 | tf_op jit(solution)/shard_map/all_to_all | solution.py:209
  143.9 0.8 copy.26
  (3 shorter events, 0.0 us)
Async XLA Ops:
  7.2 57.5 %copy-start = (bf16[256,4096]{1,0:T(8,128)(2,1)S(1)}, bf16[256,4096]{1,0:T(8,128)(2,1)}, u32[]{:S(2)}) copy-start(bf16[256,4096]{1,0:T(8,128)(2,1)} %param.10) | copy-start | bytes 6291460
  7.2 57.5 %all-gather.2.cloned.1.call-start = ((), (), s32[]{:S(2)}) async-start(), calls=%async_computation.5 | async-start | bytes 2228224 | tf_op jit(solution)/shard_map/all_gather | solution.py:181
  9.8 21.6 %all-to-all-start = ((bf16[2,256,256]{1,0,2:T(2,128)(2,1)}), bf16[2,256,256]{1,0,2:T(2,128)(2,1)S(1)}, u32[]{:S(2)}, u32[]{:S(2)}) async-start(bf16[2,256,256]{1,0,2:T(2,128)(2,1)} %copy.21), calls=%async_computation | async-start | bytes 524288 | tf_op jit(solution)/shard_map/all_to_all | solution.py:177
  38.4 8.9 %copy-start.2 = (bf16[256,256]{1,0:T(8,128)(2,1)S(1)}, bf16[256,256]{1,0:T(8,128)(2,1)}, u32[]{:S(2)}) copy-start(bf16[256,256]{1,0:T(8,128)(2,1)} %param.6) | copy-start | bytes 393220
  43.9 23.8 %all-to-all-start.1 = ((f32[256,16,16]{0,2,1:T(8,128)}), f32[256,16,16]{0,2,1:T(8,128)S(1)}, u32[]{:S(2)}, u32[]{:S(2)}) async-start(f32[256,16,16]{0,2,1:T(8,128)} %bitcast.36), calls=%async_computation.1 | async-start | bytes 524288 | tf_op jit(solution)/shard_map/all_to_all | solution.py:200
  49.1 28.6 %copy-start.3 = (f32[256]{0:T(256)S(1)}, f32[256]{0:T(256)}, u32[]{:S(2)}) copy-start(f32[256]{0:T(256)} %param.9) | copy-start | bytes 3076
  67.7 0.7 copy-start.1
  68.4 20.9 %all-to-all-start.3 = ((f32[256,16,16]{0,2,1:T(8,128)}), f32[256,16,16]{0,2,1:T(8,128)S(1)}, u32[]{:S(2)}, u32[]{:S(2)}) async-start(f32[256,16,16]{0,2,1:T(8,128)} %bitcast.35), calls=%async_computation.3 | async-start | bytes 524288 | tf_op jit(solution)/shard_map/all_to_all | solution.py:190
  89.3 38.8 %all-to-all-start.2 = ((bf16[256,16,256]{2,0,1:T(8,128)(2,1)}), bf16[256,16,256]{2,0,1:T(8,128)(2,1)}, u32[]{:S(2)}, u32[]{:S(2)}) async-start(bf16[256,16,256]{2,0,1:T(8,128)(2,1)} %bitcast.32), calls=%async_computation.2 | async-start | bytes 4194304 | tf_op jit(solution)/shard_map/all_to_all | solution.py:205
  128.0 15.9 %all-to-all-start.4 = ((f32[256,16,16]{0,2,1:T(8,128)}), f32[256,16,16]{0,2,1:T(8,128)S(1)}, u32[]{:S(2)}, u32[]{:S(2)}) async-start(f32[256,16,16]{0,2,1:T(8,128)} %bitcast.9), calls=%async_computation.4 | async-start | bytes 524288 | tf_op jit(solution)/shard_map/all_to_all | solution.py:209
Sparse Core Ops, SparseCore 0:
  10.4 54.2 all-gather.1

commit v6 on v5

--- a/solution.py
+++ b/solution.py
@@ -187,7 +187,6 @@
     )
     gate_wide = gating.astype(jnp.float32)
     grad_mixed = upstream * gate_wide
-    grad_t = lax.all_to_all(grad_mixed, "ctx", 1, 1, tiled=True)
 
     conv_spec, seg_spec = conv_products(
         transform_t(first_half, signal_t),
@@ -203,6 +202,8 @@
     gated_rows = (gate_wide * mixed_sum).astype(jnp.bfloat16)
     partial_out = jnp.dot(gated_rows, w_out, preferred_element_type=jnp.float32)
     pieces = lax.all_to_all(partial_out.astype(jnp.bfloat16), "ch", 1, 0, tiled=True)
+    pieces, grad_mixed = lax.optimization_barrier((pieces, grad_mixed))
+    grad_t = lax.all_to_all(grad_mixed, "ctx", 1, 1, tiled=True)
 
     lag_spec = lag_products(seg_spec, transform_t(second_half, grad_t), width)
     filter_grad_t = inverse_t(inverse[:block_len], lag_spec)

time: 152 us -> 152 us (level)
  blocking collectives: 0 us -> 30.5 us
  waiting for transfers between devices: 65.3 us -> 47.5 us
  starting transfers between devices: 31.6 us -> 20.3 us
    all_to_all x0 -> x2, blocking collectives: none -> 30.5 us  [the longest x1 15.6 us: body(): grad_t = lax.all_to_all(grad_mixed, 'ctx', 1, 1, tiled=True)]
    all_to_all x2 -> x0, starting transfers between devices: 12.7 us -> none  [the longest x1 9.3 us: body(): grad_t = lax.all_to_all(grad_mixed, 'ctx', 1, 1, tiled=True)]
    all_to_all x1, waiting for transfers between devices: 27.1 us -> 16.7 us  [body(): lax.all_to_all(partial_out.astype(jnp.bfloat16), 'ch', 1, 0, tiled=True)]
    all_to_all x2 -> x0, waiting for transfers between devices: 8.18 us -> none  [the longest x1 8.18 us: body(): grad_t = lax.all_to_all(grad_mixed, 'ctx', 1, 1, tiled=True)]
    unnamed x13 -> x9, local copies, waits for them, and re-layouts: 5.47 us -> 3 us
    all_gather x1, waiting for transfers between devices: 15.5 us -> 17.9 us  [body(): cot_rows = lax.all_gather(cotangent, 'ch', axis=1, tiled=True)]
    all_to_all x1, starting transfers between devices: 4.72 us -> 6.82 us  [body(): lax.all_to_all(partial_out.astype(jnp.bfloat16), 'ch', 1, 0, tiled=True)]
  transfers between devices with their start and end apart: 6 -> 4, of which waited for: 5 -> 4; matrix products, arithmetic and copies ran while one was open for 22% -> 17% of each run, Pallas kernels for 4% -> 2%
where the time goes in v6:
time: 152 us; the launch traced here: 151 us
  waiting for transfers between devices  47.5 us (31%)
  blocking collectives  30.5 us (20%)
  starting transfers between devices  20.3 us (13%)
  between operations  14.2 us (9%)
  matrix products  13.6 us (9%)
  other arithmetic  10.7 us (7%)
  local copies, waits for them, and re-layouts  8.46 us (6%)
  Pallas kernels  5.84 us (4%)
    all_gather x1, waiting for transfers between devices, body(): cot_rows = lax.all_gather(cotangent, 'ch', axis=1, tiled=True)  17.9 us
    all_to_all x1, waiting for transfers between devices, body(): lax.all_to_all(partial_out.astype(jnp.bfloat16), 'ch', 1, 0, tiled=True)  16.7 us
    all_to_all x1, blocking collectives, body(): grad_t = lax.all_to_all(grad_mixed, 'ctx', 1, 1, tiled=True)  15.6 us
    all_to_all x1, blocking collectives, body(): convolved = lax.all_to_all(convolved_t, 'ctx', 1, 1, tiled=True)  14.9 us
    all_to_all x1, starting transfers between devices, body(): pair_t = lax.all_to_all(pair, 'ctx', 2, 2, tiled=True)  9.97 us
    all_to_all x1, waiting for transfers between devices, body(): filter_grad = lax.all_to_all(filter_grad_t, 'ctx', 1, 1, tiled=True)  8.37 us
    all_to_all x1, starting transfers between devices, body(): lax.all_to_all(partial_out.astype(jnp.bfloat16), 'ch', 1, 0, tiled=True)  6.82 us
    dot_general x4, matrix products, transform_t(): lax.dot_general(block_rows.astype(jnp.float32), dft_table, (((0,), (1,)),...  5.25 us
  transfers between devices with their start and end apart: 4, of which 4 were waited for; matrix products, arithmetic and copies ran while one was open for 17% of the time, Pallas kernels for 2%

profile of v6, /device:TPU:1, one launch (start us, length us, event | category | flops | bytes accessed | tf_op | source)
XLA Modules:
  0.0 151.0 jit_solution(7812269091847910356)
XLA Ops:
  7.2 0.0 copy-start
  7.2 1.1 pad_maximum_fusion.1
  8.3 0.9 copy.20
  9.2 10.0 %all-to-all-start = ((bf16[2,256,256]{1,0,2:T(2,128)(2,1)}), bf16[2,256,256]{1,0,2:T(2,128)(2,1)S(1)}, u32[]{:S(2)}, u32[]{:S(2)}) async-start(bf16[2,256,256]{1,0,2:T(2,128)(2,1)} %copy.20), calls=%async_computation | async-start | bytes 524288 | tf_op jit(solution)/shard_map/all_to_all | solution.py:177
  19.2 0.0 all-gather.2.cloned.1.call-start
  19.2 0.7 all-gather.2.cloned.1.call-update
  19.9 2.0 %select_multiply_fusion = (f32[256,512]{1,0:T(8,128)S(1)}, f32[256,512]{1,0:T(8,128)S(1)}) fusion(f32[512]{0:T(512)S(1)} %fusion.28, pred[256]{0:T(512)(128)(4,1)S(1)} %iota_compare_fusion), kind=kLoop, calls=%fused_computation.19 | loop fusion | flops 2490368 | bytes 1050880 | tf_op jit(solution)/shard_map/mul | solution.py:26
  22.0 2.0 %multiply_multiply_fusion = f32[256,512]{1,0:T(8,128)S(1)} fusion(f32[256]{0:T(256)S(1)} %broadcast_select_fusion), kind=kLoop, calls=%fused_computation.20 | loop fusion | flops 2097152 | bytes 525312 | tf_op jit(solution)/shard_map/mul | solution.py:25
  24.0 1.9 %fusion.13 = f32[256,512]{1,0:T(8,128)S(1)} fusion(), kind=kLoop, calls=%fused_computation.28 | loop fusion | flops 1835008 | bytes 524288 | tf_op jit(solution)/shard_map/cos | solution.py:25
  25.9 1.1 maximum_bitcast_fusion
  26.9 3.8 %all-to-all-done = bf16[2,256,256]{1,0,2:T(2,128)(2,1)S(1)} async-done(((bf16[2,256,256]{1,0,2:T(2,128)(2,1)}), bf16[2,256,256]{1,0,2:T(2,128)(2,1)S(1)}, u32[]{:S(2)}, u32[]{:S(2)}) %all-to-all-start) | async-done | bytes 262176 | tf_op jit(solution)/shard_map/all_to_all | solution.py:177
  30.8 1.2 fusion.34
  31.9 1.1 copy.27
  33.0 1.1 copy.28
  34.1 1.3 fusion.14.high_ref
  35.3 1.3 fusion.20.low_ref
  36.6 1.3 fusion.17.taps_ref
  37.9 0.0 copy-start.1
  37.9 0.0 copy-start.2
  37.9 2.9 %shard_map.77 = (f32[256,512]{1,0:T(8,128)}, f32[256,512]{1,0:T(8,128)}) custom-call(f32[256,512]{1,0:T(8,128)} %fusion.20.low_ref, f32[256,512]{1,0:T(8,128)} %fusion.14.high_ref, f32[256,512]{1,0:T(8,128)} %fusion.17.taps_ref), custom_call_target="tpu_custom_call" | custom-call | flops 4456448 | bytes 2621440 | tf_op jit(solution)/shard_map/pallas_call | solution.py:125
  40.8 1.8 %fusion.6 = f32[256,256]{0,1:T(8,128)S(1)} fusion(f32[256,512]{1,0:T(8,128)} %get-tuple-element.6, f32[512,512]{0,1:T(8,128)} %maximum_bitcast_fusion), kind=kOutput, calls=%fused_computation.16 | convolution fusion | flops 402653184 | bytes 1310720 | tf_op jit(solution)/shard_map/dot_general | solution.py:163
  42.6 14.9 %all_to_all.60 = f32[256,16,16]{0,2,1:T(8,128)} all-to-all(f32[256,16,16]{0,2,1:T(8,128)S(1)} %bitcast.35), channel_id=1, replica_groups=mesh['ctx'=16,'ch'=16] {'ctx'}, dimensions={1} | all-to-all | bytes 524288 | tf_op jit(solution)/shard_map/all_to_all | solution.py:199
  57.5 1.1 copy.23
  58.6 0.0 copy-done
  58.6 0.0 copy-done.1
  58.6 0.0 copy-done.2
  58.6 1.6 %convolution_convert_fusion = bf16[256,4096]{1,0:T(8,128)(2,1)S(1)} fusion(bf16[256,4096]{1,0:T(8,128)(2,1)S(1)} %copy-done, bf16[256,256]{1,0:T(8,128)(2,1)S(1)} %copy-done.1, f32[256,256]{1,0:T(8,128)S(1)} %copy.23, bf16[256,256]{1,0:T(8,128)(2,1)} %param.6, f32[256]{0:T(256)S(1)} %copy-done.2), kind=kOutput, calls=%fused_computation | convolution fusion | flops 538312704 | bytes 4719616 | tf_op jit(solution)/shard_map/dot_general | solution.py:203
  60.2 1.5 %copy.31 = bf16[32,16,8,256]{3,2,0,1:T(8,128)(2,1)} copy(bf16[32,16,8,256]{3,2,1,0:T(8,128)(2,1)S(1)} %bitcast.33) | data formatting | bytes 4194304 | tf_op jit(solution)/shard_map/all_to_all | solution.py:204
  61.8 6.8 %all-to-all-start.2 = ((bf16[256,16,256]{2,0,1:T(8,128)(2,1)}), bf16[256,16,256]{2,0,1:T(8,128)(2,1)}, u32[]{:S(2)}, u32[]{:S(2)}) async-start(bf16[256,16,256]{2,0,1:T(8,128)(2,1)} %bitcast.32), calls=%async_computation.2 | async-start | bytes 4194304 | tf_op jit(solution)/shard_map/all_to_all | solution.py:204
  68.6 17.9 %all-gather.2.cloned.1.call-done = bf16[256,4096]{1,0:T(8,128)(2,1)} async-done(((bf16[256,256]{1,0:T(8,128)(2,1)}), bf16[256,4096]{1,0:T(8,128)(2,1)}) %all-gather.2.cloned.1.call-update) | async-done | bytes 2097168 | tf_op jit(solution)/shard_map/all_gather | solution.py:181
  86.5 2.3 %convolution_multiply_fusion = f32[256,256]{1,0:T(8,128)S(1)} fusion(bf16[256,4096]{1,0:T(8,128)(2,1)} %all-gather.2.cloned.1.call-done, bf16[256,4096]{1,0:T(8,128)(2,1)S(1)} %copy-done, bf16[256,256]{1,0:T(8,128)(2,1)S(1)} %copy-done.1), kind=kOutput, calls=%fused_computation.2 | convolution fusion | flops 537001984 | bytes 4587520 | tf_op jit(solution)/shard_map/dot_general | solution.py:182
  88.8 16.7 %all-to-all-done.2 = bf16[256,16,256]{2,0,1:T(8,128)(2,1)} async-done(((bf16[256,16,256]{2,0,1:T(8,128)(2,1)}), bf16[256,16,256]{2,0,1:T(8,128)(2,1)}, u32[]{:S(2)}, u32[]{:S(2)}) %all-to-all-start.2) | async-done | bytes 2097184 | tf_op jit(solution)/shard_map/all_to_all | solution.py:204
  105.5 0.8 copy.25
  106.3 15.6 %all_to_all.61 = f32[256,16,16]{0,2,1:T(8,128)S(1)} all-to-all(f32[256,16,16]{0,2,1:T(8,128)} %bitcast.38), channel_id=1, replica_groups=mesh['ctx'=16,'ch'=16] {'ctx'}, dimensions={1} | all-to-all | bytes 524288 | tf_op jit(solution)/shard_map/all_to_all | solution.py:206
  122.0 1.4 fusion.15.grad_ref
  123.4 3.0 %shard_map.78 = f32[256,512]{1,0:T(8,128)} custom-call(f32[256,512]{1,0:T(8,128)} %get-tuple-element.8.seg_ref, f32[256,512]{1,0:T(8,128)} %fusion.15.grad_ref), custom_call_target="tpu_custom_call" | custom-call | flops 4456448 | bytes 1572864 | tf_op jit(solution)/shard_map/pallas_call | solution.py:142
  126.4 2.5 %fusion.4 = f32[256,256]{0,1:T(8,128)} fusion(f32[256,512]{1,0:T(8,128)} %shard_map.78, f32[512,512]{0,1:T(8,128)} %maximum_bitcast_fusion), kind=kOutput, calls=%fused_computation.13 | convolution fusion | flops 402653184 | bytes 1310720 | tf_op jit(solution)/shard_map/dot_general | solution.py:163
  128.9 3.4 %all-to-all-start.4 = ((f32[256,16,16]{0,2,1:T(8,128)}), f32[256,16,16]{0,2,1:T(8,128)S(1)}, u32[]{:S(2)}, u32[]{:S(2)}) async-start(f32[256,16,16]{0,2,1:T(8,128)} %bitcast.12), calls=%async_computation.4 | async-start | bytes 524288 | tf_op jit(solution)/shard_map/all_to_all | solution.py:210
  132.3 2.6 %reduce = bf16[256,256]{1,0:T(8,128)(2,1)} reduce(bf16[16,256,256]{2,1,0:T(8,128)(2,1)} %bitcast.9, bf16[]{:T(256)} %constant.46), dimensions={0}, to_apply=%region_0.1.clone | reduce | flops 983040 | bytes 2228226 | tf_op jit(solution)/shard_map/reduce_sum | solution.py:215
  134.9 8.4 %all-to-all-done.4 = f32[256,16,16]{0,2,1:T(8,128)S(1)} async-done(((f32[256,16,16]{0,2,1:T(8,128)}), f32[256,16,16]{0,2,1:T(8,128)S(1)}, u32[]{:S(2)}, u32[]{:S(2)}) %all-to-all-start.4) | async-done | bytes 262176 | tf_op jit(solution)/shard_map/all_to_all | solution.py:210
  143.3 0.8 copy.26
  (3 shorter events, 0.0 us)
Async XLA Ops:
  7.2 51.4 %copy-start = (bf16[256,4096]{1,0:T(8,128)(2,1)S(1)}, bf16[256,4096]{1,0:T(8,128)(2,1)}, u32[]{:S(2)}) copy-start(bf16[256,4096]{1,0:T(8,128)(2,1)} %param.10) | copy-start | bytes 6291460
  9.2 21.6 %all-to-all-start = ((bf16[2,256,256]{1,0,2:T(2,128)(2,1)}), bf16[2,256,256]{1,0,2:T(2,128)(2,1)S(1)}, u32[]{:S(2)}, u32[]{:S(2)}) async-start(bf16[2,256,256]{1,0,2:T(2,128)(2,1)} %copy.20), calls=%async_computation | async-start | bytes 524288 | tf_op jit(solution)/shard_map/all_to_all | solution.py:177
  19.2 67.3 %all-gather.2.cloned.1.call-start = ((), (), s32[]{:S(2)}) async-start(), calls=%async_computation.5 | async-start | bytes 2228224 | tf_op jit(solution)/shard_map/all_gather | solution.py:181
  37.9 20.7 %copy-start.1 = (bf16[256,256]{1,0:T(8,128)(2,1)S(1)}, bf16[256,256]{1,0:T(8,128)(2,1)}, u32[]{:S(2)}) copy-start(bf16[256,256]{1,0:T(8,128)(2,1)} %param.7) | copy-start | bytes 393220
  37.9 20.7 %copy-start.2 = (f32[256]{0:T(256)S(1)}, f32[256]{0:T(256)}, u32[]{:S(2)}) copy-start(f32[256]{0:T(256)} %param.9) | copy-start | bytes 3076
  61.8 43.8 %all-to-all-start.2 = ((bf16[256,16,256]{2,0,1:T(8,128)(2,1)}), bf16[256,16,256]{2,0,1:T(8,128)(2,1)}, u32[]{:S(2)}, u32[]{:S(2)}) async-start(bf16[256,16,256]{2,0,1:T(8,128)(2,1)} %bitcast.32), calls=%async_computation.2 | async-start | bytes 4194304 | tf_op jit(solution)/shard_map/all_to_all | solution.py:204
  128.9 14.4 %all-to-all-start.4 = ((f32[256,16,16]{0,2,1:T(8,128)}), f32[256,16,16]{0,2,1:T(8,128)S(1)}, u32[]{:S(2)}, u32[]{:S(2)}) async-start(f32[256,16,16]{0,2,1:T(8,128)} %bitcast.12), calls=%async_computation.4 | async-start | bytes 524288 | tf_op jit(solution)/shard_map/all_to_all | solution.py:210
Sparse Core Ops, SparseCore 0:
  22.4 64.0 all-gather.1

commit v7 on v6

--- a/solution.py
+++ b/solution.py
@@ -178,24 +178,28 @@
     signal_t, taps_t = pair_t[0], pair_t[1]
 
     ch_count = lax.axis_size("ch")
-    cot_rows = lax.all_gather(cotangent, "ch", axis=1, tiled=True)
+    cot_copies = jnp.tile(cotangent, (1, ch_count))
+    pair_t, cot_copies = lax.optimization_barrier((pair_t, cot_copies))
+    signal_t, taps_t = pair_t[0], pair_t[1]
+    cot_rows = lax.all_to_all(cot_copies, "ch", 1, 1, tiled=True)
+    gate_wide = gating.astype(jnp.float32)
+
+    conv_spec, seg_spec = conv_products(
+        transform_t(first_half, signal_t),
+        transform_t(second_half, signal_t),
+        transform_t(first_half, taps_t),
+        width,
+    )
+
+    conv_spec, cot_rows = lax.optimization_barrier((conv_spec, cot_rows))
+    convolved_t = inverse_t(inverse[block_len:], conv_spec)
     upstream = lax.dot_general(
         cot_rows,
         w_out,
         (((1,), (1,)), ((), ())),
         preferred_element_type=jnp.float32,
     )
-    gate_wide = gating.astype(jnp.float32)
     grad_mixed = upstream * gate_wide
-
-    conv_spec, seg_spec = conv_products(
-        transform_t(first_half, signal_t),
-        transform_t(second_half, signal_t),
-        transform_t(first_half, taps_t),
-        width,
-    )
-
-    convolved_t = inverse_t(inverse[block_len:], conv_spec)
     convolved = lax.all_to_all(convolved_t, "ctx", 1, 1, tiled=True)
 
     mixed_sum = convolved + skip_gain[None, :] * inputs.astype(jnp.float32)

time: 152 us -> 174 us (1.14)
  waiting for transfers between devices: 47.5 us -> 70.1 us
  between operations: 14.2 us -> 0.78 us
  local copies, waits for them, and re-layouts: 8.46 us -> 16.6 us
  starting transfers between devices: 20.3 us -> 24.6 us
    all_to_all x0 -> x1, waiting for transfers between devices: none -> 19.3 us  [body(): cot_rows = lax.all_to_all(cot_copies, 'ch', 1, 1, tiled=True)]
    all_gather x1 -> x0, waiting for transfers between devices: 17.9 us -> none  [body(): cot_rows = lax.all_gather(cotangent, 'ch', axis=1, tiled=True)]
    all_to_all x1, waiting for transfers between devices: 16.7 us -> 31.9 us  [body(): lax.all_to_all(partial_out.astype(jnp.bfloat16), 'ch', 1, 0, tiled=True)]
    all_to_all x0 -> x2, local copies, waits for them, and re-layouts: none -> 7.82 us  [body(): cot_rows = lax.all_to_all(cot_copies, 'ch', 1, 1, tiled=True)]
    all_to_all x0 -> x1, starting transfers between devices: none -> 6.81 us  [body(): cot_rows = lax.all_to_all(cot_copies, 'ch', 1, 1, tiled=True)]
    all_to_all x1, waiting for transfers between devices: 3.84 us -> 10.6 us  [body(): pair_t = lax.all_to_all(pair, 'ctx', 2, 2, tiled=True)]
    all_to_all x1, starting transfers between devices: 6.82 us -> 4.42 us  [body(): lax.all_to_all(partial_out.astype(jnp.bfloat16), 'ch', 1, 0, tiled=True)]
  transfers between devices with their start and end apart: 4 -> 4, of which waited for: 4 -> 4; matrix products, arithmetic and copies ran while one was open for 17% -> 10% of each run, Pallas kernels for 2% -> 2%
where the time goes in v7:
time: 174 us; the launch traced here: 173 us
  waiting for transfers between devices  70.1 us (40%)
  blocking collectives  31.1 us (18%)
  starting transfers between devices  24.6 us (14%)
  local copies, waits for them, and re-layouts  16.6 us (10%)
  matrix products  13.6 us (8%)
  other arithmetic  10.7 us (6%)
  Pallas kernels  5.8 us (3%)
    all_to_all x1, waiting for transfers between devices, body(): lax.all_to_all(partial_out.astype(jnp.bfloat16), 'ch', 1, 0, tiled=True)  31.9 us
    all_to_all x1, waiting for transfers between devices, body(): cot_rows = lax.all_to_all(cot_copies, 'ch', 1, 1, tiled=True)  19.3 us
    all_to_all x1, blocking collectives, body(): convolved = lax.all_to_all(convolved_t, 'ctx', 1, 1, tiled=True)  15.7 us
    all_to_all x1, blocking collectives, body(): grad_t = lax.all_to_all(grad_mixed, 'ctx', 1, 1, tiled=True)  15.4 us
    all_to_all x1, waiting for transfers between devices, body(): pair_t = lax.all_to_all(pair, 'ctx', 2, 2, tiled=True)  10.6 us
    all_to_all x1, starting transfers between devices, body(): pair_t = lax.all_to_all(pair, 'ctx', 2, 2, tiled=True)  9.97 us
    all_to_all x1, waiting for transfers between devices, body(): filter_grad = lax.all_to_all(filter_grad_t, 'ctx', 1, 1, tiled=True)  8.37 us
    all_to_all x2, local copies, waits for them, and re-layouts, body(): cot_rows = lax.all_to_all(cot_copies, 'ch', 1, 1, tiled=True)  7.82 us
  transfers between devices with their start and end apart: 4, of which 4 were waited for; matrix products, arithmetic and copies ran while one was open for 10% of the time, Pallas kernels for 2%

profile of v7, /device:TPU:1, one launch (start us, length us, event | category | flops | bytes accessed | tf_op | source)
XLA Modules:
  0.0 173.4 jit_solution(5843391361346847251)
XLA Ops:
  0.6 0.0 copy-start
  0.6 1.1 pad_maximum_fusion.1
  1.8 0.9 copy.20
  2.7 10.0 %all-to-all-start = ((bf16[2,256,256]{1,0,2:T(2,128)(2,1)}), bf16[2,256,256]{1,0,2:T(2,128)(2,1)S(1)}, u32[]{:S(2)}, u32[]{:S(2)}) async-start(bf16[2,256,256]{1,0,2:T(2,128)(2,1)} %copy.20), calls=%async_computation | async-start | bytes 524288 | tf_op jit(solution)/shard_map/all_to_all | solution.py:177
  12.6 1.0 copy.21
  13.6 10.6 %all-to-all-done = bf16[2,256,256]{1,0,2:T(2,128)(2,1)S(1)} async-done(((bf16[2,256,256]{1,0,2:T(2,128)(2,1)}), bf16[2,256,256]{1,0,2:T(2,128)(2,1)S(1)}, u32[]{:S(2)}, u32[]{:S(2)}) %all-to-all-start) | async-done | bytes 262176 | tf_op jit(solution)/shard_map/all_to_all | solution.py:177
  24.2 0.0 copy-start.1
  24.2 1.5 tile.4
  25.8 3.9 %copy.24 = bf16[256,16,256]{2,0,1:T(8,128)(2,1)} copy(bf16[256,16,256]{0,2,1:T(8,128)(2,1)} %tile.4) | data formatting | bytes 4194304 | tf_op jit(solution)/shard_map/all_to_all | solution.py:184
  29.7 0.0 copy-done.1
  29.7 6.8 %all-to-all-start.1 = ((bf16[256,16,256]{2,0,1:T(8,128)(2,1)}), bf16[256,16,256]{2,0,1:T(8,128)(2,1)}, u32[]{:S(2)}, u32[]{:S(2)}) async-start(bf16[256,16,256]{2,0,1:T(8,128)(2,1)} %copy.24), calls=%async_computation.1 | async-start | bytes 4194304 | tf_op jit(solution)/shard_map/all_to_all | solution.py:184
  36.5 1.9 %fusion.13 = f32[256,512]{1,0:T(8,128)S(1)} fusion(), kind=kLoop, calls=%fused_computation.28 | loop fusion | flops 1835008 | bytes 524288 | tf_op jit(solution)/shard_map/cos | solution.py:25
  38.4 2.0 %multiply_multiply_fusion = f32[256,512]{1,0:T(8,128)S(1)} fusion(f32[256]{0:T(256)S(1)} %broadcast_select_fusion), kind=kLoop, calls=%fused_computation.20 | loop fusion | flops 2097152 | bytes 525312 | tf_op jit(solution)/shard_map/mul | solution.py:25
  40.4 2.0 %select_multiply_fusion = (f32[256,512]{1,0:T(8,128)S(1)}, f32[256,512]{1,0:T(8,128)S(1)}) fusion(f32[512]{0:T(512)S(1)} %fusion.25, pred[256]{0:T(512)(128)(4,1)S(1)} %iota_compare_fusion), kind=kLoop, calls=%fused_computation.19 | loop fusion | flops 2490368 | bytes 1050880 | tf_op jit(solution)/shard_map/mul | solution.py:26
  42.4 1.1 maximum_bitcast_fusion
  43.5 1.1 copy.22
  44.6 1.3 fusion.14.high_ref
  45.9 1.2 fusion.17.taps_ref
  47.2 1.3 fusion.19.low_ref
  48.4 2.9 %shard_map.77 = (f32[256,512]{1,0:T(8,128)}, f32[256,512]{1,0:T(8,128)}) custom-call(f32[256,512]{1,0:T(8,128)} %fusion.19.low_ref, f32[256,512]{1,0:T(8,128)} %fusion.14.high_ref, f32[256,512]{1,0:T(8,128)} %fusion.17.taps_ref), custom_call_target="tpu_custom_call" | custom-call | flops 4456448 | bytes 2621440 | tf_op jit(solution)/shard_map/pallas_call | solution.py:125
  51.3 19.3 %all-to-all-done.1 = bf16[256,16,256]{2,0,1:T(8,128)(2,1)} async-done(((bf16[256,16,256]{2,0,1:T(8,128)(2,1)}), bf16[256,16,256]{2,0,1:T(8,128)(2,1)}, u32[]{:S(2)}, u32[]{:S(2)}) %all-to-all-start.1) | async-done | bytes 2097184 | tf_op jit(solution)/shard_map/all_to_all | solution.py:184
  70.5 3.9 %copy.25 = bf16[256,16,256]{0,2,1:T(8,128)(2,1)} copy(bf16[256,16,256]{2,0,1:T(8,128)(2,1)} %all-to-all-done.1) | data formatting | bytes 4194304 | tf_op jit(solution)/shard_map/all_to_all | solution.py:184
  74.4 0.0 copy-start.2
  74.4 0.0 copy-start.3
  74.4 1.9 %fusion.6 = f32[256,256]{0,1:T(8,128)S(1)} fusion(f32[256,512]{1,0:T(8,128)} %get-tuple-element.13, f32[512,512]{0,1:T(8,128)} %maximum_bitcast_fusion), kind=kOutput, calls=%fused_computation.16 | convolution fusion | flops 402653184 | bytes 1310720 | tf_op jit(solution)/shard_map/dot_general | solution.py:163
  76.3 15.7 %all_to_all.72 = f32[256,16,16]{0,2,1:T(8,128)} all-to-all(f32[256,16,16]{0,2,1:T(8,128)S(1)} %bitcast.38), channel_id=1, replica_groups=mesh['ctx'=16,'ch'=16] {'ctx'}, dimensions={1} | all-to-all | bytes 524288 | tf_op jit(solution)/shard_map/all_to_all | solution.py:203
  92.0 1.1 copy.26
  93.1 0.0 copy-done
  93.1 0.0 copy-done.2
  93.1 0.0 copy-done.3
  93.1 1.6 convolution_convert_fusion
  94.7 1.5 copy.32
  96.2 4.4 %all-to-all-start.3 = ((bf16[256,16,256]{2,0,1:T(8,128)(2,1)}), bf16[256,16,256]{2,0,1:T(8,128)(2,1)}, u32[]{:S(2)}, u32[]{:S(2)}) async-start(bf16[256,16,256]{2,0,1:T(8,128)(2,1)} %bitcast.35), calls=%async_computation.3 | async-start | bytes 4194304 | tf_op jit(solution)/shard_map/all_to_all | solution.py:208
  100.7 2.3 %convolution_multiply_fusion = f32[256,256]{1,0:T(8,128)S(1)} fusion(bf16[256,4096]{0,1:T(8,128)(2,1)} %bitcast.34, bf16[256,4096]{1,0:T(8,128)(2,1)S(1)} %copy-done, bf16[256,256]{1,0:T(8,128)(2,1)S(1)} %copy-done.2), kind=kOutput, calls=%fused_computation.2 | convolution fusion | flops 537001984 | bytes 4587520 | tf_op jit(solution)/shard_map/dot_general | solution.py:196
  103.0 31.9 %all-to-all-done.3 = bf16[256,16,256]{2,0,1:T(8,128)(2,1)} async-done(((bf16[256,16,256]{2,0,1:T(8,128)(2,1)}), bf16[256,16,256]{2,0,1:T(8,128)(2,1)}, u32[]{:S(2)}, u32[]{:S(2)}) %all-to-all-start.3) | async-done | bytes 2097184 | tf_op jit(solution)/shard_map/all_to_all | solution.py:208
  135.0 0.8 copy.28
  135.8 15.4 %all_to_all.73 = f32[256,16,16]{0,2,1:T(8,128)S(1)} all-to-all(f32[256,16,16]{0,2,1:T(8,128)} %bitcast.41), channel_id=1, replica_groups=mesh['ctx'=16,'ch'=16] {'ctx'}, dimensions={1} | all-to-all | bytes 524288 | tf_op jit(solution)/shard_map/all_to_all | solution.py:210
  151.3 1.4 fusion.15.grad_ref
  152.7 3.0 %shard_map.78 = f32[256,512]{1,0:T(8,128)} custom-call(f32[256,512]{1,0:T(8,128)} %get-tuple-element.16.seg_ref, f32[256,512]{1,0:T(8,128)} %fusion.15.grad_ref), custom_call_target="tpu_custom_call" | custom-call | flops 4456448 | bytes 1572864 | tf_op jit(solution)/shard_map/pallas_call | solution.py:142
  155.6 2.5 %fusion.4 = f32[256,256]{0,1:T(8,128)} fusion(f32[256,512]{1,0:T(8,128)} %shard_map.78, f32[512,512]{0,1:T(8,128)} %maximum_bitcast_fusion), kind=kOutput, calls=%fused_computation.13 | convolution fusion | flops 402653184 | bytes 1310720 | tf_op jit(solution)/shard_map/dot_general | solution.py:163
  158.2 3.4 %all-to-all-start.5 = ((f32[256,16,16]{0,2,1:T(8,128)}), f32[256,16,16]{0,2,1:T(8,128)S(1)}, u32[]{:S(2)}, u32[]{:S(2)}) async-start(f32[256,16,16]{0,2,1:T(8,128)} %bitcast.15), calls=%async_computation.5 | async-start | bytes 524288 | tf_op jit(solution)/shard_map/all_to_all | solution.py:214
  161.6 2.6 %reduce = bf16[256,256]{1,0:T(8,128)(2,1)} reduce(bf16[16,256,256]{2,1,0:T(8,128)(2,1)} %bitcast.12, bf16[]{:T(256)} %constant.46), dimensions={0}, to_apply=%region_0.1.clone | reduce | flops 983040 | bytes 2228226 | tf_op jit(solution)/shard_map/reduce_sum | solution.py:219
  164.2 8.4 %all-to-all-done.5 = f32[256,16,16]{0,2,1:T(8,128)S(1)} async-done(((f32[256,16,16]{0,2,1:T(8,128)}), f32[256,16,16]{0,2,1:T(8,128)S(1)}, u32[]{:S(2)}, u32[]{:S(2)}) %all-to-all-start.5) | async-done | bytes 262176 | tf_op jit(solution)/shard_map/all_to_all | solution.py:214
  172.5 0.8 copy.29
  (3 shorter events, 0.0 us)
Async XLA Ops:
  0.6 92.4 %copy-start = (bf16[256,4096]{1,0:T(8,128)(2,1)S(1)}, bf16[256,4096]{1,0:T(8,128)(2,1)}, u32[]{:S(2)}) copy-start(bf16[256,4096]{1,0:T(8,128)(2,1)} %param.10) | copy-start | bytes 6291460
  2.7 21.6 %all-to-all-start = ((bf16[2,256,256]{1,0,2:T(2,128)(2,1)}), bf16[2,256,256]{1,0,2:T(2,128)(2,1)S(1)}, u32[]{:S(2)}, u32[]{:S(2)}) async-start(bf16[2,256,256]{1,0,2:T(2,128)(2,1)} %copy.20), calls=%async_computation | async-start | bytes 524288 | tf_op jit(solution)/shard_map/all_to_all | solution.py:177
  24.2 5.4 %copy-start.1 = (bf16[2,256,256]{1,0,2:T(2,128)(2,1)}, bf16[2,256,256]{1,0,2:T(2,128)(2,1)S(1)}, u32[]{:S(2)}) copy-start(bf16[2,256,256]{1,0,2:T(2,128)(2,1)S(1)} %all-to-all-done) | copy-start | bytes 786436
  29.7 40.9 %all-to-all-start.1 = ((bf16[256,16,256]{2,0,1:T(8,128)(2,1)}), bf16[256,16,256]{2,0,1:T(8,128)(2,1)}, u32[]{:S(2)}, u32[]{:S(2)}) async-start(bf16[256,16,256]{2,0,1:T(8,128)(2,1)} %copy.24), calls=%async_computation.1 | async-start | bytes 4194304 | tf_op jit(solution)/shard_map/all_to_all | solution.py:184
  74.4 18.6 %copy-start.2 = (bf16[256,256]{1,0:T(8,128)(2,1)S(1)}, bf16[256,256]{1,0:T(8,128)(2,1)}, u32[]{:S(2)}) copy-start(bf16[256,256]{1,0:T(8,128)(2,1)} %param.7) | copy-start | bytes 393220
  74.4 18.6 %copy-start.3 = (f32[256]{0:T(256)S(1)}, f32[256]{0:T(256)}, u32[]{:S(2)}) copy-start(f32[256]{0:T(256)} %param.9) | copy-start | bytes 3076
  96.2 38.7 %all-to-all-start.3 = ((bf16[256,16,256]{2,0,1:T(8,128)(2,1)}), bf16[256,16,256]{2,0,1:T(8,128)(2,1)}, u32[]{:S(2)}, u32[]{:S(2)}) async-start(bf16[256,16,256]{2,0,1:T(8,128)(2,1)} %bitcast.35), calls=%async_computation.3 | async-start | bytes 4194304 | tf_op jit(solution)/shard_map/all_to_all | solution.py:208
  158.2 14.4 %all-to-all-start.5 = ((f32[256,16,16]{0,2,1:T(8,128)}), f32[256,16,16]{0,2,1:T(8,128)S(1)}, u32[]{:S(2)}, u32[]{:S(2)}) async-start(f32[256,16,16]{0,2,1:T(8,128)} %bitcast.15), calls=%async_computation.5 | async-start | bytes 524288 | tf_op jit(solution)/shard_map/all_to_all | solution.py:214

commit v8 on v6

--- a/solution.py
+++ b/solution.py
@@ -154,14 +154,14 @@
 
 def transform_t(dft_table, block_rows):
     return lax.dot_general(
-        block_rows.astype(jnp.float32), dft_table, (((0,), (1,)), ((), ())),
+        block_rows.astype(jnp.float32), dft_table, (((1,), (1,)), ((), ())),
         precision=exact_prec,
     )
 
 
 def inverse_t(inverse_rows, spec_t):
     return lax.dot_general(
-        inverse_rows, spec_t, (((1,), (1,)), ((), ())), precision=exact_prec
+        spec_t, inverse_rows, (((1,), (1,)), ((), ())), precision=exact_prec
     )
 
 
@@ -173,8 +173,8 @@
     first_half = forward[:, :block_len]
     second_half = forward[:, block_len:]
 
-    pair = jnp.stack([inputs, filter_taps])
-    pair_t = lax.all_to_all(pair, "ctx", 2, 2, tiled=True)
+    pair = jnp.stack([inputs.T, filter_taps.T])
+    pair_t = lax.all_to_all(pair, "ctx", 1, 1, tiled=True)
     signal_t, taps_t = pair_t[0], pair_t[1]
 
     ch_count = lax.axis_size("ch")
@@ -196,18 +196,18 @@
     )
 
     convolved_t = inverse_t(inverse[block_len:], conv_spec)
-    convolved = lax.all_to_all(convolved_t, "ctx", 1, 1, tiled=True)
+    convolved = lax.all_to_all(convolved_t, "ctx", 0, 0, tiled=True).T
 
     mixed_sum = convolved + skip_gain[None, :] * inputs.astype(jnp.float32)
     gated_rows = (gate_wide * mixed_sum).astype(jnp.bfloat16)
     partial_out = jnp.dot(gated_rows, w_out, preferred_element_type=jnp.float32)
     pieces = lax.all_to_all(partial_out.astype(jnp.bfloat16), "ch", 1, 0, tiled=True)
     pieces, grad_mixed = lax.optimization_barrier((pieces, grad_mixed))
-    grad_t = lax.all_to_all(grad_mixed, "ctx", 1, 1, tiled=True)
+    grad_t = lax.all_to_all(grad_mixed.T, "ctx", 0, 0, tiled=True)
 
     lag_spec = lag_products(seg_spec, transform_t(second_half, grad_t), width)
     filter_grad_t = inverse_t(inverse[:block_len], lag_spec)
-    filter_grad = lax.all_to_all(filter_grad_t, "ctx", 1, 1, tiled=True)
+    filter_grad = lax.all_to_all(filter_grad_t, "ctx", 0, 0, tiled=True).T
 
     output = (
         pieces.astype(jnp.float32)

time: 152 us -> 151 us (level)
    all_gather x1, waiting for transfers between devices: 17.9 us -> 20.1 us  [body(): cot_rows = lax.all_gather(cotangent, 'ch', axis=1, tiled=True)]
  transfers between devices with their start and end apart: 4 -> 4, of which waited for: 4 -> 4; matrix products, arithmetic and copies ran while one was open for 17% -> 15% of each run, Pallas kernels for 2% -> 2%
where the time goes in v8:
time: 151 us; the launch traced here: 150 us
  waiting for transfers between devices  48.3 us (32%)
  blocking collectives  30.6 us (20%)
  starting transfers between devices  20.3 us (13%)
  between operations  14.2 us (9%)
  matrix products  13.4 us (9%)
  other arithmetic  9.58 us (6%)
  local copies, waits for them, and re-layouts  7.79 us (5%)
  Pallas kernels  5.88 us (4%)
    all_gather x1, waiting for transfers between devices, body(): cot_rows = lax.all_gather(cotangent, 'ch', axis=1, tiled=True)  20.1 us
    all_to_all x1, blocking collectives, body(): grad_t = lax.all_to_all(grad_mixed.T, 'ctx', 0, 0, tiled=True)  15.8 us
    all_to_all x1, waiting for transfers between devices, body(): lax.all_to_all(partial_out.astype(jnp.bfloat16), 'ch', 1, 0, tiled=True)  15.3 us
    all_to_all x1, blocking collectives, body(): convolved = lax.all_to_all(convolved_t, 'ctx', 0, 0, tiled=True).T  14.8 us
    all_to_all x1, starting transfers between devices, body(): pair_t = lax.all_to_all(pair, 'ctx', 1, 1, tiled=True)  9.97 us
    all_to_all x1, waiting for transfers between devices, body(): filter_grad = lax.all_to_all(filter_grad_t, 'ctx', 0, 0, tiled=True).T  8.37 us
    all_to_all x1, starting transfers between devices, body(): lax.all_to_all(partial_out.astype(jnp.bfloat16), 'ch', 1, 0, tiled=True)  6.83 us
    dot_general x4, matrix products, transform_t(): lax.dot_general(block_rows.astype(jnp.float32), dft_table, (((1,), (1,)),...  5.19 us
  transfers between devices with their start and end apart: 4, of which 4 were waited for; matrix products, arithmetic and copies ran while one was open for 15% of the time, Pallas kernels for 2%

profile of v8, /device:TPU:1, one launch (start us, length us, event | category | flops | bytes accessed | tf_op | source)
XLA Modules:
  0.0 150.0 jit_solution(17735991603270827347)
XLA Ops:
  7.2 0.0 copy-start
  7.2 1.2 copy.20
  8.3 1.0 copy.21
  9.4 1.0 copy.22
  10.4 10.0 %all-to-all-start = ((bf16[2,256,256]{2,0,1:T(2,128)(2,1)}), bf16[2,256,256]{2,0,1:T(2,128)(2,1)S(1)}, u32[]{:S(2)}, u32[]{:S(2)}) async-start(bf16[2,256,256]{2,0,1:T(2,128)(2,1)} %copy.22), calls=%async_computation | async-start | bytes 524288 | tf_op jit(solution)/shard_map/all_to_all | solution.py:177
  20.3 0.0 all-gather.2.cloned.1.call-start
  20.4 0.7 all-gather.2.cloned.1.call-update
  21.1 2.0 %select_multiply_fusion = (f32[256,512]{1,0:T(8,128)S(1)}, f32[256,512]{1,0:T(8,128)S(1)}) fusion(f32[512]{0:T(512)S(1)} %fusion.25, pred[256]{0:T(512)(128)(4,1)S(1)} %iota_compare_fusion), kind=kLoop, calls=%fused_computation.18 | loop fusion | flops 2490368 | bytes 1050880 | tf_op jit(solution)/shard_map/mul | solution.py:26
  23.1 2.0 %multiply_multiply_fusion = f32[256,512]{1,0:T(8,128)S(1)} fusion(f32[256]{0:T(256)S(1)} %broadcast_select_fusion), kind=kLoop, calls=%fused_computation.19 | loop fusion | flops 2097152 | bytes 525312 | tf_op jit(solution)/shard_map/mul | solution.py:25
  25.1 1.9 %fusion.13 = f32[256,512]{1,0:T(8,128)S(1)} fusion(), kind=kLoop, calls=%fused_computation.29 | loop fusion | flops 1835008 | bytes 524288 | tf_op jit(solution)/shard_map/cos | solution.py:22
  27.0 1.1 maximum_bitcast_fusion
  28.1 3.8 %all-to-all-done = bf16[2,256,256]{2,0,1:T(2,128)(2,1)S(1)} async-done(((bf16[2,256,256]{2,0,1:T(2,128)(2,1)}), bf16[2,256,256]{2,0,1:T(2,128)(2,1)S(1)}, u32[]{:S(2)}, u32[]{:S(2)}) %all-to-all-start) | async-done | bytes 262176 | tf_op jit(solution)/shard_map/all_to_all | solution.py:177
  31.9 0.4 fusion.31
  32.3 1.3 fusion.14.high_ref
  33.5 1.3 fusion.19.low_ref
  34.8 1.3 fusion.17.taps_ref
  36.0 0.0 copy-start.1
  36.1 0.0 copy-start.2
  36.1 2.9 %shard_map.77 = (f32[256,512]{1,0:T(8,128)}, f32[256,512]{1,0:T(8,128)}) custom-call(f32[256,512]{1,0:T(8,128)} %fusion.19.low_ref, f32[256,512]{1,0:T(8,128)} %fusion.14.high_ref, f32[256,512]{1,0:T(8,128)} %fusion.17.taps_ref), custom_call_target="tpu_custom_call" | custom-call | flops 4456448 | bytes 2621440 | tf_op jit(solution)/shard_map/pallas_call | solution.py:125
  39.0 1.8 %fusion.6 = f32[256,256]{1,0:T(8,128)S(1)} fusion(f32[256,512]{1,0:T(8,128)} %get-tuple-element.6, f32[512,512]{0,1:T(8,128)} %maximum_bitcast_fusion), kind=kOutput, calls=%fused_computation.15 | convolution fusion | flops 402653184 | bytes 1310720 | tf_op jit(solution)/shard_map/dot_general | solution.py:163
  40.8 14.8 %all_to_all.60 = f32[16,16,256]{2,1,0:T(8,128)} all-to-all(f32[16,16,256]{2,1,0:T(8,128)S(1)} %bitcast.47), channel_id=1, replica_groups=mesh['ctx'=16,'ch'=16] {'ctx'}, dimensions={0} | all-to-all | bytes 524288 | tf_op jit(solution)/shard_map/all_to_all | solution.py:199
  55.6 1.1 copy.25
  56.7 0.0 copy-done
  56.7 0.0 copy-done.1
  56.7 0.0 copy-done.2
  56.7 1.6 %convolution_convert_fusion = bf16[256,4096]{1,0:T(8,128)(2,1)S(1)} fusion(bf16[256,4096]{1,0:T(8,128)(2,1)S(1)} %copy-done, bf16[256,256]{1,0:T(8,128)(2,1)S(1)} %copy-done.1, f32[256,256]{0,1:T(8,128)S(1)} %copy.25, bf16[256,256]{1,0:T(8,128)(2,1)} %param.6, f32[256]{0:T(256)S(1)} %copy-done.2), kind=kOutput, calls=%fused_computation | convolution fusion | flops 538312704 | bytes 4719616 | tf_op jit(solution)/shard_map/dot_general | solution.py:203
  58.3 1.5 %copy.38 = bf16[32,16,8,256]{3,2,0,1:T(8,128)(2,1)} copy(bf16[32,16,8,256]{3,2,1,0:T(8,128)(2,1)S(1)} %bitcast.44) | data formatting | bytes 4194304 | tf_op jit(solution)/shard_map/all_to_all | solution.py:204
  59.9 6.8 %all-to-all-start.2 = ((bf16[256,16,256]{2,0,1:T(8,128)(2,1)}), bf16[256,16,256]{2,0,1:T(8,128)(2,1)}, u32[]{:S(2)}, u32[]{:S(2)}) async-start(bf16[256,16,256]{2,0,1:T(8,128)(2,1)} %bitcast.43), calls=%async_computation.2 | async-start | bytes 4194304 | tf_op jit(solution)/shard_map/all_to_all | solution.py:204
  66.7 20.1 %all-gather.2.cloned.1.call-done = bf16[256,4096]{1,0:T(8,128)(2,1)} async-done(((bf16[256,256]{1,0:T(8,128)(2,1)}), bf16[256,4096]{1,0:T(8,128)(2,1)}) %all-gather.2.cloned.1.call-update) | async-done | bytes 2097168 | tf_op jit(solution)/shard_map/all_gather | solution.py:181
  86.8 2.3 %convolution_multiply_fusion = f32[256,256]{1,0:T(8,128)S(1)} fusion(bf16[256,4096]{1,0:T(8,128)(2,1)} %all-gather.2.cloned.1.call-done, bf16[256,4096]{1,0:T(8,128)(2,1)S(1)} %copy-done, bf16[256,256]{1,0:T(8,128)(2,1)S(1)} %copy-done.1), kind=kOutput, calls=%fused_computation.2 | convolution fusion | flops 537001984 | bytes 4587520 | tf_op jit(solution)/shard_map/dot_general | solution.py:182
  89.2 15.3 %all-to-all-done.2 = bf16[256,16,256]{2,0,1:T(8,128)(2,1)} async-done(((bf16[256,16,256]{2,0,1:T(8,128)(2,1)}), bf16[256,16,256]{2,0,1:T(8,128)(2,1)}, u32[]{:S(2)}, u32[]{:S(2)}) %all-to-all-start.2) | async-done | bytes 2097184 | tf_op jit(solution)/shard_map/all_to_all | solution.py:204
  104.4 0.8 copy.27
  105.3 15.8 %all_to_all.61 = f32[16,16,256]{2,1,0:T(8,128)S(1)} all-to-all(f32[16,16,256]{2,1,0:T(8,128)} %bitcast.50), channel_id=1, replica_groups=mesh['ctx'=16,'ch'=16] {'ctx'}, dimensions={0} | all-to-all | bytes 524288 | tf_op jit(solution)/shard_map/all_to_all | solution.py:206
  121.1 1.4 fusion.15.grad_ref
  122.5 3.0 %shard_map.78 = f32[256,512]{1,0:T(8,128)} custom-call(f32[256,512]{1,0:T(8,128)} %get-tuple-element.8.seg_ref, f32[256,512]{1,0:T(8,128)} %fusion.15.grad_ref), custom_call_target="tpu_custom_call" | custom-call | flops 4456448 | bytes 1572864 | tf_op jit(solution)/shard_map/pallas_call | solution.py:142
  125.5 2.5 %fusion.4 = f32[256,256]{1,0:T(8,128)} fusion(f32[256,512]{1,0:T(8,128)} %shard_map.78, f32[512,512]{0,1:T(8,128)} %maximum_bitcast_fusion), kind=kOutput, calls=%fused_computation.13 | convolution fusion | flops 402653184 | bytes 1310720 | tf_op jit(solution)/shard_map/dot_general | solution.py:163
  128.0 3.4 %all-to-all-start.4 = ((f32[16,16,256]{2,1,0:T(8,128)}), f32[16,16,256]{2,1,0:T(8,128)S(1)}, u32[]{:S(2)}, u32[]{:S(2)}) async-start(f32[16,16,256]{2,1,0:T(8,128)} %bitcast.16), calls=%async_computation.4 | async-start | bytes 524288 | tf_op jit(solution)/shard_map/all_to_all | solution.py:210
  131.4 2.6 %reduce = bf16[256,256]{1,0:T(8,128)(2,1)} reduce(bf16[16,256,256]{2,1,0:T(8,128)(2,1)} %bitcast.12, bf16[]{:T(256)} %constant.46), dimensions={0}, to_apply=%region_0.1.clone | reduce | flops 983040 | bytes 2228226 | tf_op jit(solution)/shard_map/reduce_sum | solution.py:215
  134.0 8.4 %all-to-all-done.4 = f32[16,16,256]{2,1,0:T(8,128)S(1)} async-done(((f32[16,16,256]{2,1,0:T(8,128)}), f32[16,16,256]{2,1,0:T(8,128)S(1)}, u32[]{:S(2)}, u32[]{:S(2)}) %all-to-all-start.4) | async-done | bytes 262176 | tf_op jit(solution)/shard_map/all_to_all | solution.py:210
  142.4 0.8 copy.28
  (4 shorter events, 0.0 us)
Async XLA Ops:
  7.2 49.5 %copy-start = (bf16[256,4096]{1,0:T(8,128)(2,1)S(1)}, bf16[256,4096]{1,0:T(8,128)(2,1)}, u32[]{:S(2)}) copy-start(bf16[256,4096]{1,0:T(8,128)(2,1)} %param.10) | copy-start | bytes 6291460
  10.4 21.6 %all-to-all-start = ((bf16[2,256,256]{2,0,1:T(2,128)(2,1)}), bf16[2,256,256]{2,0,1:T(2,128)(2,1)S(1)}, u32[]{:S(2)}, u32[]{:S(2)}) async-start(bf16[2,256,256]{2,0,1:T(2,128)(2,1)} %copy.22), calls=%async_computation | async-start | bytes 524288 | tf_op jit(solution)/shard_map/all_to_all | solution.py:177
  20.3 66.5 %all-gather.2.cloned.1.call-start = ((), (), s32[]{:S(2)}) async-start(), calls=%async_computation.5 | async-start | bytes 2228224 | tf_op jit(solution)/shard_map/all_gather | solution.py:181
  36.0 20.6 %copy-start.1 = (bf16[256,256]{1,0:T(8,128)(2,1)S(1)}, bf16[256,256]{1,0:T(8,128)(2,1)}, u32[]{:S(2)}) copy-start(bf16[256,256]{1,0:T(8,128)(2,1)} %param.7) | copy-start | bytes 393220
  36.1 20.6 %copy-start.2 = (f32[256]{0:T(256)S(1)}, f32[256]{0:T(256)}, u32[]{:S(2)}) copy-start(f32[256]{0:T(256)} %param.9) | copy-start | bytes 3076
  59.9 44.6 %all-to-all-start.2 = ((bf16[256,16,256]{2,0,1:T(8,128)(2,1)}), bf16[256,16,256]{2,0,1:T(8,128)(2,1)}, u32[]{:S(2)}, u32[]{:S(2)}) async-start(bf16[256,16,256]{2,0,1:T(8,128)(2,1)} %bitcast.43), calls=%async_computation.2 | async-start | bytes 4194304 | tf_op jit(solution)/shard_map/all_to_all | solution.py:204
  128.0 14.4 %all-to-all-start.4 = ((f32[16,16,256]{2,1,0:T(8,128)}), f32[16,16,256]{2,1,0:T(8,128)S(1)}, u32[]{:S(2)}, u32[]{:S(2)}) async-start(f32[16,16,256]{2,1,0:T(8,128)} %bitcast.16), calls=%async_computation.4 | async-start | bytes 524288 | tf_op jit(solution)/shard_map/all_to_all | solution.py:210
Sparse Core Ops, SparseCore 0:
  23.5 63.2 all-gather.1

commit v9 on v8

--- a/solution.py
+++ b/solution.py
@@ -196,18 +196,22 @@
     )
 
     convolved_t = inverse_t(inverse[block_len:], conv_spec)
-    convolved = lax.all_to_all(convolved_t, "ctx", 0, 0, tiled=True).T
+    convolved = lax.all_to_all(
+        convolved_t.astype(jnp.bfloat16), "ctx", 0, 0, tiled=True
+    ).T.astype(jnp.float32)
 
     mixed_sum = convolved + skip_gain[None, :] * inputs.astype(jnp.float32)
     gated_rows = (gate_wide * mixed_sum).astype(jnp.bfloat16)
     partial_out = jnp.dot(gated_rows, w_out, preferred_element_type=jnp.float32)
     pieces = lax.all_to_all(partial_out.astype(jnp.bfloat16), "ch", 1, 0, tiled=True)
     pieces, grad_mixed = lax.optimization_barrier((pieces, grad_mixed))
-    grad_t = lax.all_to_all(grad_mixed.T, "ctx", 0, 0, tiled=True)
+    grad_t = lax.all_to_all(grad_mixed.T.astype(jnp.bfloat16), "ctx", 0, 0, tiled=True)
 
     lag_spec = lag_products(seg_spec, transform_t(second_half, grad_t), width)
     filter_grad_t = inverse_t(inverse[:block_len], lag_spec)
-    filter_grad = lax.all_to_all(filter_grad_t, "ctx", 0, 0, tiled=True).T
+    filter_grad = lax.all_to_all(
+        filter_grad_t.astype(jnp.bfloat16), "ctx", 0, 0, tiled=True
+    ).T.astype(jnp.float32)
 
     output = (
         pieces.astype(jnp.float32)

time: 151 us -> 145 us (0.960)
  blocking collectives: 30.6 us -> 27 us
  waiting for transfers between devices: 48.3 us -> 46.2 us
    all_to_all x1, waiting for transfers between devices: 15.3 us -> 4.78 us  [body(): lax.all_to_all(partial_out.astype(jnp.bfloat16), 'ch', 1, 0, tiled=True)]
    all_gather x1, waiting for transfers between devices: 20.1 us -> 30.6 us  [body(): cot_rows = lax.all_gather(cotangent, 'ch', axis=1, tiled=True)]
    all_to_all x2, blocking collectives: 30.6 us -> 27 us  [the longest x1 15 us: body(): lax.all_to_all(grad_mixed.T.astype(jnp.bfloat16), 'ctx', 0, 0, tiled=True)]
    all_to_all x1, waiting for transfers between devices: 8.37 us -> 6.36 us  [body(): lax.all_to_all(filter_grad_t.astype(jnp.bfloat16), 'ctx', 0, 0, tiled=True)]
  transfers between devices with their start and end apart: 4 -> 4, of which waited for: 4 -> 4; matrix products, arithmetic and copies ran while one was open for 15% -> 16% of each run, Pallas kernels for 2% -> 2%
where the time goes in v9:
time: 145 us; the launch traced here: 144 us
  waiting for transfers between devices  46.2 us (32%)
  blocking collectives  27 us (19%)
  starting transfers between devices  20.4 us (14%)
  between operations  14.2 us (10%)
  matrix products  13.2 us (9%)
  other arithmetic  10.4 us (7%)
  local copies, waits for them, and re-layouts  7.07 us (5%)
  Pallas kernels  5.86 us (4%)
    all_gather x1, waiting for transfers between devices, body(): cot_rows = lax.all_gather(cotangent, 'ch', axis=1, tiled=True)  30.6 us
    all_to_all x1, blocking collectives, body(): lax.all_to_all(grad_mixed.T.astype(jnp.bfloat16), 'ctx', 0, 0, tiled=True)  15 us
    all_to_all x1, blocking collectives, body(): lax.all_to_all(convolved_t.astype(jnp.bfloat16), 'ctx', 0, 0, tiled=True)  12.1 us
    all_to_all x1, starting transfers between devices, body(): pair_t = lax.all_to_all(pair, 'ctx', 1, 1, tiled=True)  9.97 us
    all_to_all x1, starting transfers between devices, body(): lax.all_to_all(partial_out.astype(jnp.bfloat16), 'ch', 1, 0, tiled=True)  6.96 us
    all_to_all x1, waiting for transfers between devices, body(): lax.all_to_all(filter_grad_t.astype(jnp.bfloat16), 'ctx', 0, 0, tiled=True)  6.36 us
    dot_general x4, matrix products, transform_t(): lax.dot_general(block_rows.astype(jnp.float32), dft_table, (((1,), (1,)),...  4.97 us
    all_to_all x1, waiting for transfers between devices, body(): lax.all_to_all(partial_out.astype(jnp.bfloat16), 'ch', 1, 0, tiled=True)  4.78 us
  transfers between devices with their start and end apart: 4, of which 4 were waited for; matrix products, arithmetic and copies ran while one was open for 16% of the time, Pallas kernels for 2%

profile of v9, /device:TPU:1, one launch (start us, length us, event | category | flops | bytes accessed | tf_op | source)
XLA Modules:
  0.0 144.2 jit_solution(1292315938119700381)
XLA Ops:
  7.2 0.0 copy-start
  7.2 1.2 copy.20
  8.3 1.0 copy.21
  9.4 1.0 copy.22
  10.4 10.0 %all-to-all-start = ((bf16[2,256,256]{2,0,1:T(2,128)(2,1)}), bf16[2,256,256]{2,0,1:T(2,128)(2,1)S(1)}, u32[]{:S(2)}, u32[]{:S(2)}) async-start(bf16[2,256,256]{2,0,1:T(2,128)(2,1)} %copy.22), calls=%async_computation | async-start | bytes 524288 | tf_op jit(solution)/shard_map/all_to_all | solution.py:177
  20.3 0.0 all-gather.2.cloned.1.call-start
  20.4 0.7 all-gather.2.cloned.1.call-update
  21.1 2.0 %select_multiply_fusion = (f32[256,512]{1,0:T(8,128)S(1)}, f32[256,512]{1,0:T(8,128)S(1)}) fusion(f32[512]{0:T(512)S(1)} %fusion.23, pred[256]{0:T(512)(128)(4,1)S(1)} %iota_compare_fusion), kind=kLoop, calls=%fused_computation.18 | loop fusion | flops 2490368 | bytes 1050880 | tf_op jit(solution)/shard_map/mul | solution.py:26
  23.1 2.0 %multiply_multiply_fusion = f32[256,512]{1,0:T(8,128)S(1)} fusion(f32[256]{0:T(256)S(1)} %broadcast_select_fusion), kind=kLoop, calls=%fused_computation.19 | loop fusion | flops 2097152 | bytes 525312 | tf_op jit(solution)/shard_map/mul | solution.py:25
  25.1 1.9 %fusion.11 = f32[256,512]{1,0:T(8,128)S(1)} fusion(), kind=kLoop, calls=%fused_computation.30 | loop fusion | flops 1835008 | bytes 524288 | tf_op jit(solution)/shard_map/cos | solution.py:22
  27.0 1.1 maximum_bitcast_fusion
  28.1 3.8 %all-to-all-done = bf16[2,256,256]{2,0,1:T(2,128)(2,1)S(1)} async-done(((bf16[2,256,256]{2,0,1:T(2,128)(2,1)}), bf16[2,256,256]{2,0,1:T(2,128)(2,1)S(1)}, u32[]{:S(2)}, u32[]{:S(2)}) %all-to-all-start) | async-done | bytes 262176 | tf_op jit(solution)/shard_map/all_to_all | solution.py:177
  31.9 0.4 fusion.29
  32.3 1.2 fusion.12.high_ref
  33.5 1.2 fusion.17.low_ref
  34.8 1.3 fusion.15.taps_ref
  36.0 0.0 copy-start.1
  36.0 0.0 copy-start.3
  36.0 2.9 %shard_map.77 = (f32[256,512]{1,0:T(8,128)}, f32[256,512]{1,0:T(8,128)}) custom-call(f32[256,512]{1,0:T(8,128)} %fusion.17.low_ref, f32[256,512]{1,0:T(8,128)} %fusion.12.high_ref, f32[256,512]{1,0:T(8,128)} %fusion.15.taps_ref), custom_call_target="tpu_custom_call" | custom-call | flops 4456448 | bytes 2621440 | tf_op jit(solution)/shard_map/pallas_call | solution.py:125
  38.9 1.8 %convolution_convert_fusion.2 = bf16[256,256]{1,0:T(8,128)(2,1)S(1)} fusion(f32[256,512]{1,0:T(8,128)} %get-tuple-element.6, f32[512,512]{0,1:T(8,128)} %maximum_bitcast_fusion), kind=kOutput, calls=%fused_computation.4 | convolution fusion | flops 402718720 | bytes 1179648 | tf_op jit(solution)/shard_map/dot_general | solution.py:163
  40.7 12.1 %all_to_all.54 = bf16[16,16,256]{2,1,0:T(8,128)(2,1)S(1)} all-to-all(bf16[16,16,256]{2,1,0:T(8,128)(2,1)S(1)} %bitcast.51), channel_id=1, replica_groups=mesh['ctx'=16,'ch'=16] {'ctx'}, dimensions={0} | all-to-all | bytes 262144 | tf_op jit(solution)/shard_map/all_to_all | solution.py:199
  52.8 0.7 bitcast_convert_fusion
  53.5 1.1 copy.25
  54.6 0.0 copy-done
  54.6 0.0 copy-done.1
  54.6 0.0 copy-done.3
  54.6 1.6 %convolution_convert_fusion = bf16[256,4096]{1,0:T(8,128)(2,1)S(1)} fusion(bf16[256,4096]{1,0:T(8,128)(2,1)S(1)} %copy-done, bf16[256,256]{1,0:T(8,128)(2,1)} %param.7, f32[256,256]{0,1:T(8,128)S(1)} %copy.25, bf16[256,256]{1,0:T(8,128)(2,1)S(1)} %copy-done.1, f32[256]{0:T(256)S(1)} %copy-done.3), kind=kOutput, calls=%fused_computation | convolution fusion | flops 538312704 | bytes 4719616 | tf_op jit(solution)/shard_map/dot_general | solution.py:205
  56.3 1.5 %copy.38 = bf16[32,16,8,256]{3,2,0,1:T(8,128)(2,1)} copy(bf16[32,16,8,256]{3,2,1,0:T(8,128)(2,1)S(1)} %bitcast.50) | data formatting | bytes 4194304 | tf_op jit(solution)/shard_map/all_to_all | solution.py:206
  57.8 0.0 copy-start.2
  57.8 7.0 %all-to-all-start.2 = ((bf16[256,16,256]{2,0,1:T(8,128)(2,1)}), bf16[256,16,256]{2,0,1:T(8,128)(2,1)}, u32[]{:S(2)}, u32[]{:S(2)}) async-start(bf16[256,16,256]{2,0,1:T(8,128)(2,1)} %bitcast.49), calls=%async_computation.2 | async-start | bytes 4194304 | tf_op jit(solution)/shard_map/all_to_all | solution.py:206
  64.8 30.6 %all-gather.2.cloned.1.call-done = bf16[256,4096]{1,0:T(8,128)(2,1)} async-done(((bf16[256,256]{1,0:T(8,128)(2,1)}), bf16[256,4096]{1,0:T(8,128)(2,1)}) %all-gather.2.cloned.1.call-update) | async-done | bytes 2097168 | tf_op jit(solution)/shard_map/all_gather | solution.py:181
  95.3 0.0 copy-done.2
  95.3 2.3 %convolution_multiply_fusion = bf16[256,256]{1,0:T(8,128)(2,1)S(1)} fusion(bf16[256,4096]{1,0:T(8,128)(2,1)} %all-gather.2.cloned.1.call-done, bf16[256,4096]{1,0:T(8,128)(2,1)S(1)} %copy-done, bf16[256,256]{1,0:T(8,128)(2,1)S(1)} %copy-done.2), kind=kOutput, calls=%fused_computation.2 | convolution fusion | flops 537067520 | bytes 4456448 | tf_op jit(solution)/shard_map/dot_general | solution.py:182
  97.7 4.8 %all-to-all-done.2 = bf16[256,16,256]{2,0,1:T(8,128)(2,1)} async-done(((bf16[256,16,256]{2,0,1:T(8,128)(2,1)}), bf16[256,16,256]{2,0,1:T(8,128)(2,1)}, u32[]{:S(2)}, u32[]{:S(2)}) %all-to-all-start.2) | async-done | bytes 2097184 | tf_op jit(solution)/shard_map/all_to_all | solution.py:206
  102.5 0.1 copy.27
  102.6 15.0 %all_to_all.55 = bf16[16,16,256]{2,1,0:T(8,128)(2,1)S(1)} all-to-all(bf16[16,16,256]{2,1,0:T(8,128)(2,1)S(1)} %bitcast.52), channel_id=1, replica_groups=mesh['ctx'=16,'ch'=16] {'ctx'}, dimensions={0} | all-to-all | bytes 262144 | tf_op jit(solution)/shard_map/all_to_all | solution.py:208
  117.5 1.2 fusion.13.grad_ref
  118.8 3.0 %shard_map.78 = f32[256,512]{1,0:T(8,128)} custom-call(f32[256,512]{1,0:T(8,128)} %get-tuple-element.8.seg_ref, f32[256,512]{1,0:T(8,128)} %fusion.13.grad_ref), custom_call_target="tpu_custom_call" | custom-call | flops 4456448 | bytes 1572864 | tf_op jit(solution)/shard_map/pallas_call | solution.py:142
  121.7 2.4 %convolution_convert_fusion.1 = bf16[256,256]{1,0:T(8,128)(2,1)} fusion(f32[256,512]{1,0:T(8,128)} %shard_map.78, f32[512,512]{0,1:T(8,128)} %maximum_bitcast_fusion), kind=kOutput, calls=%fused_computation.3 | convolution fusion | flops 402718720 | bytes 1179648 | tf_op jit(solution)/shard_map/dot_general | solution.py:163
  124.2 3.4 %all-to-all-start.4 = ((bf16[16,16,256]{2,1,0:T(8,128)(2,1)}), bf16[16,16,256]{2,1,0:T(8,128)(2,1)S(1)}, u32[]{:S(2)}, u32[]{:S(2)}) async-start(bf16[16,16,256]{2,1,0:T(8,128)(2,1)} %bitcast.16), calls=%async_computation.4 | async-start | bytes 262144 | tf_op jit(solution)/shard_map/all_to_all | solution.py:212
  127.6 2.6 %reduce = bf16[256,256]{1,0:T(8,128)(2,1)} reduce(bf16[16,256,256]{2,1,0:T(8,128)(2,1)} %bitcast.12, bf16[]{:T(256)} %constant.46), dimensions={0}, to_apply=%region_0.1.clone | reduce | flops 983040 | bytes 2228226 | tf_op jit(solution)/shard_map/reduce_sum | solution.py:219
  130.2 6.4 %all-to-all-done.4 = bf16[16,16,256]{2,1,0:T(8,128)(2,1)S(1)} async-done(((bf16[16,16,256]{2,1,0:T(8,128)(2,1)}), bf16[16,16,256]{2,1,0:T(8,128)(2,1)S(1)}, u32[]{:S(2)}, u32[]{:S(2)}) %all-to-all-start.4) | async-done | bytes 131104 | tf_op jit(solution)/shard_map/all_to_all | solution.py:212
  136.5 0.8 copy.28
  (5 shorter events, 0.1 us)
Async XLA Ops:
  7.2 47.4 %copy-start = (bf16[256,4096]{1,0:T(8,128)(2,1)S(1)}, bf16[256,4096]{1,0:T(8,128)(2,1)}, u32[]{:S(2)}) copy-start(bf16[256,4096]{1,0:T(8,128)(2,1)} %param.10) | copy-start | bytes 6291460
  10.4 21.6 %all-to-all-start = ((bf16[2,256,256]{2,0,1:T(2,128)(2,1)}), bf16[2,256,256]{2,0,1:T(2,128)(2,1)S(1)}, u32[]{:S(2)}, u32[]{:S(2)}) async-start(bf16[2,256,256]{2,0,1:T(2,128)(2,1)} %copy.22), calls=%async_computation | async-start | bytes 524288 | tf_op jit(solution)/shard_map/all_to_all | solution.py:177
  20.3 75.0 %all-gather.2.cloned.1.call-start = ((), (), s32[]{:S(2)}) async-start(), calls=%async_computation.5 | async-start | bytes 2228224 | tf_op jit(solution)/shard_map/all_gather | solution.py:181
  36.0 18.6 %copy-start.1 = (bf16[256,256]{1,0:T(8,128)(2,1)S(1)}, bf16[256,256]{1,0:T(8,128)(2,1)}, u32[]{:S(2)}) copy-start(bf16[256,256]{1,0:T(8,128)(2,1)} %param.6) | copy-start | bytes 393220
  36.0 18.6 %copy-start.3 = (f32[256]{0:T(256)S(1)}, f32[256]{0:T(256)}, u32[]{:S(2)}) copy-start(f32[256]{0:T(256)} %param.9) | copy-start | bytes 3076
  57.8 37.5 %copy-start.2 = (bf16[256,256]{1,0:T(8,128)(2,1)S(1)}, bf16[256,256]{1,0:T(8,128)(2,1)}, u32[]{:S(2)}) copy-start(bf16[256,256]{1,0:T(8,128)(2,1)} %param.7) | copy-start | bytes 393220
  57.8 44.7 %all-to-all-start.2 = ((bf16[256,16,256]{2,0,1:T(8,128)(2,1)}), bf16[256,16,256]{2,0,1:T(8,128)(2,1)}, u32[]{:S(2)}, u32[]{:S(2)}) async-start(bf16[256,16,256]{2,0,1:T(8,128)(2,1)} %bitcast.49), calls=%async_computation.2 | async-start | bytes 4194304 | tf_op jit(solution)/shard_map/all_to_all | solution.py:206
  124.2 12.4 %all-to-all-start.4 = ((bf16[16,16,256]{2,1,0:T(8,128)(2,1)}), bf16[16,16,256]{2,1,0:T(8,128)(2,1)S(1)}, u32[]{:S(2)}, u32[]{:S(2)}) async-start(bf16[16,16,256]{2,1,0:T(8,128)(2,1)} %bitcast.16), calls=%async_computation.4 | async-start | bytes 262144 | tf_op jit(solution)/shard_map/all_to_all | solution.py:212
Sparse Core Ops, SparseCore 0:
  23.5 71.7 all-gather.1

commit v10 on v9

--- a/solution.py
+++ b/solution.py
@@ -178,13 +178,22 @@
     signal_t, taps_t = pair_t[0], pair_t[1]
 
     ch_count = lax.axis_size("ch")
-    cot_rows = lax.all_gather(cotangent, "ch", axis=1, tiled=True)
-    upstream = lax.dot_general(
-        cot_rows,
-        w_out,
-        (((1,), (1,)), ((), ())),
-        preferred_element_type=jnp.float32,
-    )
+    me_ch = lax.axis_index("ch")
+    upstream = jnp.zeros((block_len, channels), jnp.float32)
+    for shift in range(ch_count):
+        if shift == 0:
+            block = cotangent
+        else:
+            block = lax.ppermute(
+                cotangent, "ch",
+                perm=[(j, (j + shift) % ch_count) for j in range(ch_count)],
+            )
+        owner = (me_ch - shift + ch_count) % ch_count
+        w_cols = lax.dynamic_slice_in_dim(w_out, owner * channels, channels, 1)
+        upstream = upstream + lax.dot_general(
+            block, w_cols, (((1,), (1,)), ((), ())),
+            preferred_element_type=jnp.float32,
+        )
     gate_wide = gating.astype(jnp.float32)
     grad_mixed = upstream * gate_wide
 

time: 145 us -> 158 us (1.090)
  starting transfers between devices: 20.4 us -> 55.8 us
  matrix products: 13.2 us -> 29.3 us
  waiting for transfers between devices: 46.2 us -> 33 us
  between operations: 14.2 us -> 1.13 us
  blocking collectives: 27 us -> 15.4 us
    all_gather x1 -> x0, waiting for transfers between devices: 30.6 us -> none  [body(): cot_rows = lax.all_gather(cotangent, 'ch', axis=1, tiled=True)]
    ppermute x0 -> x15, starting transfers between devices: none -> 27.8 us  [body(): lax.ppermute(cotangent, 'ch', perm=[(j, (j + shift) % ch_count) for j in...]
    ppermute x0 -> x15, waiting for transfers between devices: none -> 26.6 us  [body(): lax.ppermute(cotangent, 'ch', perm=[(j, (j + shift) % ch_count) for j in...]
    dot_general x1 -> x16, matrix products: 2.33 us -> 18.6 us  [body(): lax.dot_general(block, w_cols, (((1,), (1,)), ((), ())), preferred_elemen...]
    all_to_all x1 -> x0, blocking collectives: 12.1 us -> none  [body(): lax.all_to_all(convolved_t.astype(jnp.bfloat16), 'ctx', 0, 0, tiled=True)]
    all_to_all x0 -> x1, starting transfers between devices: none -> 8.07 us  [body(): lax.all_to_all(convolved_t.astype(jnp.bfloat16), 'ctx', 0, 0, tiled=True)]
    all_to_all x1, waiting for transfers between devices: 4.78 us -> 0.01 us  [body(): lax.all_to_all(partial_out.astype(jnp.bfloat16), 'ch', 1, 0, tiled=True)]
    all_to_all x1, waiting for transfers between devices: 3.82 us -> 0.01 us  [body(): pair_t = lax.all_to_all(pair, 'ctx', 1, 1, tiled=True)]
  transfers between devices with their start and end apart: 4 -> 19, of which waited for: 4 -> 4; matrix products, arithmetic and copies ran while one was open for 16% -> 26% of each run, Pallas kernels for 2% -> 2%
where the time goes in v10:
time: 158 us; the launch traced here: 156 us
  starting transfers between devices  55.8 us (35%)
  waiting for transfers between devices  33 us (21%)
  matrix products  29.3 us (19%)
  blocking collectives  15.4 us (10%)
  other arithmetic  9.65 us (6%)
  local copies, waits for them, and re-layouts  5.92 us (4%)
  Pallas kernels  5.84 us (4%)
    ppermute x15, starting transfers between devices, body(): lax.ppermute(cotangent, 'ch', perm=[(j, (j + shift) % ch_count) for j in...  27.8 us
    ppermute x15, waiting for transfers between devices, body(): lax.ppermute(cotangent, 'ch', perm=[(j, (j + shift) % ch_count) for j in...  26.6 us
    dot_general x16, matrix products, body(): lax.dot_general(block, w_cols, (((1,), (1,)), ((), ())), preferred_elemen...  18.6 us
    all_to_all x1, blocking collectives, body(): lax.all_to_all(grad_mixed.T.astype(jnp.bfloat16), 'ctx', 0, 0, tiled=True)  15.4 us
    all_to_all x1, starting transfers between devices, body(): pair_t = lax.all_to_all(pair, 'ctx', 1, 1, tiled=True)  10.6 us
    all_to_all x1, starting transfers between devices, body(): lax.all_to_all(convolved_t.astype(jnp.bfloat16), 'ctx', 0, 0, tiled=True)  8.07 us
    all_to_all x1, waiting for transfers between devices, body(): lax.all_to_all(filter_grad_t.astype(jnp.bfloat16), 'ctx', 0, 0, tiled=True)  6.37 us
    all_to_all x1, starting transfers between devices, body(): lax.all_to_all(partial_out.astype(jnp.bfloat16), 'ch', 1, 0, tiled=True)  6.01 us
  transfers between devices with their start and end apart: 19, of which 4 were waited for; matrix products, arithmetic and copies ran while one was open for 26% of the time, Pallas kernels for 2%

profile of v10, /device:TPU:1, one launch (start us, length us, event | category | flops | bytes accessed | tf_op | source)
XLA Modules:
  0.0 156.0 jit_solution(15771785115844864998)
XLA Ops:
  0.6 0.0 copy-start
  0.6 0.0 copy-start.9
  0.7 4.6 %collective-permute-start.12 = (bf16[256,256]{1,0:T(8,128)(2,1)}, bf16[256,256]{1,0:T(8,128)(2,1)}, u32[]{:S(2)}, u32[]{:S(2)}) collective-permute-start(bf16[256,256]{1,0:T(8,128)(2,1)} %param.11), channel_id=1, source_target_pairs={{0,13},{1,14},{2,15},{3,0},{4,1},{5,2},{6,3},{7,4},{8,5},{9,6},{10... | collective-permute-start | bytes 393224 | tf_op jit(solution)/shard_map/ppermute | solution.py:187
  5.2 0.5 collective-permute-start.11
  5.7 1.4 collective-permute-start.10
  7.0 3.9 %collective-permute-start.9 = (bf16[256,256]{1,0:T(8,128)(2,1)}, bf16[256,256]{1,0:T(8,128)(2,1)}, u32[]{:S(2)}, u32[]{:S(2)}) collective-permute-start(bf16[256,256]{1,0:T(8,128)(2,1)} %param.11), channel_id=1, source_target_pairs={{0,10},{1,11},{2,12},{3,13},{4,14},{5,15},{6,0},{7,1},{8,2},{9,3},... | collective-permute-start | bytes 393224 | tf_op jit(solution)/shard_map/ppermute | solution.py:187
  10.9 0.4 collective-permute-start.8
  11.3 1.0 copy.22
  12.3 1.1 copy.23
  13.4 1.0 copy.24
  14.4 10.6 %all-to-all-start = ((bf16[2,256,256]{2,0,1:T(2,128)(2,1)}), bf16[2,256,256]{2,0,1:T(2,128)(2,1)S(1)}, u32[]{:S(2)}, u32[]{:S(2)}) async-start(bf16[2,256,256]{2,0,1:T(2,128)(2,1)} %copy.24), calls=%async_computation | async-start | bytes 524288 | tf_op jit(solution)/shard_map/all_to_all | solution.py:177
  24.9 0.0 copy-start.11
  25.0 2.0 %multiply_multiply_fusion = f32[256,512]{1,0:T(8,128)S(1)} fusion(f32[256]{0:T(256)S(1)} %broadcast_select_fusion), kind=kLoop, calls=%fused_computation.35 | loop fusion | flops 2097152 | bytes 525312 | tf_op jit(solution)/shard_map/mul | solution.py:25
  27.0 0.9 fusion.60
  27.9 2.0 %select_multiply_fusion = (f32[256,512]{1,0:T(8,128)S(1)}, f32[256,512]{1,0:T(8,128)S(1)}) fusion(f32[512]{0:T(512)S(1)} %fusion.85, pred[256]{0:T(512)(128)(4,1)S(1)} %iota_compare_fusion), kind=kLoop, calls=%fused_computation.34 | loop fusion | flops 2490368 | bytes 1050880 | tf_op jit(solution)/shard_map/mul | solution.py:26
  29.9 1.1 maximum_bitcast_fusion
  31.0 0.1 copy.21
  31.2 1.9 %fusion.27 = f32[256,512]{1,0:T(8,128)S(1)} fusion(), kind=kLoop, calls=%fused_computation.47 | loop fusion | flops 1835008 | bytes 524288 | tf_op jit(solution)/shard_map/cos | solution.py:22
  33.2 2.7 %collective-permute-start.7 = (bf16[256,256]{1,0:T(8,128)(2,1)}, bf16[256,256]{1,0:T(8,128)(2,1)}, u32[]{:S(2)}, u32[]{:S(2)}) collective-permute-start(bf16[256,256]{1,0:T(8,128)(2,1)} %param.11), channel_id=1, source_target_pairs={{0,8},{1,9},{2,10},{3,11},{4,12},{5,13},{6,14},{7,15},{8,0},{9,1},... | collective-permute-start | bytes 393224 | tf_op jit(solution)/shard_map/ppermute | solution.py:187
  35.9 1.8 %fusion.36 = f32[256,256]{1,0:T(8,128)} fusion(bf16[256,256]{1,0:T(8,128)(2,1)} %collective-permute-done.12, bf16[256,4096]{1,0:T(8,128)(2,1)S(1)} %copy-done, s32[]{:T(128)S(6)} %select_n.198), kind=kOutput, calls=%fused_computation.57 | convolution fusion | flops 33554432 | bytes 524292 | tf_op jit(solution)/shard_map/dot_general | solution.py:193
  37.7 0.6 collective-permute-start.6
  38.3 1.8 %fusion.38 = f32[256,256]{1,0:T(8,128)} fusion(bf16[256,256]{1,0:T(8,128)(2,1)} %collective-permute-done.11, bf16[256,4096]{1,0:T(8,128)(2,1)S(1)} %copy-done, s32[]{:T(128)S(6)} %select_n.196), kind=kOutput, calls=%fused_computation.59 | convolution fusion | flops 33554432 | bytes 524292 | tf_op jit(solution)/shard_map/dot_general | solution.py:193
  40.2 2.3 %collective-permute-start.5 = (bf16[256,256]{1,0:T(8,128)(2,1)}, bf16[256,256]{1,0:T(8,128)(2,1)}, u32[]{:S(2)}, u32[]{:S(2)}) collective-permute-start(bf16[256,256]{1,0:T(8,128)(2,1)} %param.11), channel_id=1, source_target_pairs={{0,6},{1,7},{2,8},{3,9},{4,10},{5,11},{6,12},{7,13},{8,14},{9,15},... | collective-permute-start | bytes 393224 | tf_op jit(solution)/shard_map/ppermute | solution.py:187
  42.4 1.8 %fusion.40 = f32[256,256]{1,0:T(8,128)} fusion(bf16[256,256]{1,0:T(8,128)(2,1)} %collective-permute-done.10, bf16[256,4096]{1,0:T(8,128)(2,1)S(1)} %copy-done, s32[]{:T(128)S(6)} %select_n.194), kind=kOutput, calls=%fused_computation.61 | convolution fusion | flops 33554432 | bytes 524292 | tf_op jit(solution)/shard_map/dot_general | solution.py:193
  44.3 0.3 collective-permute-start.4
  44.5 1.8 %fusion.42 = f32[256,256]{1,0:T(8,128)} fusion(bf16[256,256]{1,0:T(8,128)(2,1)} %collective-permute-done.9, bf16[256,4096]{1,0:T(8,128)(2,1)S(1)} %copy-done, s32[]{:T(128)S(6)} %select_n.192), kind=kOutput, calls=%fused_computation.63 | convolution fusion | flops 33554432 | bytes 524292 | tf_op jit(solution)/shard_map/dot_general | solution.py:193
  46.4 0.4 fusion.91
  46.7 1.3 fusion.28.high_ref
  48.0 1.2 fusion.63.low_ref
  49.2 1.2 fusion.31.taps_ref
  50.4 2.9 %shard_map.77 = (f32[256,512]{1,0:T(8,128)}, f32[256,512]{1,0:T(8,128)}) custom-call(f32[256,512]{1,0:T(8,128)} %fusion.63.low_ref, f32[256,512]{1,0:T(8,128)} %fusion.28.high_ref, f32[256,512]{1,0:T(8,128)} %fusion.31.taps_ref), custom_call_target="tpu_custom_call" | custom-call | flops 4456448 | bytes 2621440 | tf_op jit(solution)/shard_map/pallas_call | solution.py:125
  53.3 2.4 %convolution_convert_fusion.2 = bf16[256,256]{1,0:T(8,128)(2,1)} fusion(f32[256,512]{1,0:T(8,128)} %get-tuple-element.6, f32[512,512]{0,1:T(8,128)} %maximum_bitcast_fusion), kind=kOutput, calls=%fused_computation.20 | convolution fusion | flops 402718720 | bytes 1179648 | tf_op jit(solution)/shard_map/dot_general | solution.py:163
  55.8 8.1 %all-to-all-start.1 = ((bf16[16,16,256]{2,1,0:T(8,128)(2,1)}), bf16[16,16,256]{2,1,0:T(8,128)(2,1)S(1)}, u32[]{:S(2)}, u32[]{:S(2)}) async-start(bf16[16,16,256]{2,1,0:T(8,128)(2,1)} %bitcast.71), calls=%async_computation.1 | async-start | bytes 262144 | tf_op jit(solution)/shard_map/all_to_all | solution.py:208
  63.8 2.5 %collective-permute-start = (bf16[256,256]{1,0:T(8,128)(2,1)}, bf16[256,256]{1,0:T(8,128)(2,1)S(1)}, u32[]{:S(2)}, u32[]{:S(2)}) collective-permute-start(bf16[256,256]{1,0:T(8,128)(2,1)} %param.11), channel_id=1, source_target_pairs={{0,1},{1,2},{2,3},{3,4},{4,5},{5,6},{6,7},{7,8},{8,9},{9,10},{10,1... | collective-permute-start | bytes 393224 | tf_op jit(solution)/shard_map/ppermute | solution.py:187
  66.3 1.8 %fusion.44 = f32[256,256]{1,0:T(8,128)} fusion(bf16[256,256]{1,0:T(8,128)(2,1)} %collective-permute-done.8, bf16[256,4096]{1,0:T(8,128)(2,1)S(1)} %copy-done, s32[]{:T(128)S(6)} %select_n.190), kind=kOutput, calls=%fused_computation.65 | convolution fusion | flops 33554432 | bytes 524292 | tf_op jit(solution)/shard_map/dot_general | solution.py:193
  68.2 4.2 %collective-permute-done = bf16[256,256]{1,0:T(8,128)(2,1)S(1)} collective-permute-done((bf16[256,256]{1,0:T(8,128)(2,1)}, bf16[256,256]{1,0:T(8,128)(2,1)S(1)}, u32[]{:S(2)}, u32[]{:S(2)}) %collective-permute-start) | collective-permute-done | bytes 131104 | tf_op jit(solution)/shard_map/ppermute | solution.py:187
  72.4 0.7 collective-permute-start.3
  73.1 1.9 %convolution_add_fusion.1 = f32[256,256]{1,0:T(8,128)} fusion(f32[256,256]{1,0:T(8,128)} %fusion.60, bf16[256,256]{1,0:T(8,128)(2,1)S(1)} %collective-permute-done, bf16[256,4096]{1,0:T(8,128)(2,1)S(1)} %copy-done, s32[]{:T(128)S(6)} %select_n.174), kind=kOutput, calls=%fused_computation.5 | convolution fusion | flops 33619968 | bytes 786436 | tf_op jit(solution)/shard_map/dot_general | solution.py:193
  75.0 0.8 convolution_convert_fusion
  75.8 1.5 copy.39
  77.3 6.0 %all-to-all-start.2 = ((bf16[256,16,256]{2,0,1:T(8,128)(2,1)}), bf16[256,16,256]{2,0,1:T(8,128)(2,1)}, u32[]{:S(2)}, u32[]{:S(2)}) async-start(bf16[256,16,256]{2,0,1:T(8,128)(2,1)} %bitcast.67), calls=%async_computation.2 | async-start | bytes 4194304 | tf_op jit(solution)/shard_map/all_to_all | solution.py:215
  83.4 2.6 %collective-permute-start.2 = (bf16[256,256]{1,0:T(8,128)(2,1)S(1)}, bf16[256,256]{1,0:T(8,128)(2,1)S(1)}, u32[]{:S(2)}, u32[]{:S(2)}) collective-permute-start(bf16[256,256]{1,0:T(8,128)(2,1)S(1)} %copy-done.10), channel_id=1, source_target_pairs={{0,3},{1,4},{2,5},{3,6},{4,7},{5,8},{6,9},{7,10},{8,11},{9,12},{10... | collective-permute-start | bytes 393224 | tf_op jit(solution)/shard_map/ppermute | solution.py:187
  86.0 1.1 fusion.46
  87.2 1.6 collective-permute-start.1
  88.7 1.1 fusion.48
  89.9 3.1 %collective-permute-start.14 = (bf16[256,256]{1,0:T(8,128)(2,1)S(1)}, bf16[256,256]{1,0:T(8,128)(2,1)S(1)}, u32[]{:S(2)}, u32[]{:S(2)}) collective-permute-start(bf16[256,256]{1,0:T(8,128)(2,1)S(1)} %copy-done.10), channel_id=1, source_target_pairs={{0,15},{1,0},{2,1},{3,2},{4,3},{5,4},{6,5},{7,6},{8,7},{9,8},{10,9... | collective-permute-start | bytes 393224 | tf_op jit(solution)/shard_map/ppermute | solution.py:187
  92.9 1.1 fusion.50
  94.1 0.9 collective-permute-start.13
  95.0 1.1 fusion.52
  96.1 1.1 fusion.54
  97.3 18.4 %collective-permute-done.2 = bf16[256,256]{1,0:T(8,128)(2,1)S(1)} collective-permute-done((bf16[256,256]{1,0:T(8,128)(2,1)S(1)}, bf16[256,256]{1,0:T(8,128)(2,1)S(1)}, u32[]{:S(2)}, u32[]{:S(2)}) %collective-permute-start.2) | collective-permute-done | bytes 131104 | tf_op jit(solution)/shard_map/ppermute | solution.py:187
  115.6 0.2 fusion.56
  115.9 4.0 %collective-permute-done.14 = bf16[256,256]{1,0:T(8,128)(2,1)S(1)} collective-permute-done((bf16[256,256]{1,0:T(8,128)(2,1)S(1)}, bf16[256,256]{1,0:T(8,128)(2,1)S(1)}, u32[]{:S(2)}, u32[]{:S(2)}) %collective-permute-start.14) | collective-permute-done | bytes 131104 | tf_op jit(solution)/shard_map/ppermute | solution.py:187
  119.8 0.2 fusion.32
  120.1 0.2 fusion.34
  120.4 0.4 fusion.14
  120.7 15.4 %all_to_all.54 = bf16[16,16,256]{2,1,0:T(8,128)(2,1)S(1)} all-to-all(bf16[16,16,256]{2,1,0:T(8,128)(2,1)S(1)} %bitcast.72), channel_id=1, replica_groups=mesh['ctx'=16,'ch'=16] {'ctx'}, dimensions={0} | all-to-all | bytes 262144 | tf_op jit(solution)/shard_map/all_to_all | solution.py:217
  136.1 1.2 fusion.29.grad_ref
  137.4 3.0 %shard_map.78 = f32[256,512]{1,0:T(8,128)} custom-call(f32[256,512]{1,0:T(8,128)} %get-tuple-element.8.seg_ref, f32[256,512]{1,0:T(8,128)} %fusion.29.grad_ref), custom_call_target="tpu_custom_call" | custom-call | flops 4456448 | bytes 1572864 | tf_op jit(solution)/shard_map/pallas_call | solution.py:142
  140.3 2.4 %convolution_convert_fusion.1 = bf16[256,256]{1,0:T(8,128)(2,1)} fusion(f32[256,512]{1,0:T(8,128)} %shard_map.78, f32[512,512]{0,1:T(8,128)} %maximum_bitcast_fusion), kind=kOutput, calls=%fused_computation.19 | convolution fusion | flops 402718720 | bytes 1179648 | tf_op jit(solution)/shard_map/dot_general | solution.py:163
  142.8 3.4 %all-to-all-start.4 = ((bf16[16,16,256]{2,1,0:T(8,128)(2,1)}), bf16[16,16,256]{2,1,0:T(8,128)(2,1)S(1)}, u32[]{:S(2)}, u32[]{:S(2)}) async-start(bf16[16,16,256]{2,1,0:T(8,128)(2,1)} %bitcast.17), calls=%async_computation.4 | async-start | bytes 262144 | tf_op jit(solution)/shard_map/all_to_all | solution.py:221
  146.2 2.6 %reduce = bf16[256,256]{1,0:T(8,128)(2,1)} reduce(bf16[16,256,256]{2,1,0:T(8,128)(2,1)} %bitcast.13, bf16[]{:T(256)} %constant.183), dimensions={0}, to_apply=%region_0.1.clone | reduce | flops 983040 | bytes 2228226 | tf_op jit(solution)/shard_map/reduce_sum | solution.py:228
  148.8 6.4 %all-to-all-done.4 = bf16[16,16,256]{2,1,0:T(8,128)(2,1)S(1)} async-done(((bf16[16,16,256]{2,1,0:T(8,128)(2,1)}), bf16[16,16,256]{2,1,0:T(8,128)(2,1)S(1)}, u32[]{:S(2)}, u32[]{:S(2)}) %all-to-all-start.4) | async-done | bytes 131104 | tf_op jit(solution)/shard_map/all_to_all | solution.py:221
  155.2 0.8 copy.29
  (43 shorter events, 0.2 us)
Async XLA Ops:
  0.6 26.3 %copy-start = (bf16[256,4096]{1,0:T(8,128)(2,1)S(1)}, bf16[256,4096]{1,0:T(8,128)(2,1)}, u32[]{:S(2)}) copy-start(bf16[256,4096]{1,0:T(8,128)(2,1)} %param.10) | copy-start | bytes 6291460
  0.6 26.3 %copy-start.9 = (bf16[256,256]{1,0:T(8,128)(2,1)S(1)}, bf16[256,256]{1,0:T(8,128)(2,1)}, u32[]{:S(2)}) copy-start(bf16[256,256]{1,0:T(8,128)(2,1)} %param.11) | copy-start | bytes 393220
  0.7 32.5 %collective-permute-start.12 = (bf16[256,256]{1,0:T(8,128)(2,1)}, bf16[256,256]{1,0:T(8,128)(2,1)}, u32[]{:S(2)}, u32[]{:S(2)}) collective-permute-start(bf16[256,256]{1,0:T(8,128)(2,1)} %param.11), channel_id=1, source_target_pairs={{0,13},{1,14},{2,15},{3,0},{4,1},{5,2},{6,3},{7,4},{8,5},{9,6},{10... | collective-permute-start | bytes 393224 | tf_op jit(solution)/shard_map/ppermute | solution.py:187
  5.2 32.5 %collective-permute-start.11 = (bf16[256,256]{1,0:T(8,128)(2,1)}, bf16[256,256]{1,0:T(8,128)(2,1)}, u32[]{:S(2)}, u32[]{:S(2)}) collective-permute-start(bf16[256,256]{1,0:T(8,128)(2,1)} %param.11), channel_id=1, source_target_pairs={{0,12},{1,13},{2,14},{3,15},{4,0},{5,1},{6,2},{7,3},{8,4},{9,5},{1... | collective-permute-start | bytes 393224 | tf_op jit(solution)/shard_map/ppermute | solution.py:187
  5.7 34.5 %collective-permute-start.10 = (bf16[256,256]{1,0:T(8,128)(2,1)}, bf16[256,256]{1,0:T(8,128)(2,1)}, u32[]{:S(2)}, u32[]{:S(2)}) collective-permute-start(bf16[256,256]{1,0:T(8,128)(2,1)} %param.11), channel_id=1, source_target_pairs={{0,11},{1,12},{2,13},{3,14},{4,15},{5,0},{6,1},{7,2},{8,3},{9,4},{... | collective-permute-start | bytes 393224 | tf_op jit(solution)/shard_map/ppermute | solution.py:187
  7.0 37.2 %collective-permute-start.9 = (bf16[256,256]{1,0:T(8,128)(2,1)}, bf16[256,256]{1,0:T(8,128)(2,1)}, u32[]{:S(2)}, u32[]{:S(2)}) collective-permute-start(bf16[256,256]{1,0:T(8,128)(2,1)} %param.11), channel_id=1, source_target_pairs={{0,10},{1,11},{2,12},{3,13},{4,14},{5,15},{6,0},{7,1},{8,2},{9,3},... | collective-permute-start | bytes 393224 | tf_op jit(solution)/shard_map/ppermute | solution.py:187
  10.9 52.9 %collective-permute-start.8 = (bf16[256,256]{1,0:T(8,128)(2,1)}, bf16[256,256]{1,0:T(8,128)(2,1)}, u32[]{:S(2)}, u32[]{:S(2)}) collective-permute-start(bf16[256,256]{1,0:T(8,128)(2,1)} %param.11), channel_id=1, source_target_pairs={{0,9},{1,10},{2,11},{3,12},{4,13},{5,14},{6,15},{7,0},{8,1},{9,2},... | collective-permute-start | bytes 393224 | tf_op jit(solution)/shard_map/ppermute | solution.py:187
  12.3 2.1 %copy-start.1 = (bf16[256,256]{0,1:T(8,128)(2,1)}, bf16[256,256]{0,1:T(8,128)(2,1)S(1)}, u32[]{:S(2)}) copy-start(bf16[256,256]{0,1:T(8,128)(2,1)S(1)} %copy.22) | copy-start | bytes 393220
  14.4 32.0 %all-to-all-start = ((bf16[2,256,256]{2,0,1:T(2,128)(2,1)}), bf16[2,256,256]{2,0,1:T(2,128)(2,1)S(1)}, u32[]{:S(2)}, u32[]{:S(2)}) async-start(bf16[2,256,256]{2,0,1:T(2,128)(2,1)} %copy.24), calls=%async_computation | async-start | bytes 524288 | tf_op jit(solution)/shard_map/all_to_all | solution.py:177
  24.9 6.1 %copy-start.11 = (bf16[256,256]{1,0:T(8,128)(2,1)S(1)}, bf16[256,256]{1,0:T(8,128)(2,1)}, u32[]{:S(2)}) copy-start(bf16[256,256]{1,0:T(8,128)(2,1)} %param.7) | copy-start | bytes 393220
  33.2 50.3 %collective-permute-start.7 = (bf16[256,256]{1,0:T(8,128)(2,1)}, bf16[256,256]{1,0:T(8,128)(2,1)}, u32[]{:S(2)}, u32[]{:S(2)}) collective-permute-start(bf16[256,256]{1,0:T(8,128)(2,1)} %param.11), channel_id=1, source_target_pairs={{0,8},{1,9},{2,10},{3,11},{4,12},{5,13},{6,14},{7,15},{8,0},{9,1},... | collective-permute-start | bytes 393224 | tf_op jit(solution)/shard_map/ppermute | solution.py:187
  37.7 49.5 %collective-permute-start.6 = (bf16[256,256]{1,0:T(8,128)(2,1)}, bf16[256,256]{1,0:T(8,128)(2,1)}, u32[]{:S(2)}, u32[]{:S(2)}) collective-permute-start(bf16[256,256]{1,0:T(8,128)(2,1)} %param.11), channel_id=1, source_target_pairs={{0,7},{1,8},{2,9},{3,10},{4,11},{5,12},{6,13},{7,14},{8,15},{9,0},... | collective-permute-start | bytes 393224 | tf_op jit(solution)/shard_map/ppermute | solution.py:187
  40.2 49.7 %collective-permute-start.5 = (bf16[256,256]{1,0:T(8,128)(2,1)}, bf16[256,256]{1,0:T(8,128)(2,1)}, u32[]{:S(2)}, u32[]{:S(2)}) collective-permute-start(bf16[256,256]{1,0:T(8,128)(2,1)} %param.11), channel_id=1, source_target_pairs={{0,6},{1,7},{2,8},{3,9},{4,10},{5,11},{6,12},{7,13},{8,14},{9,15},... | collective-permute-start | bytes 393224 | tf_op jit(solution)/shard_map/ppermute | solution.py:187
  44.3 49.8 %collective-permute-start.4 = (bf16[256,256]{1,0:T(8,128)(2,1)}, bf16[256,256]{1,0:T(8,128)(2,1)}, u32[]{:S(2)}, u32[]{:S(2)}) collective-permute-start(bf16[256,256]{1,0:T(8,128)(2,1)} %param.11), channel_id=1, source_target_pairs={{0,5},{1,6},{2,7},{3,8},{4,9},{5,10},{6,11},{7,12},{8,13},{9,14},{... | collective-permute-start | bytes 393224 | tf_op jit(solution)/shard_map/ppermute | solution.py:187
  50.4 24.5 %copy-start.2 = (bf16[256,256]{0,1:T(8,128)(2,1)S(1)}, bf16[256,256]{0,1:T(8,128)(2,1)}, u32[]{:S(2)}) copy-start(bf16[256,256]{0,1:T(8,128)(2,1)} %copy-done.1) | copy-start | bytes 393220
  50.4 24.5 %copy-start.12 = (f32[256]{0:T(256)S(1)}, f32[256]{0:T(256)}, u32[]{:S(2)}) copy-start(f32[256]{0:T(256)} %param.9) | copy-start | bytes 3076
  55.8 19.2 %all-to-all-start.1 = ((bf16[16,16,256]{2,1,0:T(8,128)(2,1)}), bf16[16,16,256]{2,1,0:T(8,128)(2,1)S(1)}, u32[]{:S(2)}, u32[]{:S(2)}) async-start(bf16[16,16,256]{2,1,0:T(8,128)(2,1)} %bitcast.71), calls=%async_computation.1 | async-start | bytes 262144 | tf_op jit(solution)/shard_map/all_to_all | solution.py:208
  63.8 8.6 %collective-permute-start = (bf16[256,256]{1,0:T(8,128)(2,1)}, bf16[256,256]{1,0:T(8,128)(2,1)S(1)}, u32[]{:S(2)}, u32[]{:S(2)}) collective-permute-start(bf16[256,256]{1,0:T(8,128)(2,1)} %param.11), channel_id=1, source_target_pairs={{0,1},{1,2},{2,3},{3,4},{4,5},{5,6},{6,7},{7,8},{8,9},{9,10},{10,1... | collective-permute-start | bytes 393224 | tf_op jit(solution)/shard_map/ppermute | solution.py:187
  72.4 23.7 %collective-permute-start.3 = (bf16[256,256]{1,0:T(8,128)(2,1)}, bf16[256,256]{1,0:T(8,128)(2,1)}, u32[]{:S(2)}, u32[]{:S(2)}) collective-permute-start(bf16[256,256]{1,0:T(8,128)(2,1)} %param.11), channel_id=1, source_target_pairs={{0,4},{1,5},{2,6},{3,7},{4,8},{5,9},{6,10},{7,11},{8,12},{9,13},{1... | collective-permute-start | bytes 393224 | tf_op jit(solution)/shard_map/ppermute | solution.py:187
  77.3 6.1 %copy-start.10 = (bf16[256,256]{1,0:T(8,128)(2,1)S(1)}, bf16[256,256]{1,0:T(8,128)(2,1)}, u32[]{:S(2)}) copy-start(bf16[256,256]{1,0:T(8,128)(2,1)} %param.11) | copy-start | bytes 393220
  77.3 43.4 %all-to-all-start.2 = ((bf16[256,16,256]{2,0,1:T(8,128)(2,1)}), bf16[256,16,256]{2,0,1:T(8,128)(2,1)}, u32[]{:S(2)}, u32[]{:S(2)}) async-start(bf16[256,16,256]{2,0,1:T(8,128)(2,1)} %bitcast.67), calls=%async_computation.2 | async-start | bytes 4194304 | tf_op jit(solution)/shard_map/all_to_all | solution.py:215
  83.4 36.9 %copy-start.3 = (f32[256,256]{1,0:T(8,128)S(1)}, f32[256,256]{1,0:T(8,128)}, u32[]{:S(2)}) copy-start(f32[256,256]{1,0:T(8,128)} %fusion.36) | copy-start | bytes 786436
  83.4 36.9 %copy-start.4 = (f32[256,256]{1,0:T(8,128)S(1)}, f32[256,256]{1,0:T(8,128)}, u32[]{:S(2)}) copy-start(f32[256,256]{1,0:T(8,128)} %fusion.38) | copy-start | bytes 786436
  83.4 36.9 %copy-start.5 = (f32[256,256]{1,0:T(8,128)S(1)}, f32[256,256]{1,0:T(8,128)}, u32[]{:S(2)}) copy-start(f32[256,256]{1,0:T(8,128)} %fusion.40) | copy-start | bytes 786436
  83.4 36.9 %copy-start.6 = (f32[256,256]{1,0:T(8,128)S(1)}, f32[256,256]{1,0:T(8,128)}, u32[]{:S(2)}) copy-start(f32[256,256]{1,0:T(8,128)} %fusion.42) | copy-start | bytes 786436
  83.4 36.9 %copy-start.7 = (f32[256,256]{1,0:T(8,128)S(1)}, f32[256,256]{1,0:T(8,128)}, u32[]{:S(2)}) copy-start(f32[256,256]{1,0:T(8,128)} %fusion.44) | copy-start | bytes 786436
  83.4 36.9 %copy-start.8 = (f32[256,256]{1,0:T(8,128)S(1)}, f32[256,256]{1,0:T(8,128)}, u32[]{:S(2)}) copy-start(f32[256,256]{1,0:T(8,128)} %convolution_add_fusion.1) | copy-start | bytes 786436
  83.4 32.2 %collective-permute-start.2 = (bf16[256,256]{1,0:T(8,128)(2,1)S(1)}, bf16[256,256]{1,0:T(8,128)(2,1)S(1)}, u32[]{:S(2)}, u32[]{:S(2)}) collective-permute-start(bf16[256,256]{1,0:T(8,128)(2,1)S(1)} %copy-done.10), channel_id=1, source_target_pairs={{0,3},{1,4},{2,5},{3,6},{4,7},{5,8},{6,9},{7,10},{8,11},{9,12},{10... | collective-permute-start | bytes 393224 | tf_op jit(solution)/shard_map/ppermute | solution.py:187
  87.2 33.1 %collective-permute-start.1 = (bf16[256,256]{1,0:T(8,128)(2,1)S(1)}, bf16[256,256]{1,0:T(8,128)(2,1)S(1)}, u32[]{:S(2)}, u32[]{:S(2)}) collective-permute-start(bf16[256,256]{1,0:T(8,128)(2,1)S(1)} %copy-done.10), channel_id=1, source_target_pairs={{0,2},{1,3},{2,4},{3,5},{4,6},{5,7},{6,8},{7,9},{8,10},{9,11},{10,... | collective-permute-start | bytes 393224 | tf_op jit(solution)/shard_map/ppermute | solution.py:187
  89.9 30.0 %collective-permute-start.14 = (bf16[256,256]{1,0:T(8,128)(2,1)S(1)}, bf16[256,256]{1,0:T(8,128)(2,1)S(1)}, u32[]{:S(2)}, u32[]{:S(2)}) collective-permute-start(bf16[256,256]{1,0:T(8,128)(2,1)S(1)} %copy-done.10), channel_id=1, source_target_pairs={{0,15},{1,0},{2,1},{3,2},{4,3},{5,4},{6,5},{7,6},{8,7},{9,8},{10,9... | collective-permute-start | bytes 393224 | tf_op jit(solution)/shard_map/ppermute | solution.py:187
  94.1 26.0 %collective-permute-start.13 = (bf16[256,256]{1,0:T(8,128)(2,1)S(1)}, bf16[256,256]{1,0:T(8,128)(2,1)S(1)}, u32[]{:S(2)}, u32[]{:S(2)}) collective-permute-start(bf16[256,256]{1,0:T(8,128)(2,1)S(1)} %copy-done.10), channel_id=1, source_target_pairs={{0,14},{1,15},{2,0},{3,1},{4,2},{5,3},{6,4},{7,5},{8,6},{9,7},{10,... | collective-permute-start | bytes 393224 | tf_op jit(solution)/shard_map/ppermute | solution.py:187
  142.8 12.4 %all-to-all-start.4 = ((bf16[16,16,256]{2,1,0:T(8,128)(2,1)}), bf16[16,16,256]{2,1,0:T(8,128)(2,1)S(1)}, u32[]{:S(2)}, u32[]{:S(2)}) async-start(bf16[16,16,256]{2,1,0:T(8,128)(2,1)} %bitcast.17), calls=%async_computation.4 | async-start | bytes 262144 | tf_op jit(solution)/shard_map/all_to_all | solution.py:221

commit v11 on v9

--- a/solution.py
+++ b/solution.py
@@ -177,8 +177,10 @@
     pair_t = lax.all_to_all(pair, "ctx", 1, 1, tiled=True)
     signal_t, taps_t = pair_t[0], pair_t[1]
 
-    ch_count = lax.axis_size("ch")
-    cot_rows = lax.all_gather(cotangent, "ch", axis=1, tiled=True)
+    ch_count = lax.axis_size(("chy", "chx"))
+    cot_rows = lax.all_gather(
+        lax.all_gather(cotangent, "chx", axis=1, tiled=True), "chy", axis=1, tiled=True
+    )
     upstream = lax.dot_general(
         cot_rows,
         w_out,
@@ -203,7 +205,7 @@
     mixed_sum = convolved + skip_gain[None, :] * inputs.astype(jnp.float32)
     gated_rows = (gate_wide * mixed_sum).astype(jnp.bfloat16)
     partial_out = jnp.dot(gated_rows, w_out, preferred_element_type=jnp.float32)
-    pieces = lax.all_to_all(partial_out.astype(jnp.bfloat16), "ch", 1, 0, tiled=True)
+    pieces = lax.all_to_all(partial_out.astype(jnp.bfloat16), ("chy", "chx"), 1, 0, tiled=True)
     pieces, grad_mixed = lax.optimization_barrier((pieces, grad_mixed))
     grad_t = lax.all_to_all(grad_mixed.T.astype(jnp.bfloat16), "ctx", 0, 0, tiled=True)
 
@@ -223,17 +225,22 @@
 
 
 def solution(mesh):
+    ch_y = mesh.shape["ch"] // 4
+    split_mesh = jax.sharding.Mesh(
+        mesh.devices.reshape(mesh.shape["ctx"], ch_y, 4), ("ctx", "chy", "chx")
+    )
+    ch = ("chy", "chx")
     return jax.shard_map(
         body,
-        mesh=mesh,
+        mesh=split_mesh,
         in_specs=(
-            P("ctx", "ch"),
-            P("ctx", "ch"),
-            P("ctx", "ch"),
-            P("ch"),
-            P("ch", None),
-            P("ctx", "ch"),
+            P("ctx", ch),
+            P("ctx", ch),
+            P("ctx", ch),
+            P(ch),
+            P(ch, None),
+            P("ctx", ch),
         ),
-        out_specs=(P("ctx", "ch"), P("ctx", "ch")),
+        out_specs=(P("ctx", ch), P("ctx", ch)),
         check_vma=False,
     )

time: 145 us -> 151 us (1.041)
  blocking collectives: 27 us -> 42.4 us
  waiting for transfers between devices: 46.2 us -> 37.2 us
    all_gather x1, waiting for transfers between devices: 30.6 us -> 0.02 us  [body(): lax.all_gather(lax.all_gather(cotangent, 'chx', axis=1, tiled=True), 'chy...]
    all_to_all x1, waiting for transfers between devices: 4.78 us -> 31.2 us  [body(): lax.all_to_all(partial_out.astype(jnp.bfloat16), ('chy', 'chx'), 1, 0, ti...]
    all_gather x0 -> x1, blocking collectives: none -> 11.6 us  [body(): lax.all_gather(cotangent, 'chx', axis=1, tiled=True)]
    all_to_all x1, blocking collectives: 12.1 us -> 18.2 us  [body(): lax.all_to_all(convolved_t.astype(jnp.bfloat16), 'ctx', 0, 0, tiled=True)]
    all_to_all x1, waiting for transfers between devices: 3.82 us -> 0.01 us  [body(): pair_t = lax.all_to_all(pair, 'ctx', 1, 1, tiled=True)]
    all_to_all x1, blocking collectives: 15 us -> 12.6 us  [body(): lax.all_to_all(grad_mixed.T.astype(jnp.bfloat16), 'ctx', 0, 0, tiled=True)]
    unnamed x11 -> x13, local copies, waits for them, and re-layouts: 3.01 us -> 3.04 us
  transfers between devices with their start and end apart: 4 -> 4, of which waited for: 4 -> 2; matrix products, arithmetic and copies ran while one was open for 16% -> 15% of each run, Pallas kernels for 2% -> 2%
where the time goes in v11:
time: 151 us; the launch traced here: 150 us
  blocking collectives  42.4 us (28%)
  waiting for transfers between devices  37.2 us (25%)
  starting transfers between devices  20.2 us (13%)
  between operations  14.2 us (9%)
  matrix products  13.2 us (9%)
  other arithmetic  10.4 us (7%)
  local copies, waits for them, and re-layouts  7.1 us (5%)
  Pallas kernels  5.84 us (4%)
    all_to_all x1, waiting for transfers between devices, body(): lax.all_to_all(partial_out.astype(jnp.bfloat16), ('chy', 'chx'), 1, 0, ti...  31.2 us
    all_to_all x1, blocking collectives, body(): lax.all_to_all(convolved_t.astype(jnp.bfloat16), 'ctx', 0, 0, tiled=True)  18.2 us
    all_to_all x1, blocking collectives, body(): lax.all_to_all(grad_mixed.T.astype(jnp.bfloat16), 'ctx', 0, 0, tiled=True)  12.6 us
    all_gather x1, blocking collectives, body(): lax.all_gather(cotangent, 'chx', axis=1, tiled=True)  11.6 us
    all_to_all x1, starting transfers between devices, body(): pair_t = lax.all_to_all(pair, 'ctx', 1, 1, tiled=True)  9.97 us
    all_to_all x1, starting transfers between devices, body(): lax.all_to_all(partial_out.astype(jnp.bfloat16), ('chy', 'chx'), 1, 0, ti...  6.8 us
    all_to_all x1, waiting for transfers between devices, body(): lax.all_to_all(filter_grad_t.astype(jnp.bfloat16), 'ctx', 0, 0, tiled=True)  5.88 us
    dot_general x4, matrix products, transform_t(): lax.dot_general(block_rows.astype(jnp.float32), dft_table, (((1,), (1,)),...  4.96 us
  transfers between devices with their start and end apart: 4, of which 2 were waited for; matrix products, arithmetic and copies ran while one was open for 15% of the time, Pallas kernels for 2%

profile of v11, /device:TPU:1, one launch (start us, length us, event | category | flops | bytes accessed | tf_op | source)
XLA Modules:
  0.0 150.5 jit_solution(1601242333108371882)
XLA Ops:
  7.2 0.0 copy-start
  7.2 0.0 copy-start.2
  7.2 1.2 copy.21
  8.4 1.0 copy.20
  9.4 1.0 copy.22
  10.4 10.0 %all-to-all-start = ((bf16[2,256,256]{2,0,1:T(2,128)(2,1)}), bf16[2,256,256]{2,0,1:T(2,128)(2,1)S(1)}, u32[]{:S(2)}, u32[]{:S(2)}) async-start(bf16[2,256,256]{2,0,1:T(2,128)(2,1)} %copy.22), calls=%async_computation | async-start | bytes 524288 | tf_op jit(solution)/shard_map/all_to_all | solution.py:177
  20.4 0.0 all-gather.2.cloned.1.call-start
  20.4 0.0 copy-done.2
  20.4 11.6 %all_gather.6 = bf16[256,1024]{1,0:T(8,128)(2,1)} all-gather(bf16[256,256]{1,0:T(8,128)(2,1)S(1)} %copy-done.2), channel_id=1, replica_groups=mesh['ctx'=16,'chy'=4,'chx'=4] {'chx'}, dimensions={1}, use_global_device_ids=true | all-gather | bytes 655360 | tf_op jit(solution)/shard_map/all_gather | solution.py:182
  32.0 0.0 all-gather.2.cloned.1.call-update
  32.1 1.9 %fusion.11 = f32[256,512]{1,0:T(8,128)S(1)} fusion(), kind=kLoop, calls=%fused_computation.30 | loop fusion | flops 1835008 | bytes 524288 | tf_op jit(solution)/shard_map/cos | solution.py:22
  34.0 2.0 %multiply_multiply_fusion = f32[256,512]{1,0:T(8,128)S(1)} fusion(f32[256]{0:T(256)S(1)} %broadcast_select_fusion), kind=kLoop, calls=%fused_computation.19 | loop fusion | flops 2097152 | bytes 525312 | tf_op jit(solution)/shard_map/mul | solution.py:25
  36.0 2.0 %select_multiply_fusion = (f32[256,512]{1,0:T(8,128)S(1)}, f32[256,512]{1,0:T(8,128)S(1)}) fusion(f32[512]{0:T(512)S(1)} %fusion.23, pred[256]{0:T(512)(128)(4,1)S(1)} %iota_compare_fusion), kind=kLoop, calls=%fused_computation.18 | loop fusion | flops 2490368 | bytes 1050880 | tf_op jit(solution)/shard_map/mul | solution.py:26
  38.0 1.1 maximum_bitcast_fusion
  39.1 0.0 all-to-all-done
  39.1 0.4 fusion.29
  39.5 1.2 fusion.12.high_ref
  40.7 1.2 fusion.17.low_ref
  41.9 1.2 fusion.15.taps_ref
  43.2 0.0 copy-start.1
  43.2 0.0 copy-start.4
  43.2 2.9 %shard_map.77 = (f32[256,512]{1,0:T(8,128)}, f32[256,512]{1,0:T(8,128)}) custom-call(f32[256,512]{1,0:T(8,128)} %fusion.17.low_ref, f32[256,512]{1,0:T(8,128)} %fusion.12.high_ref, f32[256,512]{1,0:T(8,128)} %fusion.15.taps_ref), custom_call_target="tpu_custom_call" | custom-call | flops 4456448 | bytes 2621440 | tf_op jit(solution)/shard_map/pallas_call | solution.py:125
  46.1 1.8 %convolution_convert_fusion.2 = bf16[256,256]{1,0:T(8,128)(2,1)S(1)} fusion(f32[256,512]{1,0:T(8,128)} %get-tuple-element.6, f32[512,512]{0,1:T(8,128)} %maximum_bitcast_fusion), kind=kOutput, calls=%fused_computation.4 | convolution fusion | flops 402718720 | bytes 1179648 | tf_op jit(solution)/shard_map/dot_general | solution.py:163
  47.9 18.2 %all_to_all.54 = bf16[16,16,256]{2,1,0:T(8,128)(2,1)S(1)} all-to-all(bf16[16,16,256]{2,1,0:T(8,128)(2,1)S(1)} %bitcast.51), channel_id=1, replica_groups=mesh['ctx'=16,'chy'=4,'chx'=4] {'ctx'}, dimensions={0} | all-to-all | bytes 262144 | tf_op jit(solution)/shard_map/all_to_all | solution.py:201
  66.1 0.7 bitcast_convert_fusion
  66.8 1.1 copy.25
  67.9 0.0 copy-done
  67.9 0.0 copy-done.1
  67.9 0.0 copy-done.4
  67.9 1.6 %convolution_convert_fusion = bf16[256,4096]{1,0:T(8,128)(2,1)S(1)} fusion(bf16[256,4096]{1,0:T(8,128)(2,1)S(1)} %copy-done, bf16[256,256]{1,0:T(8,128)(2,1)} %param.7, f32[256,256]{0,1:T(8,128)S(1)} %copy.25, bf16[256,256]{1,0:T(8,128)(2,1)S(1)} %copy-done.1, f32[256]{0:T(256)S(1)} %copy-done.4), kind=kOutput, calls=%fused_computation | convolution fusion | flops 538312704 | bytes 4719616 | tf_op jit(solution)/shard_map/dot_general | solution.py:207
  69.6 1.5 %copy.38 = bf16[32,16,8,256]{3,2,0,1:T(8,128)(2,1)} copy(bf16[32,16,8,256]{3,2,1,0:T(8,128)(2,1)S(1)} %bitcast.50) | data formatting | bytes 4194304 | tf_op jit(solution)/shard_map/all_to_all | solution.py:208
  71.1 0.0 copy-start.3
  71.1 6.8 %all-to-all-start.2 = ((bf16[256,16,256]{2,0,1:T(8,128)(2,1)}), bf16[256,16,256]{2,0,1:T(8,128)(2,1)}, u32[]{:S(2)}, u32[]{:S(2)}) async-start(bf16[256,16,256]{2,0,1:T(8,128)(2,1)} %bitcast.49), calls=%async_computation.2 | async-start | bytes 4194304 | tf_op jit(solution)/shard_map/all_to_all | solution.py:208
  77.9 0.0 all-gather.2.cloned.1.call-done
  77.9 0.0 copy-done.3
  78.0 2.3 %convolution_multiply_fusion = bf16[256,256]{1,0:T(8,128)(2,1)S(1)} fusion(bf16[256,4096]{1,0:T(8,128)(2,1)} %all-gather.2.cloned.1.call-done, bf16[256,4096]{1,0:T(8,128)(2,1)S(1)} %copy-done, bf16[256,256]{1,0:T(8,128)(2,1)S(1)} %copy-done.3), kind=kOutput, calls=%fused_computation.2 | convolution fusion | flops 537067520 | bytes 4456448 | tf_op jit(solution)/shard_map/dot_general | solution.py:184
  80.3 31.2 %all-to-all-done.2 = bf16[256,16,256]{2,0,1:T(8,128)(2,1)} async-done(((bf16[256,16,256]{2,0,1:T(8,128)(2,1)}), bf16[256,16,256]{2,0,1:T(8,128)(2,1)}, u32[]{:S(2)}, u32[]{:S(2)}) %all-to-all-start.2) | async-done | bytes 2097184 | tf_op jit(solution)/shard_map/all_to_all | solution.py:208
  111.5 0.1 copy.27
  111.7 12.6 %all_to_all.55 = bf16[16,16,256]{2,1,0:T(8,128)(2,1)S(1)} all-to-all(bf16[16,16,256]{2,1,0:T(8,128)(2,1)S(1)} %bitcast.52), channel_id=1, replica_groups=mesh['ctx'=16,'chy'=4,'chx'=4] {'ctx'}, dimensions={0} | all-to-all | bytes 262144 | tf_op jit(solution)/shard_map/all_to_all | solution.py:210
  124.2 1.2 fusion.13.grad_ref
  125.5 3.0 %shard_map.78 = f32[256,512]{1,0:T(8,128)} custom-call(f32[256,512]{1,0:T(8,128)} %get-tuple-element.8.seg_ref, f32[256,512]{1,0:T(8,128)} %fusion.13.grad_ref), custom_call_target="tpu_custom_call" | custom-call | flops 4456448 | bytes 1572864 | tf_op jit(solution)/shard_map/pallas_call | solution.py:142
  128.4 2.4 %convolution_convert_fusion.1 = bf16[256,256]{1,0:T(8,128)(2,1)} fusion(f32[256,512]{1,0:T(8,128)} %shard_map.78, f32[512,512]{0,1:T(8,128)} %maximum_bitcast_fusion), kind=kOutput, calls=%fused_computation.3 | convolution fusion | flops 402718720 | bytes 1179648 | tf_op jit(solution)/shard_map/dot_general | solution.py:163
  130.9 3.4 %all-to-all-start.4 = ((bf16[16,16,256]{2,1,0:T(8,128)(2,1)}), bf16[16,16,256]{2,1,0:T(8,128)(2,1)S(1)}, u32[]{:S(2)}, u32[]{:S(2)}) async-start(bf16[16,16,256]{2,1,0:T(8,128)(2,1)} %bitcast.16), calls=%async_computation.4 | async-start | bytes 262144 | tf_op jit(solution)/shard_map/all_to_all | solution.py:214
  134.3 2.6 %reduce = bf16[256,256]{1,0:T(8,128)(2,1)} reduce(bf16[16,256,256]{2,1,0:T(8,128)(2,1)} %bitcast.12, bf16[]{:T(256)} %constant.46), dimensions={0}, to_apply=%region_0.1.clone | reduce | flops 983040 | bytes 2228226 | tf_op jit(solution)/shard_map/reduce_sum | solution.py:221
  136.9 5.9 %all-to-all-done.4 = bf16[16,16,256]{2,1,0:T(8,128)(2,1)S(1)} async-done(((bf16[16,16,256]{2,1,0:T(8,128)(2,1)}), bf16[16,16,256]{2,1,0:T(8,128)(2,1)S(1)}, u32[]{:S(2)}, u32[]{:S(2)}) %all-to-all-start.4) | async-done | bytes 131104 | tf_op jit(solution)/shard_map/all_to_all | solution.py:214
  142.8 0.8 copy.28
  (5 shorter events, 0.1 us)
Async XLA Ops:
  7.2 60.7 %copy-start = (bf16[256,4096]{1,0:T(8,128)(2,1)S(1)}, bf16[256,4096]{1,0:T(8,128)(2,1)}, u32[]{:S(2)}) copy-start(bf16[256,4096]{1,0:T(8,128)(2,1)} %param.10) | copy-start | bytes 6291460
  7.2 13.2 %copy-start.2 = (bf16[256,256]{1,0:T(8,128)(2,1)S(1)}, bf16[256,256]{1,0:T(8,128)(2,1)}, u32[]{:S(2)}) copy-start(bf16[256,256]{1,0:T(8,128)(2,1)} %param.11) | copy-start | bytes 393220
  10.4 28.7 %all-to-all-start = ((bf16[2,256,256]{2,0,1:T(2,128)(2,1)}), bf16[2,256,256]{2,0,1:T(2,128)(2,1)S(1)}, u32[]{:S(2)}, u32[]{:S(2)}) async-start(bf16[2,256,256]{2,0,1:T(2,128)(2,1)} %copy.22), calls=%async_computation | async-start | bytes 524288 | tf_op jit(solution)/shard_map/all_to_all | solution.py:177
  20.4 57.6 %all-gather.2.cloned.1.call-start = ((), (), s32[]{:S(2)}) async-start(), calls=%async_computation.5 | async-start | bytes 2621440 | tf_op jit(solution)/shard_map/all_gather | solution.py:181
  43.2 24.7 %copy-start.1 = (bf16[256,256]{1,0:T(8,128)(2,1)S(1)}, bf16[256,256]{1,0:T(8,128)(2,1)}, u32[]{:S(2)}) copy-start(bf16[256,256]{1,0:T(8,128)(2,1)} %param.6) | copy-start | bytes 393220
  43.2 24.7 %copy-start.4 = (f32[256]{0:T(256)S(1)}, f32[256]{0:T(256)}, u32[]{:S(2)}) copy-start(f32[256]{0:T(256)} %param.9) | copy-start | bytes 3076
  71.1 6.8 %copy-start.3 = (bf16[256,256]{1,0:T(8,128)(2,1)S(1)}, bf16[256,256]{1,0:T(8,128)(2,1)}, u32[]{:S(2)}) copy-start(bf16[256,256]{1,0:T(8,128)(2,1)} %param.7) | copy-start | bytes 393220
  71.1 40.4 %all-to-all-start.2 = ((bf16[256,16,256]{2,0,1:T(8,128)(2,1)}), bf16[256,16,256]{2,0,1:T(8,128)(2,1)}, u32[]{:S(2)}, u32[]{:S(2)}) async-start(bf16[256,16,256]{2,0,1:T(8,128)(2,1)} %bitcast.49), calls=%async_computation.2 | async-start | bytes 4194304 | tf_op jit(solution)/shard_map/all_to_all | solution.py:208
  130.9 11.9 %all-to-all-start.4 = ((bf16[16,16,256]{2,1,0:T(8,128)(2,1)}), bf16[16,16,256]{2,1,0:T(8,128)(2,1)S(1)}, u32[]{:S(2)}, u32[]{:S(2)}) async-start(bf16[16,16,256]{2,1,0:T(8,128)(2,1)} %bitcast.16), calls=%async_computation.4 | async-start | bytes 262144 | tf_op jit(solution)/shard_map/all_to_all | solution.py:214
Sparse Core Ops, SparseCore 0:
  32.2 36.2 all-gather.1

commit v12 on v9

--- a/solution.py
+++ b/solution.py
@@ -173,9 +173,9 @@
     first_half = forward[:, :block_len]
     second_half = forward[:, block_len:]
 
-    pair = jnp.stack([inputs.T, filter_taps.T])
-    pair_t = lax.all_to_all(pair, "ctx", 1, 1, tiled=True)
-    signal_t, taps_t = pair_t[0], pair_t[1]
+    pair = jnp.concatenate([inputs.T, filter_taps.T], axis=1)
+    pair_t = lax.all_to_all(pair, "ctx", 0, 0, tiled=True)
+    signal_t, taps_t = pair_t[:, :block_len], pair_t[:, block_len:]
 
     ch_count = lax.axis_size("ch")
     cot_rows = lax.all_gather(cotangent, "ch", axis=1, tiled=True)

time: 145 us -> 145 us (level)
    all_to_all x1, waiting for transfers between devices: 4.78 us -> 3.2 us  [body(): lax.all_to_all(partial_out.astype(jnp.bfloat16), 'ch', 1, 0, tiled=True)]
where the time goes in v12:
time: 145 us; the launch traced here: 144 us
  waiting for transfers between devices  46 us (32%)
  blocking collectives  27.6 us (19%)
  starting transfers between devices  20.3 us (14%)
  between operations  14.2 us (10%)
  matrix products  13.2 us (9%)
  other arithmetic  11 us (8%)
  Pallas kernels  5.87 us (4%)
  local copies, waits for them, and re-layouts  5.72 us (4%)
    all_gather x1, waiting for transfers between devices, body(): cot_rows = lax.all_gather(cotangent, 'ch', axis=1, tiled=True)  31.9 us
    all_to_all x1, blocking collectives, body(): lax.all_to_all(grad_mixed.T.astype(jnp.bfloat16), 'ctx', 0, 0, tiled=True)  15.6 us
    all_to_all x1, blocking collectives, body(): lax.all_to_all(convolved_t.astype(jnp.bfloat16), 'ctx', 0, 0, tiled=True)  12 us
    all_to_all x1, starting transfers between devices, body(): pair_t = lax.all_to_all(pair, 'ctx', 0, 0, tiled=True)  9.97 us
    all_to_all x1, starting transfers between devices, body(): lax.all_to_all(partial_out.astype(jnp.bfloat16), 'ch', 1, 0, tiled=True)  6.93 us
    all_to_all x1, waiting for transfers between devices, body(): lax.all_to_all(filter_grad_t.astype(jnp.bfloat16), 'ctx', 0, 0, tiled=True)  6.37 us
    dot_general x4, matrix products, transform_t(): lax.dot_general(block_rows.astype(jnp.float32), dft_table, (((1,), (1,)),...  5 us
    dot_general x2, matrix products, inverse_t(): lax.dot_general(spec_t, inverse_rows, (((1,), (1,)), ((), ())), precision...  4.24 us
  transfers between devices with their start and end apart: 4, of which 4 were waited for; matrix products, arithmetic and copies ran while one was open for 16% of the time, Pallas kernels for 2%

profile of v12, /device:TPU:1, one launch (start us, length us, event | category | flops | bytes accessed | tf_op | source)
XLA Modules:
  0.0 144.0 jit_solution(4317595484577024888)
XLA Ops:
  7.2 0.0 copy-start
  7.2 1.2 copy.10
  8.3 1.0 copy.11
  9.3 0.7 pad_maximum_fusion.1
  10.1 10.0 %all-to-all-start = ((bf16[16,16,512]{2,1,0:T(8,128)(2,1)}), bf16[16,16,512]{2,1,0:T(8,128)(2,1)S(1)}, u32[]{:S(2)}, u32[]{:S(2)}) async-start(bf16[16,16,512]{2,1,0:T(8,128)(2,1)} %bitcast.2), calls=%async_computation | async-start | bytes 524288 | tf_op jit(solution)/shard_map/all_to_all | solution.py:177
  20.0 0.0 all-gather.2.cloned.1.call-start
  20.1 0.7 all-gather.2.cloned.1.call-update
  20.8 1.9 %fusion.11 = f32[256,512]{1,0:T(8,128)S(1)} fusion(), kind=kLoop, calls=%fused_computation.30 | loop fusion | flops 1835008 | bytes 524288 | tf_op jit(solution)/shard_map/cos | solution.py:22
  22.7 2.0 %multiply_multiply_fusion = f32[256,512]{1,0:T(8,128)S(1)} fusion(f32[256]{0:T(256)S(1)} %broadcast_select_fusion), kind=kLoop, calls=%fused_computation.19 | loop fusion | flops 2097152 | bytes 525312 | tf_op jit(solution)/shard_map/mul | solution.py:25
  24.7 2.0 %select_multiply_fusion = (f32[256,512]{1,0:T(8,128)S(1)}, f32[256,512]{1,0:T(8,128)S(1)}) fusion(f32[512]{0:T(512)S(1)} %fusion.26, pred[256]{0:T(512)(128)(4,1)S(1)} %iota_compare_fusion), kind=kLoop, calls=%fused_computation.18 | loop fusion | flops 2490368 | bytes 1050880 | tf_op jit(solution)/shard_map/mul | solution.py:26
  26.7 1.1 maximum_bitcast_fusion
  27.8 3.8 %all-to-all-done = bf16[16,16,512]{2,1,0:T(8,128)(2,1)S(1)} async-done(((bf16[16,16,512]{2,1,0:T(8,128)(2,1)}), bf16[16,16,512]{2,1,0:T(8,128)(2,1)S(1)}, u32[]{:S(2)}, u32[]{:S(2)}) %all-to-all-start) | async-done | bytes 262176 | tf_op jit(solution)/shard_map/all_to_all | solution.py:177
  31.6 1.3 fusion.12.high_ref
  32.9 1.3 fusion.15.taps_ref
  34.1 1.2 fusion.19.low_ref
  35.4 0.0 copy-start.1
  35.4 0.0 copy-start.3
  35.4 2.9 %shard_map.77 = (f32[256,512]{1,0:T(8,128)}, f32[256,512]{1,0:T(8,128)}) custom-call(f32[256,512]{1,0:T(8,128)} %fusion.19.low_ref, f32[256,512]{1,0:T(8,128)} %fusion.12.high_ref, f32[256,512]{1,0:T(8,128)} %fusion.15.taps_ref), custom_call_target="tpu_custom_call" | custom-call | flops 4456448 | bytes 2621440 | tf_op jit(solution)/shard_map/pallas_call | solution.py:125
  38.3 1.8 %convolution_convert_fusion.2 = bf16[256,256]{1,0:T(8,128)(2,1)S(1)} fusion(f32[256,512]{1,0:T(8,128)} %get-tuple-element.6, f32[512,512]{0,1:T(8,128)} %maximum_bitcast_fusion), kind=kOutput, calls=%fused_computation.4 | convolution fusion | flops 402718720 | bytes 1179648 | tf_op jit(solution)/shard_map/dot_general | solution.py:163
  40.1 12.0 %all_to_all.61 = bf16[16,16,256]{2,1,0:T(8,128)(2,1)S(1)} all-to-all(bf16[16,16,256]{2,1,0:T(8,128)(2,1)S(1)} %bitcast.45), channel_id=1, replica_groups=mesh['ctx'=16,'ch'=16] {'ctx'}, dimensions={0} | all-to-all | bytes 262144 | tf_op jit(solution)/shard_map/all_to_all | solution.py:199
  52.1 0.7 bitcast_convert_fusion
  52.9 1.1 copy.12
  54.0 0.0 copy-done
  54.0 0.0 copy-done.1
  54.0 0.0 copy-done.3
  54.0 1.6 %convolution_convert_fusion = bf16[256,4096]{1,0:T(8,128)(2,1)S(1)} fusion(bf16[256,4096]{1,0:T(8,128)(2,1)S(1)} %copy-done, bf16[256,256]{1,0:T(8,128)(2,1)} %param.7, f32[256,256]{0,1:T(8,128)S(1)} %copy.12, bf16[256,256]{1,0:T(8,128)(2,1)S(1)} %copy-done.1, f32[256]{0:T(256)S(1)} %copy-done.3), kind=kOutput, calls=%fused_computation | convolution fusion | flops 538312704 | bytes 4719616 | tf_op jit(solution)/shard_map/dot_general | solution.py:205
  55.6 1.5 %copy.18 = bf16[32,16,8,256]{3,2,0,1:T(8,128)(2,1)} copy(bf16[32,16,8,256]{3,2,1,0:T(8,128)(2,1)S(1)} %bitcast.41) | data formatting | bytes 4194304 | tf_op jit(solution)/shard_map/all_to_all | solution.py:206
  57.1 0.0 copy-start.2
  57.1 6.9 %all-to-all-start.2 = ((bf16[256,16,256]{2,0,1:T(8,128)(2,1)}), bf16[256,16,256]{2,0,1:T(8,128)(2,1)}, u32[]{:S(2)}, u32[]{:S(2)}) async-start(bf16[256,16,256]{2,0,1:T(8,128)(2,1)} %bitcast.40), calls=%async_computation.2 | async-start | bytes 4194304 | tf_op jit(solution)/shard_map/all_to_all | solution.py:206
  64.1 31.9 %all-gather.2.cloned.1.call-done = bf16[256,4096]{1,0:T(8,128)(2,1)} async-done(((bf16[256,256]{1,0:T(8,128)(2,1)}), bf16[256,4096]{1,0:T(8,128)(2,1)}) %all-gather.2.cloned.1.call-update) | async-done | bytes 2097168 | tf_op jit(solution)/shard_map/all_gather | solution.py:181
  96.0 0.0 copy-done.2
  96.0 2.3 %convolution_multiply_fusion = bf16[256,256]{1,0:T(8,128)(2,1)S(1)} fusion(bf16[256,4096]{1,0:T(8,128)(2,1)} %all-gather.2.cloned.1.call-done, bf16[256,4096]{1,0:T(8,128)(2,1)S(1)} %copy-done, bf16[256,256]{1,0:T(8,128)(2,1)S(1)} %copy-done.2), kind=kOutput, calls=%fused_computation.2 | convolution fusion | flops 537067520 | bytes 4456448 | tf_op jit(solution)/shard_map/dot_general | solution.py:182
  98.4 3.2 %all-to-all-done.2 = bf16[256,16,256]{2,0,1:T(8,128)(2,1)} async-done(((bf16[256,16,256]{2,0,1:T(8,128)(2,1)}), bf16[256,16,256]{2,0,1:T(8,128)(2,1)}, u32[]{:S(2)}, u32[]{:S(2)}) %all-to-all-start.2) | async-done | bytes 2097184 | tf_op jit(solution)/shard_map/all_to_all | solution.py:206
  101.6 0.1 copy.14
  101.7 15.6 %all_to_all.62 = bf16[16,16,256]{2,1,0:T(8,128)(2,1)S(1)} all-to-all(bf16[16,16,256]{2,1,0:T(8,128)(2,1)S(1)} %bitcast.46), channel_id=1, replica_groups=mesh['ctx'=16,'ch'=16] {'ctx'}, dimensions={0} | all-to-all | bytes 262144 | tf_op jit(solution)/shard_map/all_to_all | solution.py:208
  117.2 1.2 fusion.13.grad_ref
  118.5 3.0 %shard_map.78 = f32[256,512]{1,0:T(8,128)} custom-call(f32[256,512]{1,0:T(8,128)} %get-tuple-element.8.seg_ref, f32[256,512]{1,0:T(8,128)} %fusion.13.grad_ref), custom_call_target="tpu_custom_call" | custom-call | flops 4456448 | bytes 1572864 | tf_op jit(solution)/shard_map/pallas_call | solution.py:142
  121.4 2.4 %convolution_convert_fusion.1 = bf16[256,256]{1,0:T(8,128)(2,1)} fusion(f32[256,512]{1,0:T(8,128)} %shard_map.78, f32[512,512]{0,1:T(8,128)} %maximum_bitcast_fusion), kind=kOutput, calls=%fused_computation.3 | convolution fusion | flops 402718720 | bytes 1179648 | tf_op jit(solution)/shard_map/dot_general | solution.py:163
  123.9 3.4 %all-to-all-start.4 = ((bf16[16,16,256]{2,1,0:T(8,128)(2,1)}), bf16[16,16,256]{2,1,0:T(8,128)(2,1)S(1)}, u32[]{:S(2)}, u32[]{:S(2)}) async-start(bf16[16,16,256]{2,1,0:T(8,128)(2,1)} %bitcast.14), calls=%async_computation.4 | async-start | bytes 262144 | tf_op jit(solution)/shard_map/all_to_all | solution.py:212
  127.3 2.6 %reduce = bf16[256,256]{1,0:T(8,128)(2,1)} reduce(bf16[16,256,256]{2,1,0:T(8,128)(2,1)} %bitcast.10, bf16[]{:T(256)} %constant.46), dimensions={0}, to_apply=%region_0.1.clone | reduce | flops 983040 | bytes 2228226 | tf_op jit(solution)/shard_map/reduce_sum | solution.py:219
  129.9 6.4 %all-to-all-done.4 = bf16[16,16,256]{2,1,0:T(8,128)(2,1)S(1)} async-done(((bf16[16,16,256]{2,1,0:T(8,128)(2,1)}), bf16[16,16,256]{2,1,0:T(8,128)(2,1)S(1)}, u32[]{:S(2)}, u32[]{:S(2)}) %all-to-all-start.4) | async-done | bytes 131104 | tf_op jit(solution)/shard_map/all_to_all | solution.py:212
  136.3 0.8 copy.15
  (4 shorter events, 0.0 us)
Async XLA Ops:
  7.2 46.8 %copy-start = (bf16[256,4096]{1,0:T(8,128)(2,1)S(1)}, bf16[256,4096]{1,0:T(8,128)(2,1)}, u32[]{:S(2)}) copy-start(bf16[256,4096]{1,0:T(8,128)(2,1)} %param.10) | copy-start | bytes 6291460
  10.1 21.6 %all-to-all-start = ((bf16[16,16,512]{2,1,0:T(8,128)(2,1)}), bf16[16,16,512]{2,1,0:T(8,128)(2,1)S(1)}, u32[]{:S(2)}, u32[]{:S(2)}) async-start(bf16[16,16,512]{2,1,0:T(8,128)(2,1)} %bitcast.2), calls=%async_computation | async-start | bytes 524288 | tf_op jit(solution)/shard_map/all_to_all | solution.py:177
  20.0 76.0 %all-gather.2.cloned.1.call-start = ((), (), s32[]{:S(2)}) async-start(), calls=%async_computation.5 | async-start | bytes 2228224 | tf_op jit(solution)/shard_map/all_gather | solution.py:181
  35.4 18.6 %copy-start.1 = (bf16[256,256]{1,0:T(8,128)(2,1)S(1)}, bf16[256,256]{1,0:T(8,128)(2,1)}, u32[]{:S(2)}) copy-start(bf16[256,256]{1,0:T(8,128)(2,1)} %param.6) | copy-start | bytes 393220
  35.4 18.6 %copy-start.3 = (f32[256]{0:T(256)S(1)}, f32[256]{0:T(256)}, u32[]{:S(2)}) copy-start(f32[256]{0:T(256)} %param.9) | copy-start | bytes 3076
  57.1 38.9 %copy-start.2 = (bf16[256,256]{1,0:T(8,128)(2,1)S(1)}, bf16[256,256]{1,0:T(8,128)(2,1)}, u32[]{:S(2)}) copy-start(bf16[256,256]{1,0:T(8,128)(2,1)} %param.7) | copy-start | bytes 393220
  57.1 44.4 %all-to-all-start.2 = ((bf16[256,16,256]{2,0,1:T(8,128)(2,1)}), bf16[256,16,256]{2,0,1:T(8,128)(2,1)}, u32[]{:S(2)}, u32[]{:S(2)}) async-start(bf16[256,16,256]{2,0,1:T(8,128)(2,1)} %bitcast.40), calls=%async_computation.2 | async-start | bytes 4194304 | tf_op jit(solution)/shard_map/all_to_all | solution.py:206
  123.9 12.4 %all-to-all-start.4 = ((bf16[16,16,256]{2,1,0:T(8,128)(2,1)}), bf16[16,16,256]{2,1,0:T(8,128)(2,1)S(1)}, u32[]{:S(2)}, u32[]{:S(2)}) async-start(bf16[16,16,256]{2,1,0:T(8,128)(2,1)} %bitcast.14), calls=%async_computation.4 | async-start | bytes 262144 | tf_op jit(solution)/shard_map/all_to_all | solution.py:212
Sparse Core Ops, SparseCore 0:
  23.3 72.7 all-gather.1

commit v13 on v12

--- a/solution.py
+++ b/solution.py
@@ -8,7 +8,7 @@
 from jax.experimental.pallas import tpu as pltpu
 from jax.sharding import PartitionSpec as P
 
-exact_prec = lax.Precision.HIGHEST
+exact_prec = lax.Precision.HIGH
 
 
 def spectral_tables(block_len):

time: 145 us -> 144 us (level)
  transfers between devices with their start and end apart: 4 -> 4, of which waited for: 4 -> 4; matrix products, arithmetic and copies ran while one was open for 16% -> 15% of each run, Pallas kernels for 2% -> 2%
where the time goes in v13:
time: 144 us
  waiting for transfers between devices  45.7 us (32%)
  blocking collectives  28.4 us (20%)
  starting transfers between devices  20.3 us (14%)
  between operations  14.2 us (10%)
  matrix products  12.4 us (9%)
  other arithmetic  11 us (8%)
  Pallas kernels  5.87 us (4%)
  local copies, waits for them, and re-layouts  5.72 us (4%)
    all_gather x1, waiting for transfers between devices, body(): cot_rows = lax.all_gather(cotangent, 'ch', axis=1, tiled=True)  31.8 us
    all_to_all x1, blocking collectives, body(): lax.all_to_all(grad_mixed.T.astype(jnp.bfloat16), 'ctx', 0, 0, tiled=True)  16.4 us
    all_to_all x1, blocking collectives, body(): lax.all_to_all(convolved_t.astype(jnp.bfloat16), 'ctx', 0, 0, tiled=True)  12 us
    all_to_all x1, starting transfers between devices, body(): pair_t = lax.all_to_all(pair, 'ctx', 0, 0, tiled=True)  9.97 us
    all_to_all x1, starting transfers between devices, body(): lax.all_to_all(partial_out.astype(jnp.bfloat16), 'ch', 1, 0, tiled=True)  6.93 us
    all_to_all x1, waiting for transfers between devices, body(): lax.all_to_all(filter_grad_t.astype(jnp.bfloat16), 'ctx', 0, 0, tiled=True)  6.36 us
    dot_general x4, matrix products, transform_t(): lax.dot_general(block_rows.astype(jnp.float32), dft_table, (((1,), (1,)),...  4.64 us
    all_to_all x1, waiting for transfers between devices, body(): pair_t = lax.all_to_all(pair, 'ctx', 0, 0, tiled=True)  3.84 us
  transfers between devices with their start and end apart: 4, of which 4 were waited for; matrix products, arithmetic and copies ran while one was open for 15% of the time, Pallas kernels for 2%

profile of v13, /device:TPU:1, one launch (start us, length us, event | category | flops | bytes accessed | tf_op | source)
XLA Modules:
  0.0 143.7 jit_solution(18194440250726537489)
XLA Ops:
  7.2 0.0 copy-start
  7.2 1.2 copy.10
  8.3 1.0 copy.11
  9.3 0.7 pad_maximum_fusion.1
  10.1 10.0 %all-to-all-start = ((bf16[16,16,512]{2,1,0:T(8,128)(2,1)}), bf16[16,16,512]{2,1,0:T(8,128)(2,1)S(1)}, u32[]{:S(2)}, u32[]{:S(2)}) async-start(bf16[16,16,512]{2,1,0:T(8,128)(2,1)} %bitcast.2), calls=%async_computation | async-start | bytes 524288 | tf_op jit(solution)/shard_map/all_to_all | solution.py:177
  20.0 0.0 all-gather.2.cloned.1.call-start
  20.1 0.7 all-gather.2.cloned.1.call-update
  20.8 1.9 %fusion.11 = f32[256,512]{1,0:T(8,128)S(1)} fusion(), kind=kLoop, calls=%fused_computation.30 | loop fusion | flops 1835008 | bytes 524288 | tf_op jit(solution)/shard_map/cos | solution.py:22
  22.7 2.0 %multiply_multiply_fusion = f32[256,512]{1,0:T(8,128)S(1)} fusion(f32[256]{0:T(256)S(1)} %broadcast_select_fusion), kind=kLoop, calls=%fused_computation.19 | loop fusion | flops 2097152 | bytes 525312 | tf_op jit(solution)/shard_map/mul | solution.py:25
  24.7 2.0 %select_multiply_fusion = (f32[256,512]{1,0:T(8,128)S(1)}, f32[256,512]{1,0:T(8,128)S(1)}) fusion(f32[512]{0:T(512)S(1)} %fusion.26, pred[256]{0:T(512)(128)(4,1)S(1)} %iota_compare_fusion), kind=kLoop, calls=%fused_computation.18 | loop fusion | flops 2490368 | bytes 1050880 | tf_op jit(solution)/shard_map/mul | solution.py:26
  26.7 1.1 maximum_bitcast_fusion
  27.8 3.8 %all-to-all-done = bf16[16,16,512]{2,1,0:T(8,128)(2,1)S(1)} async-done(((bf16[16,16,512]{2,1,0:T(8,128)(2,1)}), bf16[16,16,512]{2,1,0:T(8,128)(2,1)S(1)}, u32[]{:S(2)}, u32[]{:S(2)}) %all-to-all-start) | async-done | bytes 262176 | tf_op jit(solution)/shard_map/all_to_all | solution.py:177
  31.6 1.2 fusion.12.high_ref
  32.8 1.2 fusion.15.taps_ref
  34.0 1.2 fusion.19.low_ref
  35.1 0.0 copy-start.1
  35.1 0.0 copy-start.3
  35.1 2.9 %shard_map.77 = (f32[256,512]{1,0:T(8,128)}, f32[256,512]{1,0:T(8,128)}) custom-call(f32[256,512]{1,0:T(8,128)} %fusion.19.low_ref, f32[256,512]{1,0:T(8,128)} %fusion.12.high_ref, f32[256,512]{1,0:T(8,128)} %fusion.15.taps_ref), custom_call_target="tpu_custom_call" | custom-call | flops 4456448 | bytes 2621440 | tf_op jit(solution)/shard_map/pallas_call | solution.py:125
  38.0 1.6 %convolution_convert_fusion.2 = bf16[256,256]{1,0:T(8,128)(2,1)S(1)} fusion(f32[256,512]{1,0:T(8,128)} %get-tuple-element.6, f32[512,512]{0,1:T(8,128)} %maximum_bitcast_fusion), kind=kOutput, calls=%fused_computation.4 | convolution fusion | flops 201392128 | bytes 1179648 | tf_op jit(solution)/shard_map/dot_general | solution.py:163
  39.6 12.0 %all_to_all.61 = bf16[16,16,256]{2,1,0:T(8,128)(2,1)S(1)} all-to-all(bf16[16,16,256]{2,1,0:T(8,128)(2,1)S(1)} %bitcast.45), channel_id=1, replica_groups=mesh['ctx'=16,'ch'=16] {'ctx'}, dimensions={0} | all-to-all | bytes 262144 | tf_op jit(solution)/shard_map/all_to_all | solution.py:199
  51.7 0.7 bitcast_convert_fusion
  52.4 1.1 copy.12
  53.5 0.0 copy-done
  53.5 0.0 copy-done.1
  53.5 0.0 copy-done.3
  53.5 1.6 %convolution_convert_fusion = bf16[256,4096]{1,0:T(8,128)(2,1)S(1)} fusion(bf16[256,4096]{1,0:T(8,128)(2,1)S(1)} %copy-done, bf16[256,256]{1,0:T(8,128)(2,1)} %param.7, f32[256,256]{0,1:T(8,128)S(1)} %copy.12, bf16[256,256]{1,0:T(8,128)(2,1)S(1)} %copy-done.1, f32[256]{0:T(256)S(1)} %copy-done.3), kind=kOutput, calls=%fused_computation | convolution fusion | flops 538312704 | bytes 4719616 | tf_op jit(solution)/shard_map/dot_general | solution.py:205
  55.1 1.5 %copy.18 = bf16[32,16,8,256]{3,2,0,1:T(8,128)(2,1)} copy(bf16[32,16,8,256]{3,2,1,0:T(8,128)(2,1)S(1)} %bitcast.41) | data formatting | bytes 4194304 | tf_op jit(solution)/shard_map/all_to_all | solution.py:206
  56.7 0.0 copy-start.2
  56.7 6.9 %all-to-all-start.2 = ((bf16[256,16,256]{2,0,1:T(8,128)(2,1)}), bf16[256,16,256]{2,0,1:T(8,128)(2,1)}, u32[]{:S(2)}, u32[]{:S(2)}) async-start(bf16[256,16,256]{2,0,1:T(8,128)(2,1)} %bitcast.40), calls=%async_computation.2 | async-start | bytes 4194304 | tf_op jit(solution)/shard_map/all_to_all | solution.py:206
  63.6 31.8 %all-gather.2.cloned.1.call-done = bf16[256,4096]{1,0:T(8,128)(2,1)} async-done(((bf16[256,256]{1,0:T(8,128)(2,1)}), bf16[256,4096]{1,0:T(8,128)(2,1)}) %all-gather.2.cloned.1.call-update) | async-done | bytes 2097168 | tf_op jit(solution)/shard_map/all_gather | solution.py:181
  95.4 0.0 copy-done.2
  95.4 2.3 %convolution_multiply_fusion = bf16[256,256]{1,0:T(8,128)(2,1)S(1)} fusion(bf16[256,4096]{1,0:T(8,128)(2,1)} %all-gather.2.cloned.1.call-done, bf16[256,4096]{1,0:T(8,128)(2,1)S(1)} %copy-done, bf16[256,256]{1,0:T(8,128)(2,1)S(1)} %copy-done.2), kind=kOutput, calls=%fused_computation.2 | convolution fusion | flops 537067520 | bytes 4456448 | tf_op jit(solution)/shard_map/dot_general | solution.py:182
  97.7 3.1 %all-to-all-done.2 = bf16[256,16,256]{2,0,1:T(8,128)(2,1)} async-done(((bf16[256,16,256]{2,0,1:T(8,128)(2,1)}), bf16[256,16,256]{2,0,1:T(8,128)(2,1)}, u32[]{:S(2)}, u32[]{:S(2)}) %all-to-all-start.2) | async-done | bytes 2097184 | tf_op jit(solution)/shard_map/all_to_all | solution.py:206
  100.8 0.1 copy.14
  100.9 16.4 %all_to_all.62 = bf16[16,16,256]{2,1,0:T(8,128)(2,1)S(1)} all-to-all(bf16[16,16,256]{2,1,0:T(8,128)(2,1)S(1)} %bitcast.46), channel_id=1, replica_groups=mesh['ctx'=16,'ch'=16] {'ctx'}, dimensions={0} | all-to-all | bytes 262144 | tf_op jit(solution)/shard_map/all_to_all | solution.py:208
  117.3 1.1 fusion.13.grad_ref
  118.4 3.0 %shard_map.78 = f32[256,512]{1,0:T(8,128)} custom-call(f32[256,512]{1,0:T(8,128)} %get-tuple-element.8.seg_ref, f32[256,512]{1,0:T(8,128)} %fusion.13.grad_ref), custom_call_target="tpu_custom_call" | custom-call | flops 4456448 | bytes 1572864 | tf_op jit(solution)/shard_map/pallas_call | solution.py:142
  121.4 2.2 %convolution_convert_fusion.1 = bf16[256,256]{1,0:T(8,128)(2,1)} fusion(f32[256,512]{1,0:T(8,128)} %shard_map.78, f32[512,512]{0,1:T(8,128)} %maximum_bitcast_fusion), kind=kOutput, calls=%fused_computation.3 | convolution fusion | flops 201392128 | bytes 1179648 | tf_op jit(solution)/shard_map/dot_general | solution.py:163
  123.6 3.4 %all-to-all-start.4 = ((bf16[16,16,256]{2,1,0:T(8,128)(2,1)}), bf16[16,16,256]{2,1,0:T(8,128)(2,1)S(1)}, u32[]{:S(2)}, u32[]{:S(2)}) async-start(bf16[16,16,256]{2,1,0:T(8,128)(2,1)} %bitcast.14), calls=%async_computation.4 | async-start | bytes 262144 | tf_op jit(solution)/shard_map/all_to_all | solution.py:212
  127.1 2.6 %reduce = bf16[256,256]{1,0:T(8,128)(2,1)} reduce(bf16[16,256,256]{2,1,0:T(8,128)(2,1)} %bitcast.10, bf16[]{:T(256)} %constant.46), dimensions={0}, to_apply=%region_0.1.clone | reduce | flops 983040 | bytes 2228226 | tf_op jit(solution)/shard_map/reduce_sum | solution.py:219
  129.6 6.4 %all-to-all-done.4 = bf16[16,16,256]{2,1,0:T(8,128)(2,1)S(1)} async-done(((bf16[16,16,256]{2,1,0:T(8,128)(2,1)}), bf16[16,16,256]{2,1,0:T(8,128)(2,1)S(1)}, u32[]{:S(2)}, u32[]{:S(2)}) %all-to-all-start.4) | async-done | bytes 131104 | tf_op jit(solution)/shard_map/all_to_all | solution.py:212
  136.0 0.8 copy.15
  (4 shorter events, 0.0 us)
Async XLA Ops:
  7.2 46.3 %copy-start = (bf16[256,4096]{1,0:T(8,128)(2,1)S(1)}, bf16[256,4096]{1,0:T(8,128)(2,1)}, u32[]{:S(2)}) copy-start(bf16[256,4096]{1,0:T(8,128)(2,1)} %param.10) | copy-start | bytes 6291460
  10.1 21.6 %all-to-all-start = ((bf16[16,16,512]{2,1,0:T(8,128)(2,1)}), bf16[16,16,512]{2,1,0:T(8,128)(2,1)S(1)}, u32[]{:S(2)}, u32[]{:S(2)}) async-start(bf16[16,16,512]{2,1,0:T(8,128)(2,1)} %bitcast.2), calls=%async_computation | async-start | bytes 524288 | tf_op jit(solution)/shard_map/all_to_all | solution.py:177
  20.0 75.4 %all-gather.2.cloned.1.call-start = ((), (), s32[]{:S(2)}) async-start(), calls=%async_computation.5 | async-start | bytes 2228224 | tf_op jit(solution)/shard_map/all_gather | solution.py:181
  35.1 18.4 %copy-start.1 = (bf16[256,256]{1,0:T(8,128)(2,1)S(1)}, bf16[256,256]{1,0:T(8,128)(2,1)}, u32[]{:S(2)}) copy-start(bf16[256,256]{1,0:T(8,128)(2,1)} %param.6) | copy-start | bytes 393220
  35.1 18.4 %copy-start.3 = (f32[256]{0:T(256)S(1)}, f32[256]{0:T(256)}, u32[]{:S(2)}) copy-start(f32[256]{0:T(256)} %param.9) | copy-start | bytes 3076
  56.7 38.7 %copy-start.2 = (bf16[256,256]{1,0:T(8,128)(2,1)S(1)}, bf16[256,256]{1,0:T(8,128)(2,1)}, u32[]{:S(2)}) copy-start(bf16[256,256]{1,0:T(8,128)(2,1)} %param.7) | copy-start | bytes 393220
  56.7 44.1 %all-to-all-start.2 = ((bf16[256,16,256]{2,0,1:T(8,128)(2,1)}), bf16[256,16,256]{2,0,1:T(8,128)(2,1)}, u32[]{:S(2)}, u32[]{:S(2)}) async-start(bf16[256,16,256]{2,0,1:T(8,128)(2,1)} %bitcast.40), calls=%async_computation.2 | async-start | bytes 4194304 | tf_op jit(solution)/shard_map/all_to_all | solution.py:206
  123.6 12.3 %all-to-all-start.4 = ((bf16[16,16,256]{2,1,0:T(8,128)(2,1)}), bf16[16,16,256]{2,1,0:T(8,128)(2,1)S(1)}, u32[]{:S(2)}, u32[]{:S(2)}) async-start(bf16[16,16,256]{2,1,0:T(8,128)(2,1)} %bitcast.14), calls=%async_computation.4 | async-start | bytes 262144 | tf_op jit(solution)/shard_map/all_to_all | solution.py:212
Sparse Core Ops, SparseCore 0:
  23.3 72.1 all-gather.1

commit v14 on v12

--- a/solution.py
+++ b/solution.py
@@ -204,7 +204,6 @@
     gated_rows = (gate_wide * mixed_sum).astype(jnp.bfloat16)
     partial_out = jnp.dot(gated_rows, w_out, preferred_element_type=jnp.float32)
     pieces = lax.all_to_all(partial_out.astype(jnp.bfloat16), "ch", 1, 0, tiled=True)
-    pieces, grad_mixed = lax.optimization_barrier((pieces, grad_mixed))
     grad_t = lax.all_to_all(grad_mixed.T.astype(jnp.bfloat16), "ctx", 0, 0, tiled=True)
 
     lag_spec = lag_products(seg_spec, transform_t(second_half, grad_t), width)

time: 145 us -> 146 us (level)
  blocking collectives: 27.6 us -> 0 us
  waiting for transfers between devices: 46 us -> 62 us
  starting transfers between devices: 20.3 us -> 32.6 us
    all_to_all x2 -> x0, blocking collectives: 27.6 us -> none  [the longest x1 15.6 us: body(): lax.all_to_all(grad_mixed.T.astype(jnp.bfloat16), 'ctx', 0, 0, tiled=True)]
    all_to_all x1, waiting for transfers between devices: 3.2 us -> 26 us  [body(): lax.all_to_all(partial_out.astype(jnp.bfloat16), 'ch', 1, 0, tiled=True)]
    all_to_all x0 -> x2, starting transfers between devices: none -> 13.6 us  [the longest x1 9.3 us: body(): lax.all_to_all(grad_mixed.T.astype(jnp.bfloat16), 'ctx', 0, 0, tiled=True)]
    all_gather x1, waiting for transfers between devices: 31.9 us -> 19 us  [body(): cot_rows = lax.all_gather(cotangent, 'ch', axis=1, tiled=True)]
    all_to_all x0 -> x2, waiting for transfers between devices: none -> 6.63 us  [the longest x1 6.63 us: body(): lax.all_to_all(grad_mixed.T.astype(jnp.bfloat16), 'ctx', 0, 0, tiled=True)]
    all_to_all x1, starting transfers between devices: 6.93 us -> 4.72 us  [body(): lax.all_to_all(partial_out.astype(jnp.bfloat16), 'ch', 1, 0, tiled=True)]
    unnamed x11 -> x10, local copies, waits for them, and re-layouts: 3.01 us -> 4.52 us
  transfers between devices with their start and end apart: 4 -> 6, of which waited for: 4 -> 5; matrix products, arithmetic and copies ran while one was open for 16% -> 21% of each run, Pallas kernels for 2% -> 4%
where the time goes in v14:
time: 146 us; the launch traced here: 145 us
  waiting for transfers between devices  62 us (42%)
  starting transfers between devices  32.6 us (22%)
  matrix products  14.6 us (10%)
  between operations  14.1 us (10%)
  other arithmetic  10.3 us (7%)
  local copies, waits for them, and re-layouts  6.05 us (4%)
  Pallas kernels  5.85 us (4%)
    all_to_all x1, waiting for transfers between devices, body(): lax.all_to_all(partial_out.astype(jnp.bfloat16), 'ch', 1, 0, tiled=True)  26 us
    all_gather x1, waiting for transfers between devices, body(): cot_rows = lax.all_gather(cotangent, 'ch', axis=1, tiled=True)  19 us
    all_to_all x1, starting transfers between devices, body(): pair_t = lax.all_to_all(pair, 'ctx', 0, 0, tiled=True)  9.97 us
    all_to_all x1, starting transfers between devices, body(): lax.all_to_all(grad_mixed.T.astype(jnp.bfloat16), 'ctx', 0, 0, tiled=True)  9.3 us
    all_to_all x1, waiting for transfers between devices, body(): lax.all_to_all(grad_mixed.T.astype(jnp.bfloat16), 'ctx', 0, 0, tiled=True)  6.63 us
    all_to_all x1, waiting for transfers between devices, body(): lax.all_to_all(filter_grad_t.astype(jnp.bfloat16), 'ctx', 0, 0, tiled=True)  6.62 us
    dot_general x4, matrix products, transform_t(): lax.dot_general(block_rows.astype(jnp.float32), dft_table, (((1,), (1,)),...  5.91 us
    dot_general x2, matrix products, inverse_t(): lax.dot_general(spec_t, inverse_rows, (((1,), (1,)), ((), ())), precision...  4.9 us
  transfers between devices with their start and end apart: 6, of which 5 were waited for; matrix products, arithmetic and copies ran while one was open for 21% of the time, Pallas kernels for 4%

profile of v14, /device:TPU:1, one launch (start us, length us, event | category | flops | bytes accessed | tf_op | source)
XLA Modules:
  0.0 145.5 jit_solution(17217835763301203215)
XLA Ops:
  7.2 0.0 copy-start
  7.2 0.0 all-gather.2.cloned.1.call-start
  7.2 0.7 all-gather.2.cloned.1.call-update
  7.9 1.0 copy.17
  8.9 1.0 copy.18
  9.9 0.7 pad_maximum_fusion.1
  10.7 10.0 %all-to-all-start = ((bf16[16,16,512]{2,1,0:T(8,128)(2,1)}), bf16[16,16,512]{2,1,0:T(8,128)(2,1)S(1)}, u32[]{:S(2)}, u32[]{:S(2)}) async-start(bf16[16,16,512]{2,1,0:T(8,128)(2,1)} %bitcast.2), calls=%async_computation | async-start | bytes 524288 | tf_op jit(solution)/shard_map/all_to_all | solution.py:177
  20.6 1.7 %copy.16 = bf16[256,256]{0,1:T(8,128)(2,1)} copy(bf16[256,256]{1,0:T(8,128)(2,1)} %param.7) | data formatting | bytes 262144 | tf_op args[1]
  22.3 1.9 %fusion.13 = f32[256,512]{1,0:T(8,128)S(1)} fusion(), kind=kLoop, calls=%fused_computation.32 | loop fusion | flops 1835008 | bytes 524288 | tf_op jit(solution)/shard_map/cos | solution.py:22
  24.2 2.0 %multiply_multiply_fusion = f32[256,512]{1,0:T(8,128)S(1)} fusion(f32[256]{0:T(256)S(1)} %broadcast_select_fusion), kind=kLoop, calls=%fused_computation.20 | loop fusion | flops 2097152 | bytes 525312 | tf_op jit(solution)/shard_map/mul | solution.py:25
  26.2 2.0 %select_multiply_fusion = (f32[256,512]{1,0:T(8,128)S(1)}, f32[256,512]{1,0:T(8,128)S(1)}) fusion(f32[512]{0:T(512)S(1)} %fusion.28, pred[256]{0:T(512)(128)(4,1)S(1)} %iota_compare_fusion), kind=kLoop, calls=%fused_computation.19 | loop fusion | flops 2490368 | bytes 1050880 | tf_op jit(solution)/shard_map/mul | solution.py:26
  28.2 1.0 maximum_bitcast_fusion
  29.3 2.9 %all-to-all-done = bf16[16,16,512]{2,1,0:T(8,128)(2,1)S(1)} async-done(((bf16[16,16,512]{2,1,0:T(8,128)(2,1)}), bf16[16,16,512]{2,1,0:T(8,128)(2,1)S(1)}, u32[]{:S(2)}, u32[]{:S(2)}) %all-to-all-start) | async-done | bytes 262176 | tf_op jit(solution)/shard_map/all_to_all | solution.py:177
  32.2 1.2 fusion.17.taps_ref
  33.5 1.3 fusion.14.high_ref
  34.7 1.3 fusion.21.low_ref
  36.0 0.0 copy-start.1
  36.0 2.9 %shard_map.77 = (f32[256,512]{1,0:T(8,128)}, f32[256,512]{1,0:T(8,128)}) custom-call(f32[256,512]{1,0:T(8,128)} %fusion.21.low_ref, f32[256,512]{1,0:T(8,128)} %fusion.14.high_ref, f32[256,512]{1,0:T(8,128)} %fusion.17.taps_ref), custom_call_target="tpu_custom_call" | custom-call | flops 4456448 | bytes 2621440 | tf_op jit(solution)/shard_map/pallas_call | solution.py:125
  38.8 2.4 %convolution_convert_fusion.2 = bf16[256,256]{1,0:T(8,128)(2,1)} fusion(f32[256,512]{1,0:T(8,128)} %get-tuple-element.4, f32[512,512]{0,1:T(8,128)} %maximum_bitcast_fusion), kind=kOutput, calls=%fused_computation.5 | convolution fusion | flops 402718720 | bytes 1179648 | tf_op jit(solution)/shard_map/dot_general | solution.py:163
  41.3 4.3 %all-to-all-start.1 = ((bf16[16,16,256]{2,1,0:T(8,128)(2,1)}), bf16[16,16,256]{2,1,0:T(8,128)(2,1)S(1)}, u32[]{:S(2)}, u32[]{:S(2)}) async-start(bf16[16,16,256]{2,1,0:T(8,128)(2,1)} %bitcast.43), calls=%async_computation.1 | async-start | bytes 262144 | tf_op jit(solution)/shard_map/all_to_all | solution.py:199
  45.6 0.0 copy-start.2
  45.6 19.0 %all-gather.2.cloned.1.call-done = bf16[256,4096]{1,0:T(8,128)(2,1)} async-done(((bf16[256,256]{1,0:T(8,128)(2,1)}), bf16[256,4096]{1,0:T(8,128)(2,1)}) %all-gather.2.cloned.1.call-update) | async-done | bytes 2097168 | tf_op jit(solution)/shard_map/all_gather | solution.py:181
  64.6 0.0 copy-done
  64.6 0.0 copy-done.1
  64.6 3.0 %fusion = bf16[256,256]{0,1:T(8,128)(2,1)} fusion(bf16[256,4096]{1,0:T(8,128)(2,1)} %all-gather.2.cloned.1.call-done, bf16[256,4096]{1,0:T(8,128)(2,1)S(1)} %copy-done, bf16[256,256]{0,1:T(8,128)(2,1)S(1)} %copy-done.1), kind=kOutput, calls=%fused_computation.3 | convolution fusion | flops 537067520 | bytes 4456448 | tf_op jit(solution)/shard_map/dot_general | solution.py:182
  67.6 0.0 all-to-all-done.1
  67.6 9.3 %all-to-all-start.3 = ((bf16[16,16,256]{2,1,0:T(8,128)(2,1)}), bf16[16,16,256]{2,1,0:T(8,128)(2,1)}, u32[]{:S(2)}, u32[]{:S(2)}) async-start(bf16[16,16,256]{2,1,0:T(8,128)(2,1)} %bitcast.45), calls=%async_computation.3 | async-start | bytes 262144 | tf_op jit(solution)/shard_map/all_to_all | solution.py:207
  76.9 0.0 copy-done.2
  76.9 0.8 convolution_convert_fusion
  77.8 1.5 %copy.24 = bf16[32,16,8,256]{3,2,0,1:T(8,128)(2,1)} copy(bf16[32,16,8,256]{3,2,1,0:T(8,128)(2,1)S(1)} %bitcast.37) | data formatting | bytes 4194304 | tf_op jit(solution)/shard_map/all_to_all | solution.py:206
  79.3 6.6 %all-to-all-done.3 = bf16[16,16,256]{2,1,0:T(8,128)(2,1)} async-done(((bf16[16,16,256]{2,1,0:T(8,128)(2,1)}), bf16[16,16,256]{2,1,0:T(8,128)(2,1)}, u32[]{:S(2)}, u32[]{:S(2)}) %all-to-all-start.3) | async-done | bytes 131104 | tf_op jit(solution)/shard_map/all_to_all | solution.py:207
  85.9 4.7 %all-to-all-start.2 = ((bf16[256,16,256]{2,0,1:T(8,128)(2,1)}), bf16[256,16,256]{2,0,1:T(8,128)(2,1)}, u32[]{:S(2)}, u32[]{:S(2)}) async-start(bf16[256,16,256]{2,0,1:T(8,128)(2,1)} %bitcast.36), calls=%async_computation.2 | async-start | bytes 4194304 | tf_op jit(solution)/shard_map/all_to_all | solution.py:206
  90.6 2.2 %fusion.15.grad_ref = f32[256,512]{1,0:T(8,128)} fusion(bf16[256,256]{1,0:T(8,128)(2,1)} %bitcast.10, f32[256,512]{1,0:T(8,128)S(1)} %get-tuple-element.11, f32[256,512]{1,0:T(8,128)S(1)} %fusion.13), kind=kOutput, calls=%fused_computation.34 | convolution fusion | flops 402784256 | bytes 1703936 | tf_op jit(solution)/shard_map/dot_general | solution.py:156
  92.8 3.0 %shard_map.78 = f32[256,512]{1,0:T(8,128)} custom-call(f32[256,512]{1,0:T(8,128)} %get-tuple-element.5.seg_ref, f32[256,512]{1,0:T(8,128)} %fusion.15.grad_ref), custom_call_target="tpu_custom_call" | custom-call | flops 4456448 | bytes 1572864 | tf_op jit(solution)/shard_map/pallas_call | solution.py:142
  95.8 2.4 %convolution_convert_fusion.1 = bf16[256,256]{1,0:T(8,128)(2,1)} fusion(f32[256,512]{1,0:T(8,128)} %shard_map.78, f32[512,512]{0,1:T(8,128)} %maximum_bitcast_fusion), kind=kOutput, calls=%fused_computation.4 | convolution fusion | flops 402718720 | bytes 1179648 | tf_op jit(solution)/shard_map/dot_general | solution.py:163
  98.2 26.0 %all-to-all-done.2 = bf16[256,16,256]{2,0,1:T(8,128)(2,1)} async-done(((bf16[256,16,256]{2,0,1:T(8,128)(2,1)}), bf16[256,16,256]{2,0,1:T(8,128)(2,1)}, u32[]{:S(2)}, u32[]{:S(2)}) %all-to-all-start.2) | async-done | bytes 2097184 | tf_op jit(solution)/shard_map/all_to_all | solution.py:206
  124.3 4.3 %all-to-all-start.4 = ((bf16[16,16,256]{2,1,0:T(8,128)(2,1)}), bf16[16,16,256]{2,1,0:T(8,128)(2,1)S(1)}, u32[]{:S(2)}, u32[]{:S(2)}) async-start(bf16[16,16,256]{2,1,0:T(8,128)(2,1)} %bitcast.11), calls=%async_computation.4 | async-start | bytes 262144 | tf_op jit(solution)/shard_map/all_to_all | solution.py:211
  128.6 2.6 %reduce_sum.12 = bf16[256,256]{1,0:T(8,128)(2,1)} reduce(bf16[256,16,256]{2,0,1:T(8,128)(2,1)} %all-to-all-done.2, bf16[]{:T(256)} %constant.46.clone.1), dimensions={1}, to_apply=%region_0.1 | reduce | flops 983040 | bytes 2228226 | tf_op jit(solution)/shard_map/reduce_sum | solution.py:218
  131.1 6.6 %all-to-all-done.4 = bf16[16,16,256]{2,1,0:T(8,128)(2,1)S(1)} async-done(((bf16[16,16,256]{2,1,0:T(8,128)(2,1)}), bf16[16,16,256]{2,1,0:T(8,128)(2,1)S(1)}, u32[]{:S(2)}, u32[]{:S(2)}) %all-to-all-start.4) | async-done | bytes 131104 | tf_op jit(solution)/shard_map/all_to_all | solution.py:211
  137.8 0.8 copy.21
  (4 shorter events, 0.0 us)
Async XLA Ops:
  7.2 57.5 %copy-start = (bf16[256,4096]{1,0:T(8,128)(2,1)S(1)}, bf16[256,4096]{1,0:T(8,128)(2,1)}, u32[]{:S(2)}) copy-start(bf16[256,4096]{1,0:T(8,128)(2,1)} %param.10) | copy-start | bytes 6291460
  7.2 57.5 %all-gather.2.cloned.1.call-start = ((), (), s32[]{:S(2)}) async-start(), calls=%async_computation.5 | async-start | bytes 2228224 | tf_op jit(solution)/shard_map/all_gather | solution.py:181
  10.7 21.6 %all-to-all-start = ((bf16[16,16,512]{2,1,0:T(8,128)(2,1)}), bf16[16,16,512]{2,1,0:T(8,128)(2,1)S(1)}, u32[]{:S(2)}, u32[]{:S(2)}) async-start(bf16[16,16,512]{2,1,0:T(8,128)(2,1)} %bitcast.2), calls=%async_computation | async-start | bytes 524288 | tf_op jit(solution)/shard_map/all_to_all | solution.py:177
  36.0 28.7 %copy-start.1 = (bf16[256,256]{0,1:T(8,128)(2,1)S(1)}, bf16[256,256]{0,1:T(8,128)(2,1)}, u32[]{:S(2)}) copy-start(bf16[256,256]{0,1:T(8,128)(2,1)} %copy.16) | copy-start | bytes 393220
  41.3 26.3 %all-to-all-start.1 = ((bf16[16,16,256]{2,1,0:T(8,128)(2,1)}), bf16[16,16,256]{2,1,0:T(8,128)(2,1)S(1)}, u32[]{:S(2)}, u32[]{:S(2)}) async-start(bf16[16,16,256]{2,1,0:T(8,128)(2,1)} %bitcast.43), calls=%async_computation.1 | async-start | bytes 262144 | tf_op jit(solution)/shard_map/all_to_all | solution.py:199
  45.6 31.3 %copy-start.2 = (f32[256]{0:T(256)S(1)}, f32[256]{0:T(256)}, u32[]{:S(2)}) copy-start(f32[256]{0:T(256)} %param.9) | copy-start | bytes 3076
  67.6 18.3 %all-to-all-start.3 = ((bf16[16,16,256]{2,1,0:T(8,128)(2,1)}), bf16[16,16,256]{2,1,0:T(8,128)(2,1)}, u32[]{:S(2)}, u32[]{:S(2)}) async-start(bf16[16,16,256]{2,1,0:T(8,128)(2,1)} %bitcast.45), calls=%async_computation.3 | async-start | bytes 262144 | tf_op jit(solution)/shard_map/all_to_all | solution.py:207
  85.9 38.3 %all-to-all-start.2 = ((bf16[256,16,256]{2,0,1:T(8,128)(2,1)}), bf16[256,16,256]{2,0,1:T(8,128)(2,1)}, u32[]{:S(2)}, u32[]{:S(2)}) async-start(bf16[256,16,256]{2,0,1:T(8,128)(2,1)} %bitcast.36), calls=%async_computation.2 | async-start | bytes 4194304 | tf_op jit(solution)/shard_map/all_to_all | solution.py:206
  124.3 13.5 %all-to-all-start.4 = ((bf16[16,16,256]{2,1,0:T(8,128)(2,1)}), bf16[16,16,256]{2,1,0:T(8,128)(2,1)S(1)}, u32[]{:S(2)}, u32[]{:S(2)}) async-start(bf16[16,16,256]{2,1,0:T(8,128)(2,1)} %bitcast.11), calls=%async_computation.4 | async-start | bytes 262144 | tf_op jit(solution)/shard_map/all_to_all | solution.py:211
Sparse Core Ops, SparseCore 0:
  10.4 54.1 all-gather.1

commit v15 on v12

--- a/solution.py
+++ b/solution.py
@@ -202,8 +202,10 @@
 
     mixed_sum = convolved + skip_gain[None, :] * inputs.astype(jnp.float32)
     gated_rows = (gate_wide * mixed_sum).astype(jnp.bfloat16)
-    partial_out = jnp.dot(gated_rows, w_out, preferred_element_type=jnp.float32)
-    pieces = lax.all_to_all(partial_out.astype(jnp.bfloat16), "ch", 1, 0, tiled=True)
+    partial_out = lax.dot_general(
+        w_out, gated_rows, (((0,), (1,)), ((), ())), preferred_element_type=jnp.float32
+    )
+    pieces = lax.all_to_all(partial_out.astype(jnp.bfloat16), "ch", 0, 0, tiled=True)
     pieces, grad_mixed = lax.optimization_barrier((pieces, grad_mixed))
     grad_t = lax.all_to_all(grad_mixed.T.astype(jnp.bfloat16), "ctx", 0, 0, tiled=True)
 
@@ -215,9 +217,10 @@
 
     output = (
         pieces.astype(jnp.float32)
-        .reshape(ch_count, block_len, channels)
+        .reshape(ch_count, channels, block_len)
         .sum(axis=0)
         .astype(jnp.bfloat16)
+        .T
     )
     return (output, filter_grad)
 

time: 145 us -> 143 us (0.986)
  blocking collectives: 27.6 us -> 65.5 us
  waiting for transfers between devices: 46 us -> 10.8 us
  starting transfers between devices: 20.3 us -> 13.4 us
  local copies, waits for them, and re-layouts: 5.72 us -> 9.08 us
    all_to_all x0 -> x1, blocking collectives: none -> 40.4 us  [body(): lax.all_to_all(partial_out.astype(jnp.bfloat16), 'ch', 0, 0, tiled=True)]
    all_gather x1, waiting for transfers between devices: 31.9 us -> 0.01 us  [body(): cot_rows = lax.all_gather(cotangent, 'ch', axis=1, tiled=True)]
    all_to_all x1 -> x0, starting transfers between devices: 6.93 us -> none  [body(): lax.all_to_all(partial_out.astype(jnp.bfloat16), 'ch', 1, 0, tiled=True)]
    all_to_all x1 -> x0, waiting for transfers between devices: 3.2 us -> none  [body(): lax.all_to_all(partial_out.astype(jnp.bfloat16), 'ch', 1, 0, tiled=True)]
    all_to_all x1 -> x2, local copies, waits for them, and re-layouts: 1.53 us -> 4.14 us  [body(): lax.all_to_all(partial_out.astype(jnp.bfloat16), 'ch', 0, 0, tiled=True)]
    all_to_all x1, blocking collectives: 15.6 us -> 13 us  [body(): lax.all_to_all(grad_mixed.T.astype(jnp.bfloat16), 'ctx', 0, 0, tiled=True)]
    unnamed x11 -> x12, local copies, waits for them, and re-layouts: 3.01 us -> 3.77 us
  transfers between devices with their start and end apart: 4 -> 3, of which waited for: 4 -> 2; matrix products, arithmetic and copies ran while one was open for 16% -> 16% of each run, Pallas kernels for 2% -> 2%
where the time goes in v15:
time: 143 us; the launch traced here: 142 us
  blocking collectives  65.5 us (46%)
  between operations  14.2 us (10%)
  starting transfers between devices  13.4 us (9%)
  matrix products  13.1 us (9%)
  waiting for transfers between devices  10.8 us (8%)
  other arithmetic  10.4 us (7%)
  local copies, waits for them, and re-layouts  9.08 us (6%)
  Pallas kernels  5.86 us (4%)
    all_to_all x1, blocking collectives, body(): lax.all_to_all(partial_out.astype(jnp.bfloat16), 'ch', 0, 0, tiled=True)  40.4 us
    all_to_all x1, blocking collectives, body(): lax.all_to_all(grad_mixed.T.astype(jnp.bfloat16), 'ctx', 0, 0, tiled=True)  13 us
    all_to_all x1, blocking collectives, body(): lax.all_to_all(convolved_t.astype(jnp.bfloat16), 'ctx', 0, 0, tiled=True)  12.1 us
    all_to_all x1, starting transfers between devices, body(): pair_t = lax.all_to_all(pair, 'ctx', 0, 0, tiled=True)  9.97 us
    all_to_all x1, waiting for transfers between devices, body(): lax.all_to_all(filter_grad_t.astype(jnp.bfloat16), 'ctx', 0, 0, tiled=True)  6.28 us
    dot_general x4, matrix products, transform_t(): lax.dot_general(block_rows.astype(jnp.float32), dft_table, (((1,), (1,)),...  4.95 us
    dot_general x2, matrix products, inverse_t(): lax.dot_general(spec_t, inverse_rows, (((1,), (1,)), ((), ())), precision...  4.24 us
    all_to_all x2, local copies, waits for them, and re-layouts, body(): lax.all_to_all(partial_out.astype(jnp.bfloat16), 'ch', 0, 0, tiled=True)  4.14 us
  transfers between devices with their start and end apart: 3, of which 2 were waited for; matrix products, arithmetic and copies ran while one was open for 16% of the time, Pallas kernels for 2%

profile of v15, /device:TPU:1, one launch (start us, length us, event | category | flops | bytes accessed | tf_op | source)
XLA Modules:
  0.0 142.3 jit_solution(12947262367389835768)
XLA Ops:
  7.2 0.0 copy-start
  7.2 1.2 copy.28
  8.3 1.0 copy.29
  9.3 0.7 pad_maximum_fusion.1
  10.1 10.0 %all-to-all-start = ((bf16[16,16,512]{2,1,0:T(8,128)(2,1)}), bf16[16,16,512]{2,1,0:T(8,128)(2,1)S(1)}, u32[]{:S(2)}, u32[]{:S(2)}) async-start(bf16[16,16,512]{2,1,0:T(8,128)(2,1)} %bitcast.2), calls=%async_computation | async-start | bytes 524288 | tf_op jit(solution)/shard_map/all_to_all | solution.py:177
  20.0 0.0 all-gather.2.cloned.1.call-start
  20.1 0.7 all-gather.2.cloned.1.call-update
  20.8 2.0 %select_multiply_fusion = (f32[256,512]{1,0:T(8,128)S(1)}, f32[256,512]{1,0:T(8,128)S(1)}) fusion(f32[512]{0:T(512)S(1)} %fusion.26, pred[256]{0:T(512)(128)(4,1)S(1)} %iota_compare_fusion), kind=kLoop, calls=%fused_computation.18 | loop fusion | flops 2490368 | bytes 1050880 | tf_op jit(solution)/shard_map/mul | solution.py:26
  22.9 2.0 %multiply_multiply_fusion = f32[256,512]{1,0:T(8,128)S(1)} fusion(f32[256]{0:T(256)S(1)} %broadcast_select_fusion), kind=kLoop, calls=%fused_computation.19 | loop fusion | flops 2097152 | bytes 525312 | tf_op jit(solution)/shard_map/mul | solution.py:25
  24.8 1.9 %fusion.11 = f32[256,512]{1,0:T(8,128)S(1)} fusion(), kind=kLoop, calls=%fused_computation.30 | loop fusion | flops 1835008 | bytes 524288 | tf_op jit(solution)/shard_map/cos | solution.py:22
  26.7 1.1 maximum_bitcast_fusion
  27.8 3.8 %all-to-all-done = bf16[16,16,512]{2,1,0:T(8,128)(2,1)S(1)} async-done(((bf16[16,16,512]{2,1,0:T(8,128)(2,1)}), bf16[16,16,512]{2,1,0:T(8,128)(2,1)S(1)}, u32[]{:S(2)}, u32[]{:S(2)}) %all-to-all-start) | async-done | bytes 262176 | tf_op jit(solution)/shard_map/all_to_all | solution.py:177
  31.6 1.2 fusion.12.high_ref
  32.9 1.2 fusion.15.taps_ref
  34.1 1.2 fusion.19.low_ref
  35.4 0.0 copy-start.1
  35.4 0.0 copy-start.3
  35.4 2.9 %shard_map.77 = (f32[256,512]{1,0:T(8,128)}, f32[256,512]{1,0:T(8,128)}) custom-call(f32[256,512]{1,0:T(8,128)} %fusion.19.low_ref, f32[256,512]{1,0:T(8,128)} %fusion.12.high_ref, f32[256,512]{1,0:T(8,128)} %fusion.15.taps_ref), custom_call_target="tpu_custom_call" | custom-call | flops 4456448 | bytes 2621440 | tf_op jit(solution)/shard_map/pallas_call | solution.py:125
  38.3 1.8 %convolution_convert_fusion.2 = bf16[256,256]{1,0:T(8,128)(2,1)S(1)} fusion(f32[256,512]{1,0:T(8,128)} %get-tuple-element.6, f32[512,512]{0,1:T(8,128)} %maximum_bitcast_fusion), kind=kOutput, calls=%fused_computation.4 | convolution fusion | flops 402718720 | bytes 1179648 | tf_op jit(solution)/shard_map/dot_general | solution.py:163
  40.1 12.1 %all_to_all.54 = bf16[16,16,256]{2,1,0:T(8,128)(2,1)S(1)} all-to-all(bf16[16,16,256]{2,1,0:T(8,128)(2,1)S(1)} %bitcast.46), channel_id=1, replica_groups=mesh['ctx'=16,'ch'=16] {'ctx'}, dimensions={0} | all-to-all | bytes 262144 | tf_op jit(solution)/shard_map/all_to_all | solution.py:199
  52.1 0.7 bitcast_convert_fusion
  52.8 1.1 copy.30
  53.9 0.0 copy-done
  53.9 0.0 copy-done.1
  54.0 0.0 copy-done.3
  54.0 1.6 %convolution_convert_fusion = bf16[256,4096]{1,0:T(8,128)(2,1)S(1)} fusion(bf16[256,4096]{1,0:T(8,128)(2,1)S(1)} %copy-done, bf16[256,256]{1,0:T(8,128)(2,1)} %param.7, f32[256,256]{0,1:T(8,128)S(1)} %copy.30, bf16[256,256]{1,0:T(8,128)(2,1)S(1)} %copy-done.1, f32[256]{0:T(256)S(1)} %copy-done.3), kind=kOutput, calls=%fused_computation | convolution fusion | flops 538312704 | bytes 4719616 | tf_op jit(solution)/shard_map/dot_general | solution.py:205
  55.6 0.2 copy.38
  55.8 40.4 %all_to_all.55 = bf16[16,256,256]{1,2,0:T(8,128)(2,1)} all-to-all(bf16[16,256,256]{1,2,0:T(8,128)(2,1)S(1)} %bitcast.41), channel_id=1, replica_groups=mesh['ctx'=16,'ch'=16] {'ch'}, dimensions={0} | all-to-all | bytes 4194304 | tf_op jit(solution)/shard_map/all_to_all | solution.py:208
  96.2 0.0 copy-start.2
  96.2 3.9 %copy.32 = bf16[16,256,256]{2,1,0:T(8,128)(2,1)} copy(bf16[16,256,256]{1,2,0:T(8,128)(2,1)} %all_to_all.55) | data formatting | bytes 4194304 | tf_op jit(solution)/shard_map/all_to_all | solution.py:208
  100.2 0.0 all-gather.2.cloned.1.call-done
  100.2 0.0 copy-done.2
  100.2 2.3 %convolution_multiply_fusion = bf16[256,256]{1,0:T(8,128)(2,1)S(1)} fusion(bf16[256,4096]{1,0:T(8,128)(2,1)} %all-gather.2.cloned.1.call-done, bf16[256,4096]{1,0:T(8,128)(2,1)S(1)} %copy-done, bf16[256,256]{1,0:T(8,128)(2,1)S(1)} %copy-done.2), kind=kOutput, calls=%fused_computation.2 | convolution fusion | flops 537067520 | bytes 4456448 | tf_op jit(solution)/shard_map/dot_general | solution.py:182
  102.5 0.1 copy.33
  102.6 13.0 %all_to_all.56 = bf16[16,16,256]{2,1,0:T(8,128)(2,1)S(1)} all-to-all(bf16[16,16,256]{2,1,0:T(8,128)(2,1)S(1)} %bitcast.47), channel_id=1, replica_groups=mesh['ctx'=16,'ch'=16] {'ctx'}, dimensions={0} | all-to-all | bytes 262144 | tf_op jit(solution)/shard_map/all_to_all | solution.py:210
  115.6 1.2 fusion.13.grad_ref
  116.9 3.0 %shard_map.78 = f32[256,512]{1,0:T(8,128)} custom-call(f32[256,512]{1,0:T(8,128)} %get-tuple-element.8.seg_ref, f32[256,512]{1,0:T(8,128)} %fusion.13.grad_ref), custom_call_target="tpu_custom_call" | custom-call | flops 4456448 | bytes 1572864 | tf_op jit(solution)/shard_map/pallas_call | solution.py:142
  119.8 2.4 %convolution_convert_fusion.1 = bf16[256,256]{1,0:T(8,128)(2,1)} fusion(f32[256,512]{1,0:T(8,128)} %shard_map.78, f32[512,512]{0,1:T(8,128)} %maximum_bitcast_fusion), kind=kOutput, calls=%fused_computation.3 | convolution fusion | flops 402718720 | bytes 1179648 | tf_op jit(solution)/shard_map/dot_general | solution.py:163
  122.3 3.4 %all-to-all-start.4 = ((bf16[16,16,256]{2,1,0:T(8,128)(2,1)}), bf16[16,16,256]{2,1,0:T(8,128)(2,1)S(1)}, u32[]{:S(2)}, u32[]{:S(2)}) async-start(bf16[16,16,256]{2,1,0:T(8,128)(2,1)} %bitcast.15), calls=%async_computation.4 | async-start | bytes 262144 | tf_op jit(solution)/shard_map/all_to_all | solution.py:214
  125.7 1.9 %reduce = bf16[256,256]{1,0:T(8,128)(2,1)S(1)} reduce(bf16[16,256,256]{2,1,0:T(8,128)(2,1)} %copy.32, bf16[]{:T(256)} %constant.46), dimensions={0}, to_apply=%region_0.1.clone | reduce | flops 983040 | bytes 2228226 | tf_op jit(solution)/shard_map/reduce_sum | solution.py:221
  127.6 0.8 copy.34
  128.3 6.3 %all-to-all-done.4 = bf16[16,16,256]{2,1,0:T(8,128)(2,1)S(1)} async-done(((bf16[16,16,256]{2,1,0:T(8,128)(2,1)}), bf16[16,16,256]{2,1,0:T(8,128)(2,1)S(1)}, u32[]{:S(2)}, u32[]{:S(2)}) %all-to-all-start.4) | async-done | bytes 131104 | tf_op jit(solution)/shard_map/all_to_all | solution.py:214
  134.6 0.8 copy.35
  (4 shorter events, 0.0 us)
Async XLA Ops:
  7.2 46.8 %copy-start = (bf16[256,4096]{1,0:T(8,128)(2,1)S(1)}, bf16[256,4096]{1,0:T(8,128)(2,1)}, u32[]{:S(2)}) copy-start(bf16[256,4096]{1,0:T(8,128)(2,1)} %param.10) | copy-start | bytes 6291460
  10.1 21.6 %all-to-all-start = ((bf16[16,16,512]{2,1,0:T(8,128)(2,1)}), bf16[16,16,512]{2,1,0:T(8,128)(2,1)S(1)}, u32[]{:S(2)}, u32[]{:S(2)}) async-start(bf16[16,16,512]{2,1,0:T(8,128)(2,1)} %bitcast.2), calls=%async_computation | async-start | bytes 524288 | tf_op jit(solution)/shard_map/all_to_all | solution.py:177
  20.0 80.1 %all-gather.2.cloned.1.call-start = ((), (), s32[]{:S(2)}) async-start(), calls=%async_computation.5 | async-start | bytes 2228224 | tf_op jit(solution)/shard_map/all_gather | solution.py:181
  35.4 18.6 %copy-start.1 = (bf16[256,256]{1,0:T(8,128)(2,1)S(1)}, bf16[256,256]{1,0:T(8,128)(2,1)}, u32[]{:S(2)}) copy-start(bf16[256,256]{1,0:T(8,128)(2,1)} %param.6) | copy-start | bytes 393220
  35.4 18.6 %copy-start.3 = (f32[256]{0:T(256)S(1)}, f32[256]{0:T(256)}, u32[]{:S(2)}) copy-start(f32[256]{0:T(256)} %param.9) | copy-start | bytes 3076
  96.2 3.9 %copy-start.2 = (bf16[256,256]{1,0:T(8,128)(2,1)S(1)}, bf16[256,256]{1,0:T(8,128)(2,1)}, u32[]{:S(2)}) copy-start(bf16[256,256]{1,0:T(8,128)(2,1)} %param.7) | copy-start | bytes 393220
  122.3 12.3 %all-to-all-start.4 = ((bf16[16,16,256]{2,1,0:T(8,128)(2,1)}), bf16[16,16,256]{2,1,0:T(8,128)(2,1)S(1)}, u32[]{:S(2)}, u32[]{:S(2)}) async-start(bf16[16,16,256]{2,1,0:T(8,128)(2,1)} %bitcast.15), calls=%async_computation.4 | async-start | bytes 262144 | tf_op jit(solution)/shard_map/all_to_all | solution.py:214
Sparse Core Ops, SparseCore 0:
  23.3 70.8 all-gather.1

commit v16 on v15

--- a/solution.py
+++ b/solution.py
@@ -179,14 +179,14 @@
 
     ch_count = lax.axis_size("ch")
     cot_rows = lax.all_gather(cotangent, "ch", axis=1, tiled=True)
-    upstream = lax.dot_general(
+    upstream_t = lax.dot_general(
+        w_out,
         cot_rows,
-        w_out,
         (((1,), (1,)), ((), ())),
         preferred_element_type=jnp.float32,
     )
     gate_wide = gating.astype(jnp.float32)
-    grad_mixed = upstream * gate_wide
+    grad_mixed_t = upstream_t * gate_wide.T
 
     conv_spec, seg_spec = conv_products(
         transform_t(first_half, signal_t),
@@ -206,8 +206,8 @@
         w_out, gated_rows, (((0,), (1,)), ((), ())), preferred_element_type=jnp.float32
     )
     pieces = lax.all_to_all(partial_out.astype(jnp.bfloat16), "ch", 0, 0, tiled=True)
-    pieces, grad_mixed = lax.optimization_barrier((pieces, grad_mixed))
-    grad_t = lax.all_to_all(grad_mixed.T.astype(jnp.bfloat16), "ctx", 0, 0, tiled=True)
+    pieces, grad_mixed_t = lax.optimization_barrier((pieces, grad_mixed_t))
+    grad_t = lax.all_to_all(grad_mixed_t.astype(jnp.bfloat16), "ctx", 0, 0, tiled=True)
 
     lag_spec = lag_products(seg_spec, transform_t(second_half, grad_t), width)
     filter_grad_t = inverse_t(inverse[:block_len], lag_spec)

time: 143 us -> 138 us (0.965)
  blocking collectives: 65.5 us -> 50.3 us
  waiting for transfers between devices: 10.8 us -> 19 us
  starting transfers between devices: 13.4 us -> 16.8 us
    all_to_all x2 -> x1, blocking collectives: 25.1 us -> 14 us  [body(): lax.all_to_all(grad_mixed_t.astype(jnp.bfloat16), 'ctx', 0, 0, tiled=True)]
    all_to_all x0 -> x1, waiting for transfers between devices: none -> 7.45 us  [body(): lax.all_to_all(convolved_t.astype(jnp.bfloat16), 'ctx', 0, 0, tiled=True)]
    all_to_all x1, blocking collectives: 40.4 us -> 36.2 us  [body(): lax.all_to_all(partial_out.astype(jnp.bfloat16), 'ch', 0, 0, tiled=True)]
    all_to_all x0 -> x1, starting transfers between devices: none -> 3.41 us  [body(): lax.all_to_all(convolved_t.astype(jnp.bfloat16), 'ctx', 0, 0, tiled=True)]
    unnamed x12 -> x9, local copies, waits for them, and re-layouts: 3.77 us -> 4.62 us
  transfers between devices with their start and end apart: 3 -> 4, of which waited for: 2 -> 3; matrix products, arithmetic and copies ran while one was open for 16% -> 18% of each run, Pallas kernels for 2% -> 2%
where the time goes in v16:
time: 138 us; the launch traced here: 137 us
  blocking collectives  50.3 us (36%)
  waiting for transfers between devices  19 us (14%)
  starting transfers between devices  16.8 us (12%)
  between operations  14.1 us (10%)
  matrix products  13 us (9%)
  other arithmetic  9.63 us (7%)
  local copies, waits for them, and re-layouts  8.72 us (6%)
  Pallas kernels  5.79 us (4%)
    all_to_all x1, blocking collectives, body(): lax.all_to_all(partial_out.astype(jnp.bfloat16), 'ch', 0, 0, tiled=True)  36.2 us
    all_to_all x1, blocking collectives, body(): lax.all_to_all(grad_mixed_t.astype(jnp.bfloat16), 'ctx', 0, 0, tiled=True)  14 us
    all_to_all x1, starting transfers between devices, body(): pair_t = lax.all_to_all(pair, 'ctx', 0, 0, tiled=True)  9.97 us
    all_to_all x1, waiting for transfers between devices, body(): lax.all_to_all(convolved_t.astype(jnp.bfloat16), 'ctx', 0, 0, tiled=True)  7.45 us
    all_to_all x1, waiting for transfers between devices, body(): lax.all_to_all(filter_grad_t.astype(jnp.bfloat16), 'ctx', 0, 0, tiled=True)  6.28 us
    dot_general x4, matrix products, transform_t(): lax.dot_general(block_rows.astype(jnp.float32), dft_table, (((1,), (1,)),...  4.96 us
    dot_general x2, matrix products, inverse_t(): lax.dot_general(spec_t, inverse_rows, (((1,), (1,)), ((), ())), precision...  4.9 us
    unnamed x9, local copies, waits for them, and re-layouts  4.62 us
  transfers between devices with their start and end apart: 4, of which 3 were waited for; matrix products, arithmetic and copies ran while one was open for 18% of the time, Pallas kernels for 2%

profile of v16, /device:TPU:1, one launch (start us, length us, event | category | flops | bytes accessed | tf_op | source)
XLA Modules:
  0.0 137.4 jit_solution(16884186916526691809)
XLA Ops:
  7.2 0.0 copy-start
  7.2 0.0 all-gather.2.cloned.1.call-start
  7.2 0.7 all-gather.2.cloned.1.call-update
  7.9 1.0 copy.30
  8.9 1.0 copy.31
  9.9 0.7 pad_maximum_fusion.1
  10.7 10.0 %all-to-all-start = ((bf16[16,16,512]{2,1,0:T(8,128)(2,1)}), bf16[16,16,512]{2,1,0:T(8,128)(2,1)S(1)}, u32[]{:S(2)}, u32[]{:S(2)}) async-start(bf16[16,16,512]{2,1,0:T(8,128)(2,1)} %bitcast.2), calls=%async_computation | async-start | bytes 524288 | tf_op jit(solution)/shard_map/all_to_all | solution.py:177
  20.6 1.9 %fusion.12 = f32[256,512]{1,0:T(8,128)S(1)} fusion(), kind=kLoop, calls=%fused_computation.32 | loop fusion | flops 1835008 | bytes 524288 | tf_op jit(solution)/shard_map/cos | solution.py:22
  22.5 2.0 %multiply_multiply_fusion = f32[256,512]{1,0:T(8,128)S(1)} fusion(f32[256]{0:T(256)S(1)} %broadcast_select_fusion), kind=kLoop, calls=%fused_computation.19 | loop fusion | flops 2097152 | bytes 525312 | tf_op jit(solution)/shard_map/mul | solution.py:25
  24.5 2.0 %select_multiply_fusion = (f32[256,512]{1,0:T(8,128)S(1)}, f32[256,512]{1,0:T(8,128)S(1)}) fusion(f32[512]{0:T(512)S(1)} %fusion.27, pred[256]{0:T(512)(128)(4,1)S(1)} %iota_compare_fusion), kind=kLoop, calls=%fused_computation.18 | loop fusion | flops 2490368 | bytes 1050880 | tf_op jit(solution)/shard_map/mul | solution.py:26
  26.6 1.1 maximum_bitcast_fusion
  27.7 4.6 %all-to-all-done = bf16[16,16,512]{2,1,0:T(8,128)(2,1)S(1)} async-done(((bf16[16,16,512]{2,1,0:T(8,128)(2,1)}), bf16[16,16,512]{2,1,0:T(8,128)(2,1)S(1)}, u32[]{:S(2)}, u32[]{:S(2)}) %all-to-all-start) | async-done | bytes 262176 | tf_op jit(solution)/shard_map/all_to_all | solution.py:177
  32.2 1.2 fusion.16.taps_ref
  33.5 1.2 fusion.13.high_ref
  34.7 0.0 copy-start.1
  34.7 1.2 fusion.20.low_ref
  35.9 2.8 %shard_map.77 = (f32[256,512]{1,0:T(8,128)}, f32[256,512]{1,0:T(8,128)}) custom-call(f32[256,512]{1,0:T(8,128)} %fusion.20.low_ref, f32[256,512]{1,0:T(8,128)} %fusion.13.high_ref, f32[256,512]{1,0:T(8,128)} %fusion.16.taps_ref), custom_call_target="tpu_custom_call" | custom-call | flops 4456448 | bytes 2621440 | tf_op jit(solution)/shard_map/pallas_call | solution.py:125
  38.8 2.4 %convolution_convert_fusion.2 = bf16[256,256]{1,0:T(8,128)(2,1)} fusion(f32[256,512]{1,0:T(8,128)} %get-tuple-element.6, f32[512,512]{0,1:T(8,128)} %maximum_bitcast_fusion), kind=kOutput, calls=%fused_computation.4 | convolution fusion | flops 402718720 | bytes 1179648 | tf_op jit(solution)/shard_map/dot_general | solution.py:163
  41.2 3.4 %all-to-all-start.1 = ((bf16[16,16,256]{2,1,0:T(8,128)(2,1)}), bf16[16,16,256]{2,1,0:T(8,128)(2,1)S(1)}, u32[]{:S(2)}, u32[]{:S(2)}) async-start(bf16[16,16,256]{2,1,0:T(8,128)(2,1)} %bitcast.5), calls=%async_computation.1 | async-start | bytes 262144 | tf_op jit(solution)/shard_map/all_to_all | solution.py:199
  44.7 1.0 copy.29
  45.7 7.5 %all-to-all-done.1 = bf16[16,16,256]{2,1,0:T(8,128)(2,1)S(1)} async-done(((bf16[16,16,256]{2,1,0:T(8,128)(2,1)}), bf16[16,16,256]{2,1,0:T(8,128)(2,1)S(1)}, u32[]{:S(2)}, u32[]{:S(2)}) %all-to-all-start.1) | async-done | bytes 131104 | tf_op jit(solution)/shard_map/all_to_all | solution.py:199
  53.1 0.0 copy-done
  53.1 0.0 copy-done.1
  53.1 0.8 convolution_convert_fusion
  54.0 0.2 copy.39
  54.2 36.2 %all_to_all.54 = bf16[16,256,256]{1,2,0:T(8,128)(2,1)} all-to-all(bf16[16,256,256]{1,2,0:T(8,128)(2,1)S(1)} %bitcast.43), channel_id=1, replica_groups=mesh['ctx'=16,'ch'=16] {'ch'}, dimensions={0} | all-to-all | bytes 4194304 | tf_op jit(solution)/shard_map/all_to_all | solution.py:208
  90.4 3.9 %copy.34 = bf16[16,256,256]{2,1,0:T(8,128)(2,1)} copy(bf16[16,256,256]{1,2,0:T(8,128)(2,1)} %all_to_all.54) | data formatting | bytes 4194304 | tf_op jit(solution)/shard_map/all_to_all | solution.py:208
  94.3 0.0 all-gather.2.cloned.1.call-done
  94.3 2.3 %convolution_multiply_fusion = bf16[256,256]{1,0:T(8,128)(2,1)S(1)} fusion(bf16[256,4096]{1,0:T(8,128)(2,1)S(1)} %copy-done, bf16[256,4096]{1,0:T(8,128)(2,1)} %all-gather.2.cloned.1.call-done, bf16[256,256]{0,1:T(8,128)(2,1)S(1)} %copy.29), kind=kOutput, calls=%fused_computation.2 | convolution fusion | flops 537067520 | bytes 4456448 | tf_op jit(solution)/shard_map/dot_general | solution.py:182
  96.6 14.0 %all_to_all.55 = bf16[16,16,256]{2,1,0:T(8,128)(2,1)S(1)} all-to-all(bf16[16,16,256]{2,1,0:T(8,128)(2,1)S(1)} %bitcast.52), channel_id=1, replica_groups=mesh['ctx'=16,'ch'=16] {'ctx'}, dimensions={0} | all-to-all | bytes 262144 | tf_op jit(solution)/shard_map/all_to_all | solution.py:210
  110.7 1.2 fusion.14.grad_ref
  111.9 3.0 %shard_map.78 = f32[256,512]{1,0:T(8,128)} custom-call(f32[256,512]{1,0:T(8,128)} %get-tuple-element.8.seg_ref, f32[256,512]{1,0:T(8,128)} %fusion.14.grad_ref), custom_call_target="tpu_custom_call" | custom-call | flops 4456448 | bytes 1572864 | tf_op jit(solution)/shard_map/pallas_call | solution.py:142
  114.8 2.4 %convolution_convert_fusion.1 = bf16[256,256]{1,0:T(8,128)(2,1)} fusion(f32[256,512]{1,0:T(8,128)} %shard_map.78, f32[512,512]{0,1:T(8,128)} %maximum_bitcast_fusion), kind=kOutput, calls=%fused_computation.3 | convolution fusion | flops 402718720 | bytes 1179648 | tf_op jit(solution)/shard_map/dot_general | solution.py:163
  117.3 3.4 %all-to-all-start.4 = ((bf16[16,16,256]{2,1,0:T(8,128)(2,1)}), bf16[16,16,256]{2,1,0:T(8,128)(2,1)S(1)}, u32[]{:S(2)}, u32[]{:S(2)}) async-start(bf16[16,16,256]{2,1,0:T(8,128)(2,1)} %bitcast.15), calls=%async_computation.4 | async-start | bytes 262144 | tf_op jit(solution)/shard_map/all_to_all | solution.py:214
  120.7 1.9 %reduce = bf16[256,256]{1,0:T(8,128)(2,1)S(1)} reduce(bf16[16,256,256]{2,1,0:T(8,128)(2,1)} %copy.34, bf16[]{:T(256)} %constant.46), dimensions={0}, to_apply=%region_0.1.clone | reduce | flops 983040 | bytes 2228226 | tf_op jit(solution)/shard_map/reduce_sum | solution.py:221
  122.6 0.8 copy.35
  123.4 6.3 %all-to-all-done.4 = bf16[16,16,256]{2,1,0:T(8,128)(2,1)S(1)} async-done(((bf16[16,16,256]{2,1,0:T(8,128)(2,1)}), bf16[16,16,256]{2,1,0:T(8,128)(2,1)S(1)}, u32[]{:S(2)}, u32[]{:S(2)}) %all-to-all-start.4) | async-done | bytes 131104 | tf_op jit(solution)/shard_map/all_to_all | solution.py:214
  129.7 0.8 copy.36
  (4 shorter events, 0.0 us)
Async XLA Ops:
  7.2 46.0 %copy-start = (bf16[256,4096]{1,0:T(8,128)(2,1)S(1)}, bf16[256,4096]{1,0:T(8,128)(2,1)}, u32[]{:S(2)}) copy-start(bf16[256,4096]{1,0:T(8,128)(2,1)} %param.10) | copy-start | bytes 6291460
  7.2 87.1 %all-gather.2.cloned.1.call-start = ((), (), s32[]{:S(2)}) async-start(), calls=%async_computation.5 | async-start | bytes 2228224 | tf_op jit(solution)/shard_map/all_gather | solution.py:181
  10.7 21.6 %all-to-all-start = ((bf16[16,16,512]{2,1,0:T(8,128)(2,1)}), bf16[16,16,512]{2,1,0:T(8,128)(2,1)S(1)}, u32[]{:S(2)}, u32[]{:S(2)}) async-start(bf16[16,16,512]{2,1,0:T(8,128)(2,1)} %bitcast.2), calls=%async_computation | async-start | bytes 524288 | tf_op jit(solution)/shard_map/all_to_all | solution.py:177
  34.7 18.4 %copy-start.1 = (f32[256]{0:T(256)S(1)}, f32[256]{0:T(256)}, u32[]{:S(2)}) copy-start(f32[256]{0:T(256)} %param.9) | copy-start | bytes 3076
  41.2 11.9 %all-to-all-start.1 = ((bf16[16,16,256]{2,1,0:T(8,128)(2,1)}), bf16[16,16,256]{2,1,0:T(8,128)(2,1)S(1)}, u32[]{:S(2)}, u32[]{:S(2)}) async-start(bf16[16,16,256]{2,1,0:T(8,128)(2,1)} %bitcast.5), calls=%async_computation.1 | async-start | bytes 262144 | tf_op jit(solution)/shard_map/all_to_all | solution.py:199
  117.3 12.3 %all-to-all-start.4 = ((bf16[16,16,256]{2,1,0:T(8,128)(2,1)}), bf16[16,16,256]{2,1,0:T(8,128)(2,1)S(1)}, u32[]{:S(2)}, u32[]{:S(2)}) async-start(bf16[16,16,256]{2,1,0:T(8,128)(2,1)} %bitcast.15), calls=%async_computation.4 | async-start | bytes 262144 | tf_op jit(solution)/shard_map/all_to_all | solution.py:214
Sparse Core Ops, SparseCore 0:
  10.4 59.0 all-gather.1

commit v17 on v16

--- a/solution.py
+++ b/solution.py
@@ -196,14 +196,14 @@
     )
 
     convolved_t = inverse_t(inverse[block_len:], conv_spec)
-    convolved = lax.all_to_all(
+    convolved_ct = lax.all_to_all(
         convolved_t.astype(jnp.bfloat16), "ctx", 0, 0, tiled=True
-    ).T.astype(jnp.float32)
-
-    mixed_sum = convolved + skip_gain[None, :] * inputs.astype(jnp.float32)
-    gated_rows = (gate_wide * mixed_sum).astype(jnp.bfloat16)
+    ).astype(jnp.float32)
+
+    mixed_ct = convolved_ct + skip_gain[:, None] * inputs.T.astype(jnp.float32)
+    gated_ct = (gate_wide.T * mixed_ct).astype(jnp.bfloat16)
     partial_out = lax.dot_general(
-        w_out, gated_rows, (((0,), (1,)), ((), ())), preferred_element_type=jnp.float32
+        w_out, gated_ct, (((0,), (0,)), ((), ())), preferred_element_type=jnp.float32
     )
     pieces = lax.all_to_all(partial_out.astype(jnp.bfloat16), "ch", 0, 0, tiled=True)
     pieces, grad_mixed_t = lax.optimization_barrier((pieces, grad_mixed_t))

time: 138 us -> 138 us (level)
  no operation moved by 1% of the time
where the time goes in v17:
time: 138 us; the launch traced here: 137 us
  blocking collectives  50.3 us (36%)
  waiting for transfers between devices  19 us (14%)
  starting transfers between devices  16.8 us (12%)
  between operations  14.1 us (10%)
  matrix products  13 us (9%)
  other arithmetic  9.63 us (7%)
  local copies, waits for them, and re-layouts  8.72 us (6%)
  Pallas kernels  5.79 us (4%)
    all_to_all x1, blocking collectives, body(): lax.all_to_all(partial_out.astype(jnp.bfloat16), 'ch', 0, 0, tiled=True)  36.2 us
    all_to_all x1, blocking collectives, body(): lax.all_to_all(grad_mixed_t.astype(jnp.bfloat16), 'ctx', 0, 0, tiled=True)  14 us
    all_to_all x1, starting transfers between devices, body(): pair_t = lax.all_to_all(pair, 'ctx', 0, 0, tiled=True)  9.97 us
    all_to_all x1, waiting for transfers between devices, body(): lax.all_to_all(convolved_t.astype(jnp.bfloat16), 'ctx', 0, 0, tiled=True)  7.45 us
    all_to_all x1, waiting for transfers between devices, body(): lax.all_to_all(filter_grad_t.astype(jnp.bfloat16), 'ctx', 0, 0, tiled=True)  6.28 us
    dot_general x4, matrix products, transform_t(): lax.dot_general(block_rows.astype(jnp.float32), dft_table, (((1,), (1,)),...  4.96 us
    dot_general x2, matrix products, inverse_t(): lax.dot_general(spec_t, inverse_rows, (((1,), (1,)), ((), ())), precision...  4.9 us
    unnamed x9, local copies, waits for them, and re-layouts  4.62 us
  transfers between devices with their start and end apart: 4, of which 3 were waited for; matrix products, arithmetic and copies ran while one was open for 18% of the time, Pallas kernels for 2%

profile of v17, /device:TPU:1, one launch (start us, length us, event | category | flops | bytes accessed | tf_op | source)
XLA Modules:
  0.0 137.4 jit_solution(5412405103680594486)
XLA Ops:
  7.2 0.0 copy-start
  7.2 0.0 all-gather.2.cloned.1.call-start
  7.2 0.7 all-gather.2.cloned.1.call-update
  7.9 1.0 copy.28
  8.9 1.0 copy.29
  9.9 0.7 pad_maximum_fusion.1
  10.7 10.0 %all-to-all-start = ((bf16[16,16,512]{2,1,0:T(8,128)(2,1)}), bf16[16,16,512]{2,1,0:T(8,128)(2,1)S(1)}, u32[]{:S(2)}, u32[]{:S(2)}) async-start(bf16[16,16,512]{2,1,0:T(8,128)(2,1)} %bitcast.3), calls=%async_computation | async-start | bytes 524288 | tf_op jit(solution)/shard_map/all_to_all | solution.py:177
  20.6 1.9 %fusion.12 = f32[256,512]{1,0:T(8,128)S(1)} fusion(), kind=kLoop, calls=%fused_computation.30 | loop fusion | flops 1835008 | bytes 524288 | tf_op jit(solution)/shard_map/cos | solution.py:22
  22.5 2.0 %multiply_multiply_fusion = f32[256,512]{1,0:T(8,128)S(1)} fusion(f32[256]{0:T(256)S(1)} %broadcast_select_fusion), kind=kLoop, calls=%fused_computation.19 | loop fusion | flops 2097152 | bytes 525312 | tf_op jit(solution)/shard_map/mul | solution.py:25
  24.5 2.0 %select_multiply_fusion = (f32[256,512]{1,0:T(8,128)S(1)}, f32[256,512]{1,0:T(8,128)S(1)}) fusion(f32[512]{0:T(512)S(1)} %fusion.27, pred[256]{0:T(512)(128)(4,1)S(1)} %iota_compare_fusion), kind=kLoop, calls=%fused_computation.18 | loop fusion | flops 2490368 | bytes 1050880 | tf_op jit(solution)/shard_map/mul | solution.py:26
  26.6 1.1 maximum_bitcast_fusion
  27.7 4.6 %all-to-all-done = bf16[16,16,512]{2,1,0:T(8,128)(2,1)S(1)} async-done(((bf16[16,16,512]{2,1,0:T(8,128)(2,1)}), bf16[16,16,512]{2,1,0:T(8,128)(2,1)S(1)}, u32[]{:S(2)}, u32[]{:S(2)}) %all-to-all-start) | async-done | bytes 262176 | tf_op jit(solution)/shard_map/all_to_all | solution.py:177
  32.2 1.2 fusion.16.taps_ref
  33.5 1.2 fusion.13.high_ref
  34.7 0.0 copy-start.1
  34.7 1.2 fusion.20.low_ref
  35.9 2.8 %shard_map.77 = (f32[256,512]{1,0:T(8,128)}, f32[256,512]{1,0:T(8,128)}) custom-call(f32[256,512]{1,0:T(8,128)} %fusion.20.low_ref, f32[256,512]{1,0:T(8,128)} %fusion.13.high_ref, f32[256,512]{1,0:T(8,128)} %fusion.16.taps_ref), custom_call_target="tpu_custom_call" | custom-call | flops 4456448 | bytes 2621440 | tf_op jit(solution)/shard_map/pallas_call | solution.py:125
  38.8 2.4 %convolution_convert_fusion.2 = bf16[256,256]{1,0:T(8,128)(2,1)} fusion(f32[256,512]{1,0:T(8,128)} %get-tuple-element.6, f32[512,512]{0,1:T(8,128)} %maximum_bitcast_fusion), kind=kOutput, calls=%fused_computation.4 | convolution fusion | flops 402718720 | bytes 1179648 | tf_op jit(solution)/shard_map/dot_general | solution.py:163
  41.2 3.4 %all-to-all-start.1 = ((bf16[16,16,256]{2,1,0:T(8,128)(2,1)}), bf16[16,16,256]{2,1,0:T(8,128)(2,1)S(1)}, u32[]{:S(2)}, u32[]{:S(2)}) async-start(bf16[16,16,256]{2,1,0:T(8,128)(2,1)} %bitcast.6), calls=%async_computation.1 | async-start | bytes 262144 | tf_op jit(solution)/shard_map/all_to_all | solution.py:199
  44.7 1.0 copy.27
  45.7 7.5 %all-to-all-done.1 = bf16[16,16,256]{2,1,0:T(8,128)(2,1)S(1)} async-done(((bf16[16,16,256]{2,1,0:T(8,128)(2,1)}), bf16[16,16,256]{2,1,0:T(8,128)(2,1)S(1)}, u32[]{:S(2)}, u32[]{:S(2)}) %all-to-all-start.1) | async-done | bytes 131104 | tf_op jit(solution)/shard_map/all_to_all | solution.py:199
  53.1 0.0 copy-done
  53.1 0.0 copy-done.1
  53.1 0.8 convolution_convert_fusion
  54.0 0.2 copy.36
  54.2 36.2 %all_to_all.54 = bf16[16,256,256]{1,2,0:T(8,128)(2,1)} all-to-all(bf16[16,256,256]{1,2,0:T(8,128)(2,1)S(1)} %bitcast.40), channel_id=1, replica_groups=mesh['ctx'=16,'ch'=16] {'ch'}, dimensions={0} | all-to-all | bytes 4194304 | tf_op jit(solution)/shard_map/all_to_all | solution.py:208
  90.4 3.9 %copy.31 = bf16[16,256,256]{2,1,0:T(8,128)(2,1)} copy(bf16[16,256,256]{1,2,0:T(8,128)(2,1)} %all_to_all.54) | data formatting | bytes 4194304 | tf_op jit(solution)/shard_map/all_to_all | solution.py:208
  94.3 0.0 all-gather.2.cloned.1.call-done
  94.3 2.3 %convolution_multiply_fusion = bf16[256,256]{1,0:T(8,128)(2,1)S(1)} fusion(bf16[256,4096]{1,0:T(8,128)(2,1)S(1)} %copy-done, bf16[256,4096]{1,0:T(8,128)(2,1)} %all-gather.2.cloned.1.call-done, bf16[256,256]{0,1:T(8,128)(2,1)S(1)} %copy.27), kind=kOutput, calls=%fused_computation.2 | convolution fusion | flops 537067520 | bytes 4456448 | tf_op jit(solution)/shard_map/dot_general | solution.py:182
  96.6 14.0 %all_to_all.55 = bf16[16,16,256]{2,1,0:T(8,128)(2,1)S(1)} all-to-all(bf16[16,16,256]{2,1,0:T(8,128)(2,1)S(1)} %bitcast.49), channel_id=1, replica_groups=mesh['ctx'=16,'ch'=16] {'ctx'}, dimensions={0} | all-to-all | bytes 262144 | tf_op jit(solution)/shard_map/all_to_all | solution.py:210
  110.7 1.2 fusion.14.grad_ref
  111.9 3.0 %shard_map.78 = f32[256,512]{1,0:T(8,128)} custom-call(f32[256,512]{1,0:T(8,128)} %get-tuple-element.8.seg_ref, f32[256,512]{1,0:T(8,128)} %fusion.14.grad_ref), custom_call_target="tpu_custom_call" | custom-call | flops 4456448 | bytes 1572864 | tf_op jit(solution)/shard_map/pallas_call | solution.py:142
  114.8 2.4 %convolution_convert_fusion.1 = bf16[256,256]{1,0:T(8,128)(2,1)} fusion(f32[256,512]{1,0:T(8,128)} %shard_map.78, f32[512,512]{0,1:T(8,128)} %maximum_bitcast_fusion), kind=kOutput, calls=%fused_computation.3 | convolution fusion | flops 402718720 | bytes 1179648 | tf_op jit(solution)/shard_map/dot_general | solution.py:163
  117.3 3.4 %all-to-all-start.4 = ((bf16[16,16,256]{2,1,0:T(8,128)(2,1)}), bf16[16,16,256]{2,1,0:T(8,128)(2,1)S(1)}, u32[]{:S(2)}, u32[]{:S(2)}) async-start(bf16[16,16,256]{2,1,0:T(8,128)(2,1)} %bitcast.14), calls=%async_computation.4 | async-start | bytes 262144 | tf_op jit(solution)/shard_map/all_to_all | solution.py:214
  120.7 1.9 %reduce = bf16[256,256]{1,0:T(8,128)(2,1)S(1)} reduce(bf16[16,256,256]{2,1,0:T(8,128)(2,1)} %copy.31, bf16[]{:T(256)} %constant.46), dimensions={0}, to_apply=%region_0.1.clone | reduce | flops 983040 | bytes 2228226 | tf_op jit(solution)/shard_map/reduce_sum | solution.py:221
  122.6 0.8 copy.32
  123.4 6.3 %all-to-all-done.4 = bf16[16,16,256]{2,1,0:T(8,128)(2,1)S(1)} async-done(((bf16[16,16,256]{2,1,0:T(8,128)(2,1)}), bf16[16,16,256]{2,1,0:T(8,128)(2,1)S(1)}, u32[]{:S(2)}, u32[]{:S(2)}) %all-to-all-start.4) | async-done | bytes 131104 | tf_op jit(solution)/shard_map/all_to_all | solution.py:214
  129.7 0.8 copy.33
  (4 shorter events, 0.0 us)
Async XLA Ops:
  7.2 46.0 %copy-start = (bf16[256,4096]{1,0:T(8,128)(2,1)S(1)}, bf16[256,4096]{1,0:T(8,128)(2,1)}, u32[]{:S(2)}) copy-start(bf16[256,4096]{1,0:T(8,128)(2,1)} %param.10) | copy-start | bytes 6291460
  7.2 87.1 %all-gather.2.cloned.1.call-start = ((), (), s32[]{:S(2)}) async-start(), calls=%async_computation.5 | async-start | bytes 2228224 | tf_op jit(solution)/shard_map/all_gather | solution.py:181
  10.7 21.6 %all-to-all-start = ((bf16[16,16,512]{2,1,0:T(8,128)(2,1)}), bf16[16,16,512]{2,1,0:T(8,128)(2,1)S(1)}, u32[]{:S(2)}, u32[]{:S(2)}) async-start(bf16[16,16,512]{2,1,0:T(8,128)(2,1)} %bitcast.3), calls=%async_computation | async-start | bytes 524288 | tf_op jit(solution)/shard_map/all_to_all | solution.py:177
  34.7 18.4 %copy-start.1 = (f32[256]{0:T(256)S(1)}, f32[256]{0:T(256)}, u32[]{:S(2)}) copy-start(f32[256]{0:T(256)} %param.9) | copy-start | bytes 3076
  41.2 11.9 %all-to-all-start.1 = ((bf16[16,16,256]{2,1,0:T(8,128)(2,1)}), bf16[16,16,256]{2,1,0:T(8,128)(2,1)S(1)}, u32[]{:S(2)}, u32[]{:S(2)}) async-start(bf16[16,16,256]{2,1,0:T(8,128)(2,1)} %bitcast.6), calls=%async_computation.1 | async-start | bytes 262144 | tf_op jit(solution)/shard_map/all_to_all | solution.py:199
  117.3 12.3 %all-to-all-start.4 = ((bf16[16,16,256]{2,1,0:T(8,128)(2,1)}), bf16[16,16,256]{2,1,0:T(8,128)(2,1)S(1)}, u32[]{:S(2)}, u32[]{:S(2)}) async-start(bf16[16,16,256]{2,1,0:T(8,128)(2,1)} %bitcast.14), calls=%async_computation.4 | async-start | bytes 262144 | tf_op jit(solution)/shard_map/all_to_all | solution.py:214
Sparse Core Ops, SparseCore 0:
  10.4 59.0 all-gather.1
